TPU v7x, 128 devices: a whole 4x4x4 slice. The times are simulated.
128 devices in a mesh: wide: 16 (over x, y_hi, core), narrow: 8 (over z, y_lo).
Axes of the slice: x: 4, y: 4 (y_hi: 2, y_lo: 2; y = y_hi * 2 + y_lo), z: 4, core: 2. Of those that a mesh axis runs over, the one named last changes fastest.
Arguments:
- hidden_in: bfloat16 [128, 8192], P('narrow', 'wide'), may hold values from -75 to 75
- lengths: int32 [128], P('wide'), may hold values from 32 to 8192, as said below
- kv_cache: bfloat16 [2, 2, 152576, 1024], P(None, None, 'wide', 'narrow'), may hold values from -210 to 210, as said below
- qkv_weight: bfloat16 [8192, 8, 1280], P('wide', 'narrow'), may hold values from -0.0625 to 0.0625
- o_weight: bfloat16 [8192, 8192], P('narrow', 'wide'), may hold values from -0.0625 to 0.0625
- gate_up: bfloat16 [8192, 2, 28672], P('wide', None, 'narrow'), may hold values from -0.0625 to 0.0625
- down_weight: bfloat16 [28672, 8192], P('narrow', 'wide'), may hold values from -0.03125 to 0.03125
- attn_gain: bfloat16 [8192], P('wide'), may hold values from 0.099609375 to 1.8984375
- mlp_gain: bfloat16 [8192], P('wide'), may hold values from 0.099609375 to 1.8984375
Outputs:
- hidden_out: bfloat16 [128, 8192], P('narrow', 'wide')
- new_entries: bfloat16 [2, 2, 128, 1024], P(None, None, 'wide', 'narrow')
Inputs may be any that keep to these rules, and one draw needn't show every extreme that they name: Exactly 8 requests have 8192 cached tokens, no two in the same aligned block of 8 requests; every other request has 32 to 192. The lengths of each aligned block of 8 requests sum to at most 9536, and those of one block to exactly 9536. `kv_cache`: cache positions that no request owns hold no live entries.
All inputs are finite; a program needn't handle non-finite values.
Results may differ from a plain program's by a relative error of at most 0.017.
Values may be sent and summed in bfloat16 or wider, within the bound.
No kernel may reach another device: no remote copies, remote signals or barrier semaphores. Data moves between devices by JAX's collectives and lax.ppermute only.
A program may use at most 128 MiB of HBM per device.

v0:
```python
import math

import jax
import jax.numpy as jnp
from jax import lax
from jax.sharding import PartitionSpec as P

D = 8192
HD = 128
LAYERS = 2


EPSILON = 1e-05
ROPE_BASE = 500000.0


def copy_for_each(shard, axis):
    length = lax.axis_size(axis)
    return lax.all_to_all(
        jnp.broadcast_to(shard[None], (length, *shard.shape)), axis, 0, 0, tiled=True
    )


def of_everyone(shard, axis):
    return copy_for_each(shard, axis).sum(axis=0)


def laid_out(parts, dim):
    parts = jnp.moveaxis(parts, 0, dim)
    lengths = parts.shape
    return parts.reshape(*lengths[:dim], lengths[dim] * lengths[dim + 1], *lengths[dim + 2 :])


def gathered_copies(shard, axis, dim):
    parts = copy_for_each(shard, axis)
    return laid_out(parts, dim)


def in_blocks(shard, dim, length):
    before, after = (shard.shape[:dim], shard.shape[dim + 1 :])
    return jnp.moveaxis(shard.reshape(*before, length, -1, *after), dim, 0)


def summed_on_arrival(shard, axis, dim):
    parts = in_blocks(shard, dim, lax.axis_size(axis))
    arrived = lax.all_to_all(parts, axis, split_axis=0, concat_axis=0, tiled=True)
    return arrived.sum(axis=0)


def sent_and_summed(shard, axis, dim):
    length = lax.axis_size(axis)
    parts = lax.all_to_all(in_blocks(shard, dim, length), axis, 0, 0, tiled=True)
    return jnp.sum(parts.astype(jnp.float32), axis=0)


def scale_rows(floats, square_sum, gain):
    scaled = (
        floats * lax.rsqrt(square_sum / D + EPSILON)[:, None] * gain.astype(jnp.float32)[None, :]
    )
    return scaled.astype(jnp.bfloat16)


def norm_rows(stream, gain):
    floats = stream.astype(jnp.float32)
    square_sum = of_everyone(jnp.sum(floats * floats, axis=1), "wide")
    return gathered_copies(scale_rows(floats, square_sum, gain), "narrow", 0)


def rotate_pairs(vectors, cosine, sine_table):
    half_dim = vectors.shape[-1] // 2
    first_half = vectors[..., :half_dim]
    second_half = vectors[..., half_dim:]
    return jnp.concatenate(
        [
            first_half * cosine - second_half * sine_table,
            second_half * cosine + first_half * sine_table,
        ],
        axis=-1,
    )


def rotary_tables(lengths, head_dim):
    half_dim = head_dim // 2
    inverse = jnp.exp(
        jnp.arange(half_dim, dtype=jnp.float32) * (-2.0 * math.log(ROPE_BASE) / head_dim)
    )
    angles = lengths.astype(jnp.float32)[:, None] * inverse[None, :]
    return (jnp.cos(angles), jnp.sin(angles))


def split_heads(projected, lengths, heads_kv, head_dim):
    row_count = projected.shape[0]
    grouped = projected.reshape(row_count, heads_kv, -1, head_dim)
    group_size = grouped.shape[2] - 2
    cosine, sine_table = rotary_tables(lengths, head_dim)
    rotated = rotate_pairs(
        grouped[:, :, : group_size + 1], cosine[:, None, None, :], sine_table[:, None, None, :]
    )
    queries = rotated[:, :, :group_size].astype(jnp.bfloat16)
    key_new = rotated[:, :, group_size].astype(jnp.bfloat16)
    value_new = grouped[:, :, group_size + 1].astype(jnp.bfloat16)
    return (queries, key_new, value_new)


def attend(queries, key_new, value_new, cached_keys, cached_values, lengths):
    row_count, heads_kv, group_size, head_dim = queries.shape
    slot_count = cached_keys.shape[0]
    score_scale = 1.0 / math.sqrt(head_dim)
    key_table = cached_keys.reshape(slot_count, heads_kv, head_dim)
    value_table = cached_values.reshape(slot_count, heads_kv, head_dim)
    starts = jnp.cumsum(lengths) - lengths
    position = jnp.arange(slot_count, dtype=jnp.int32)
    owned = (position[None, :] >= starts[:, None]) & (
        position[None, :] < (starts + lengths)[:, None]
    )
    scores = (
        jnp.einsum("rkgd,tkd->krgt", queries, key_table, preferred_element_type=jnp.float32)
        * score_scale
    )
    scores = jnp.where(owned[None, :, None, :], scores, -jnp.inf)
    own_score = (
        jnp.einsum("rkgd,rkd->krg", queries, key_new, preferred_element_type=jnp.float32)
        * score_scale
    )
    row_peak = jnp.maximum(jnp.max(scores, axis=3), own_score)
    weights = jnp.exp(scores - row_peak[..., None])
    own_weight = jnp.exp(own_score - row_peak)
    weight_sum = jnp.sum(weights, axis=3) + own_weight
    blended = jnp.einsum(
        "krgt,tkd->krgd",
        weights.astype(jnp.bfloat16),
        value_table,
        preferred_element_type=jnp.float32,
    )
    own_rounded = lax.optimization_barrier(own_weight.astype(jnp.bfloat16)).astype(jnp.float32)
    blended = blended + own_rounded[..., None] * jnp.transpose(value_new, (1, 0, 2))[
        :, :, None, :
    ].astype(jnp.float32)
    normalized = (blended / weight_sum[..., None]).astype(jnp.bfloat16)
    return jnp.transpose(normalized, (1, 0, 2, 3)).reshape(
        row_count, heads_kv * group_size * head_dim
    )


def on_device(
    hidden_in, lengths, kv_cache, qkv_weight, o_weight, gate_up, down_weight, attn_gain, mlp_gain
):
    width_dev = hidden_in.shape[1]
    heads_kv = qkv_weight.shape[1]
    hidden_dev = down_weight.shape[0]
    flat_qkv = qkv_weight.reshape(width_dev, -1)
    flat_gate = gate_up.reshape(width_dev, -1)
    stream = hidden_in
    entries = []
    for layer_index in range(LAYERS):
        normed = norm_rows(stream, attn_gain)
        total_rows = normed.shape[0]
        rows_in = normed
        own_qkv = summed_on_arrival(
            jnp.dot(rows_in, flat_qkv, preferred_element_type=jnp.float32), "wide", 0
        )
        queries, key_new, value_new = split_heads(own_qkv, lengths, heads_kv, HD)
        own_rows = key_new.shape[0]
        entries.append(
            jnp.stack(
                [
                    key_new.reshape(own_rows, heads_kv * HD),
                    value_new.reshape(own_rows, heads_kv * HD),
                ]
            )
        )
        attended = attend(
            queries, key_new, value_new, kv_cache[layer_index, 0], kv_cache[layer_index, 1], lengths
        )
        heads_all = gathered_copies(attended, "wide", 0)
        summed = summed_on_arrival(
            jnp.dot(heads_all, o_weight, preferred_element_type=jnp.float32), "narrow", 0
        )
        stream = (stream.astype(jnp.float32) + summed).astype(jnp.bfloat16)
        normed = norm_rows(stream, mlp_gain)
        both_parts = jnp.dot(normed, flat_gate, preferred_element_type=jnp.float32).reshape(
            total_rows, 2, hidden_dev
        )
        own_cols = sent_and_summed(both_parts.astype(jnp.bfloat16), "wide", 2)
        activated = (jax.nn.silu(own_cols[:, 0]) * own_cols[:, 1]).astype(jnp.bfloat16)
        partial_down = jnp.dot(
            gathered_copies(activated, "wide", 1), down_weight, preferred_element_type=jnp.float32
        )
        summed = summed_on_arrival(partial_down, "narrow", 0)
        stream = (stream.astype(jnp.float32) + summed).astype(jnp.bfloat16)
    return (stream, jnp.stack(entries))


def solution(mesh):
    return jax.shard_map(
        on_device,
        mesh=mesh,
        in_specs=(
            P("narrow", "wide"),
            P("wide"),
            P(None, None, "wide", "narrow"),
            P("wide", "narrow", None),
            P("narrow", "wide"),
            P("wide", None, "narrow"),
            P("narrow", "wide"),
            P("wide"),
            P("wide"),
        ),
        out_specs=(P("narrow", "wide"), P(None, None, "wide", "narrow")),
        check_vma=False,
    )
```

profile of v0, /device:TPU:1, one launch (start us, length us, event | category | flops | bytes accessed | tf_op | source)
XLA Modules:
  0.0 348.7 jit_solution(1540085844589671065)
XLA Ops:
  2.2 8.4 %all-to-all-start = ((f32[16,1,16]{2,1,0:T(1,128)}), f32[16,1,16]{2,1,0:T(1,128)S(1)}, u32[]{:S(2)}, u32[]{:S(2)}) async-start(f32[16,1,16]{2,1,0:T(1,128)} %broadcast_in_dim.45), calls=%async_computation | async-start | bytes 16384 | tf_op jit(solution)/shard_map/all_to_all | solution.py:19
  12.1 5.4 %all-to-all-done = f32[16,1,16]{2,1,0:T(1,128)S(1)} async-done(((f32[16,1,16]{2,1,0:T(1,128)}), f32[16,1,16]{2,1,0:T(1,128)S(1)}, u32[]{:S(2)}, u32[]{:S(2)}) %all-to-all-start) | async-done | bytes 1056 | tf_op jit(solution)/shard_map/all_to_all | solution.py:19
  19.0 5.1 %all-to-all-start.1 = ((bf16[8,16,512]{2,1,0:T(8,128)(2,1)}), bf16[8,16,512]{2,1,0:T(8,128)(2,1)S(1)}, u32[]{:S(2)}, u32[]{:S(2)}) async-start(bf16[8,16,512]{2,1,0:T(8,128)(2,1)} %broadcast_in_dim.46), calls=%async_computation.1 | async-start | bytes 262144 | tf_op jit(solution)/shard_map/all_to_all | solution.py:19
  24.9 4.8 %all-to-all-done.1 = bf16[8,16,512]{2,1,0:T(8,128)(2,1)S(1)} async-done(((bf16[8,16,512]{2,1,0:T(8,128)(2,1)}), bf16[8,16,512]{2,1,0:T(8,128)(2,1)S(1)}, u32[]{:S(2)}, u32[]{:S(2)}) %all-to-all-start.1) | async-done | bytes 131104 | tf_op jit(solution)/shard_map/all_to_all | solution.py:19
  31.0 5.4 %all-to-all-start.2 = ((f32[16,8,1280]{2,1,0:T(8,128)}), f32[16,8,1280]{2,1,0:T(8,128)S(1)}, u32[]{:S(2)}, u32[]{:S(2)}) async-start(f32[16,8,1280]{2,1,0:T(8,128)} %fusion.22), calls=%async_computation.2 | async-start | bytes 1310720 | tf_op jit(solution)/shard_map/all_to_all | solution.py:46
  36.7 12.0 %all-to-all-done.2 = f32[16,8,1280]{2,1,0:T(8,128)S(1)} async-done(((f32[16,8,1280]{2,1,0:T(8,128)}), f32[16,8,1280]{2,1,0:T(8,128)S(1)}, u32[]{:S(2)}, u32[]{:S(2)}) %all-to-all-start.2) | async-done | bytes 655392 | tf_op jit(solution)/shard_map/all_to_all | solution.py:46
  55.0 13.0 %all_to_all.104 = bf16[16,8,1024]{2,1,0:T(8,128)(2,1)S(1)} all-to-all(bf16[16,8,1024]{2,1,0:T(8,128)(2,1)S(1)} %broadcast_in_dim.49), channel_id=1, replica_groups=mesh['wide'=16,'narrow'=8] {'wide'}, dimensions={0} | all-to-all | bytes 524288 | tf_op jit(solution)/shard_map/all_to_all | solution.py:19
  68.3 9.4 %all_to_all.105 = f32[8,16,512]{2,1,0:T(8,128)S(1)} all-to-all(f32[8,16,512]{2,1,0:T(8,128)S(1)} %fusion.70), channel_id=1, replica_groups=mesh['wide'=16,'narrow'=8] {'narrow'}, dimensions={0} | all-to-all | bytes 524288 | tf_op jit(solution)/shard_map/all_to_all | solution.py:46
  78.4 4.5 %all-to-all-start.5 = ((f32[16,1,16]{2,1,0:T(1,128)}), f32[16,1,16]{2,1,0:T(1,128)S(1)}, u32[]{:S(2)}, u32[]{:S(2)}) async-start(f32[16,1,16]{2,1,0:T(1,128)} %broadcast_in_dim.50), calls=%async_computation.5 | async-start | bytes 16384 | tf_op jit(solution)/shard_map/all_to_all | solution.py:19
  83.0 7.0 %all-to-all-done.5 = f32[16,1,16]{2,1,0:T(1,128)S(1)} async-done(((f32[16,1,16]{2,1,0:T(1,128)}), f32[16,1,16]{2,1,0:T(1,128)S(1)}, u32[]{:S(2)}, u32[]{:S(2)}) %all-to-all-start.5) | async-done | bytes 1056 | tf_op jit(solution)/shard_map/all_to_all | solution.py:19
  90.7 3.4 all-to-all-start.6
  94.1 7.9 %copy.107 = bf16[64,8,2,3584]{3,1,2,0:T(8,128)(2,1)} copy(bf16[64,8,2,3584]{3,2,1,0:T(2,128)(2,1)} %bitcast.179) | data formatting | bytes 14680064
  102.0 10.4 %copy.77 = bf16[7168,512]{1,0:T(8,128)(2,1)} copy(bf16[7168,512]{0,1:T(8,128)(2,1)} %bitcast.178) | data formatting | bytes 14680064 | tf_op jit(solution)/shard_map/dot_general | solution.py:181
  112.4 6.9 %convolution_convert_fusion.1 = bf16[128,2,3584]{2,0,1:T(8,128)(2,1)} fusion(bf16[128,512,1]{1,0,2:T(8,128)(2,1)S(1)} %bitcast.186, bf16[2,3584,512]{2,1,0:T(8,128)(2,1)} %bitcast.176), kind=kOutput, calls=%fused_computation.5 | convolution fusion | flops 940441600 | bytes 9306112 | tf_op jit(solution)/shard_map/dot_general | solution.py:181
  119.3 2.9 copy.78
  122.4 28.9 %all_to_all.106 = bf16[16,128,2,224]{1,3,2,0:T(8,128)(2,1)S(1)} all-to-all(bf16[16,128,2,224]{1,3,2,0:T(8,128)(2,1)S(1)} %copy.79), channel_id=1, replica_groups=mesh['wide'=16,'narrow'=8] {'wide'}, dimensions={0} | all-to-all | bytes 3670016 | tf_op jit(solution)/shard_map/all_to_all | solution.py:52
  151.7 18.6 %all_to_all.107 = bf16[16,128,224]{1,2,0:T(8,128)(2,1)S(1)} all-to-all(bf16[16,128,224]{1,2,0:T(8,128)(2,1)S(1)} %broadcast_in_dim.52), channel_id=1, replica_groups=mesh['wide'=16,'narrow'=8] {'wide'}, dimensions={0} | all-to-all | bytes 1835008 | tf_op jit(solution)/shard_map/all_to_all | solution.py:19
  175.7 11.3 %all_to_all.108 = f32[8,16,512]{2,1,0:T(8,128)S(1)} all-to-all(f32[8,16,512]{2,1,0:T(8,128)S(1)} %fusion.4), channel_id=1, replica_groups=mesh['wide'=16,'narrow'=8] {'narrow'}, dimensions={0} | all-to-all | bytes 524288 | tf_op jit(solution)/shard_map/all_to_all | solution.py:46
  187.2 12.5 %all_to_all.109 = f32[16,1,16]{2,1,0:T(1,128)S(1)} all-to-all(f32[16,1,16]{2,1,0:T(1,128)S(1)} %broadcast_in_dim.53), channel_id=1, replica_groups=mesh['wide'=16,'narrow'=8] {'wide'}, dimensions={0} | all-to-all | bytes 2048 | tf_op jit(solution)/shard_map/all_to_all | solution.py:19
  199.8 7.9 %all_to_all.110 = bf16[8,16,512]{2,1,0:T(8,128)(2,1)S(1)} all-to-all(bf16[8,16,512]{2,1,0:T(8,128)(2,1)S(1)} %broadcast_in_dim.54), channel_id=1, replica_groups=mesh['wide'=16,'narrow'=8] {'narrow'}, dimensions={0} | all-to-all | bytes 262144 | tf_op jit(solution)/shard_map/all_to_all | solution.py:19
  208.1 17.6 %all_to_all.111 = f32[16,8,1280]{2,1,0:T(8,128)S(1)} all-to-all(f32[16,8,1280]{2,1,0:T(8,128)S(1)} %fusion.20), channel_id=1, replica_groups=mesh['wide'=16,'narrow'=8] {'wide'}, dimensions={0} | all-to-all | bytes 1310720 | tf_op jit(solution)/shard_map/all_to_all | solution.py:46
  231.9 11.7 %all_to_all.112 = bf16[16,8,1024]{2,1,0:T(8,128)(2,1)S(1)} all-to-all(bf16[16,8,1024]{2,1,0:T(8,128)(2,1)S(1)} %broadcast_in_dim.56), channel_id=1, replica_groups=mesh['wide'=16,'narrow'=8] {'wide'}, dimensions={0} | all-to-all | bytes 524288 | tf_op jit(solution)/shard_map/all_to_all | solution.py:19
  243.9 9.4 %all_to_all.113 = f32[8,16,512]{2,1,0:T(8,128)S(1)} all-to-all(f32[8,16,512]{2,1,0:T(8,128)S(1)} %fusion.68), channel_id=1, replica_groups=mesh['wide'=16,'narrow'=8] {'narrow'}, dimensions={0} | all-to-all | bytes 524288 | tf_op jit(solution)/shard_map/all_to_all | solution.py:46
  253.5 11.2 %all_to_all.114 = f32[16,1,16]{2,1,0:T(1,128)S(1)} all-to-all(f32[16,1,16]{2,1,0:T(1,128)S(1)} %broadcast_in_dim.57), channel_id=1, replica_groups=mesh['wide'=16,'narrow'=8] {'wide'}, dimensions={0} | all-to-all | bytes 2048 | tf_op jit(solution)/shard_map/all_to_all | solution.py:19
  264.8 7.9 %all_to_all.115 = bf16[8,16,512]{2,1,0:T(8,128)(2,1)S(1)} all-to-all(bf16[8,16,512]{2,1,0:T(8,128)(2,1)S(1)} %broadcast_in_dim.58), channel_id=1, replica_groups=mesh['wide'=16,'narrow'=8] {'narrow'}, dimensions={0} | all-to-all | bytes 262144 | tf_op jit(solution)/shard_map/all_to_all | solution.py:19
  272.7 6.9 %convolution_convert_fusion = bf16[128,2,3584]{2,0,1:T(8,128)(2,1)} fusion(bf16[128,512,1]{1,0,2:T(8,128)(2,1)S(1)} %bitcast.187, bf16[2,3584,512]{2,1,0:T(8,128)(2,1)} %bitcast.177), kind=kOutput, calls=%fused_computation.4 | convolution fusion | flops 940441600 | bytes 9306112 | tf_op jit(solution)/shard_map/dot_general | solution.py:181
  279.6 2.9 copy.86
  282.7 30.1 %all_to_all.116 = bf16[16,128,2,224]{1,3,2,0:T(8,128)(2,1)S(1)} all-to-all(bf16[16,128,2,224]{1,3,2,0:T(8,128)(2,1)S(1)} %copy.87), channel_id=1, replica_groups=mesh['wide'=16,'narrow'=8] {'wide'}, dimensions={0} | all-to-all | bytes 3670016 | tf_op jit(solution)/shard_map/all_to_all | solution.py:52
  313.2 18.6 %all_to_all.117 = bf16[16,128,224]{1,2,0:T(8,128)(2,1)S(1)} all-to-all(bf16[16,128,224]{1,2,0:T(8,128)(2,1)S(1)} %broadcast_in_dim.59), channel_id=1, replica_groups=mesh['wide'=16,'narrow'=8] {'wide'}, dimensions={0} | all-to-all | bytes 1835008 | tf_op jit(solution)/shard_map/all_to_all | solution.py:19
  334.6 3.4 fusion.2
  338.0 3.4 all-to-all-start.19
  342.0 6.0 %all-to-all-done.19 = f32[8,16,512]{2,1,0:T(8,128)S(1)} async-done(((f32[8,16,512]{2,1,0:T(8,128)}), f32[8,16,512]{2,1,0:T(8,128)S(1)}, u32[]{:S(2)}, u32[]{:S(2)}) %all-to-all-start.19) | async-done | bytes 262176 | tf_op jit(solution)/shard_map/all_to_all | solution.py:46
  (98 shorter events, 32.7 us)
Async XLA Ops:
  0.6 29.1 %copy-start = (bf16[512,1,1280]{2,0,1:T(8,128)(2,1)S(1)}, bf16[512,1,1280]{2,0,1:T(8,128)(2,1)}, u32[]{:S(2)}) copy-start(bf16[512,1,1280]{2,0,1:T(8,128)(2,1)} %param.12) | copy-start | bytes 3932164
  2.2 15.4 %all-to-all-start = ((f32[16,1,16]{2,1,0:T(1,128)}), f32[16,1,16]{2,1,0:T(1,128)S(1)}, u32[]{:S(2)}, u32[]{:S(2)}) async-start(f32[16,1,16]{2,1,0:T(1,128)} %broadcast_in_dim.45), calls=%async_computation | async-start | bytes 16384 | tf_op jit(solution)/shard_map/all_to_all | solution.py:19
  19.0 10.7 %all-to-all-start.1 = ((bf16[8,16,512]{2,1,0:T(8,128)(2,1)}), bf16[8,16,512]{2,1,0:T(8,128)(2,1)S(1)}, u32[]{:S(2)}, u32[]{:S(2)}) async-start(bf16[8,16,512]{2,1,0:T(8,128)(2,1)} %broadcast_in_dim.46), calls=%async_computation.1 | async-start | bytes 262144 | tf_op jit(solution)/shard_map/all_to_all | solution.py:19
  31.0 17.8 %all-to-all-start.2 = ((f32[16,8,1280]{2,1,0:T(8,128)}), f32[16,8,1280]{2,1,0:T(8,128)S(1)}, u32[]{:S(2)}, u32[]{:S(2)}) async-start(f32[16,8,1280]{2,1,0:T(8,128)} %fusion.22), calls=%async_computation.2 | async-start | bytes 1310720 | tf_op jit(solution)/shard_map/all_to_all | solution.py:46
  52.5 15.5 %copy-start.1 = (bf16[1024,512]{1,0:T(8,128)(2,1)S(1)}, bf16[1024,512]{1,0:T(8,128)(2,1)}, u32[]{:S(2)}) copy-start(bf16[1024,512]{1,0:T(8,128)(2,1)} %param.13) | copy-start | bytes 3145732
  54.9 22.7 %copy-start.3 = (bf16[16,512]{1,0:T(8,128)(2,1)S(1)}, bf16[16,512]{1,0:T(8,128)(2,1)}, u32[]{:S(2)}) copy-start(bf16[16,512]{1,0:T(8,128)(2,1)} %param.9) | copy-start | bytes 49156
  55.0 28.0 %copy-start.4 = (bf16[512]{0:T(512)(128)(2,1)S(1)}, bf16[512]{0:T(512)(128)(2,1)}, u32[]{:S(2)}) copy-start(bf16[512]{0:T(512)(128)(2,1)} %param.17) | copy-start | bytes 3076
  78.4 11.5 %all-to-all-start.5 = ((f32[16,1,16]{2,1,0:T(1,128)}), f32[16,1,16]{2,1,0:T(1,128)S(1)}, u32[]{:S(2)}, u32[]{:S(2)}) async-start(f32[16,1,16]{2,1,0:T(1,128)} %broadcast_in_dim.50), calls=%async_computation.5 | async-start | bytes 16384 | tf_op jit(solution)/shard_map/all_to_all | solution.py:19
  90.7 21.7 %all-to-all-start.6 = ((bf16[8,16,512]{2,1,0:T(8,128)(2,1)}), bf16[8,16,512]{2,1,0:T(8,128)(2,1)S(1)}, u32[]{:S(2)}, u32[]{:S(2)}) async-start(bf16[8,16,512]{2,1,0:T(8,128)(2,1)} %broadcast_in_dim.51), calls=%async_computation.6 | async-start | bytes 262144 | tf_op jit(solution)/shard_map/all_to_all | solution.py:19
  229.4 14.2 %copy-start.2 = (bf16[1024,512]{1,0:T(8,128)(2,1)S(1)}, bf16[1024,512]{1,0:T(8,128)(2,1)}, u32[]{:S(2)}) copy-start(bf16[1024,512]{1,0:T(8,128)(2,1)} %param.13) | copy-start | bytes 3145732
  338.0 10.1 %all-to-all-start.19 = ((f32[8,16,512]{2,1,0:T(8,128)}), f32[8,16,512]{2,1,0:T(8,128)S(1)}, u32[]{:S(2)}, u32[]{:S(2)}) async-start(f32[8,16,512]{2,1,0:T(8,128)} %fusion.2), calls=%async_computation.19 | async-start | bytes 524288 | tf_op jit(solution)/shard_map/all_to_all | solution.py:46
where the time goes:
time: 351 us; the launch traced here: 349 us
  blocking collectives  208 us (59%)
  waiting for transfers between devices  35.3 us (10%)
  local copies, waits for them, and re-layouts  32.9 us (9%)
  matrix products  32.6 us (9%)
  starting transfers between devices  30.3 us (9%)
  other arithmetic  8.43 us (2%)
    all_to_all x8, blocking collectives, copy_for_each(): lax.all_to_all(jnp.broadcast_to(shard[None], (length, *shard.shape)), axi...  101 us
    all_to_all x2, blocking collectives, sent_and_summed(): lax.all_to_all(in_blocks(shard, dim, length), axis, 0, 0, tiled=True)  59 us
    all_to_all x4, blocking collectives, summed_on_arrival(): lax.all_to_all(parts, axis, split_axis=0, concat_axis=0, tiled=True)  47.6 us
    all_to_all x4, starting transfers between devices, copy_for_each(): lax.all_to_all(jnp.broadcast_to(shard[None], (length, *shard.shape)), axi...  21.5 us
    all_to_all x2, waiting for transfers between devices, summed_on_arrival(): lax.all_to_all(parts, axis, split_axis=0, concat_axis=0, tiled=True)  18.1 us
    all_to_all x4, waiting for transfers between devices, copy_for_each(): lax.all_to_all(jnp.broadcast_to(shard[None], (length, *shard.shape)), axi...  17.3 us
    dot_general x2, matrix products, on_device(): jnp.dot(normed, flat_gate, preferred_element_type=jnp.float32)  13.8 us
    dot_general x1, local copies, waits for them, and re-layouts, on_device(): jnp.dot(normed, flat_gate, preferred_element_type=jnp.float32)  10.4 us
  transfers between devices with their start and end apart: 6, of which 5 were waited for; matrix products, arithmetic and copies ran while one was open for 6% of the time, Pallas kernels for 0%

commit v1 on v0

--- a/solution.py
+++ b/solution.py
@@ -62,8 +62,8 @@
 
 def norm_rows(stream, gain):
     floats = stream.astype(jnp.float32)
-    square_sum = of_everyone(jnp.sum(floats * floats, axis=1), "wide")
-    return gathered_copies(scale_rows(floats, square_sum, gain), "narrow", 0)
+    square_sum = lax.psum(jnp.sum(floats * floats, axis=1), "wide")
+    return lax.all_gather(scale_rows(floats, square_sum, gain), "narrow", axis=0, tiled=True)
 
 
 def rotate_pairs(vectors, cosine, sine_table):
@@ -147,17 +147,16 @@
 ):
     width_dev = hidden_in.shape[1]
     heads_kv = qkv_weight.shape[1]
-    hidden_dev = down_weight.shape[0]
     flat_qkv = qkv_weight.reshape(width_dev, -1)
-    flat_gate = gate_up.reshape(width_dev, -1)
     stream = hidden_in
     entries = []
     for layer_index in range(LAYERS):
         normed = norm_rows(stream, attn_gain)
-        total_rows = normed.shape[0]
-        rows_in = normed
-        own_qkv = summed_on_arrival(
-            jnp.dot(rows_in, flat_qkv, preferred_element_type=jnp.float32), "wide", 0
+        own_qkv = lax.psum_scatter(
+            jnp.dot(normed, flat_qkv, preferred_element_type=jnp.float32),
+            "wide",
+            scatter_dimension=0,
+            tiled=True,
         )
         queries, key_new, value_new = split_heads(own_qkv, lengths, heads_kv, HD)
         own_rows = key_new.shape[0]
@@ -172,21 +171,28 @@
         attended = attend(
             queries, key_new, value_new, kv_cache[layer_index, 0], kv_cache[layer_index, 1], lengths
         )
-        heads_all = gathered_copies(attended, "wide", 0)
-        summed = summed_on_arrival(
-            jnp.dot(heads_all, o_weight, preferred_element_type=jnp.float32), "narrow", 0
+        heads_all = lax.all_gather(attended, "wide", axis=0, tiled=True)
+        summed = lax.psum_scatter(
+            jnp.dot(heads_all, o_weight, preferred_element_type=jnp.float32),
+            "narrow",
+            scatter_dimension=0,
+            tiled=True,
         )
         stream = (stream.astype(jnp.float32) + summed).astype(jnp.bfloat16)
         normed = norm_rows(stream, mlp_gain)
-        both_parts = jnp.dot(normed, flat_gate, preferred_element_type=jnp.float32).reshape(
-            total_rows, 2, hidden_dev
-        )
-        own_cols = sent_and_summed(both_parts.astype(jnp.bfloat16), "wide", 2)
-        activated = (jax.nn.silu(own_cols[:, 0]) * own_cols[:, 1]).astype(jnp.bfloat16)
+        both_parts = jnp.einsum(
+            "rd,dkh->rkh", normed, gate_up, preferred_element_type=jnp.float32
+        )
+        own_rows_parts = lax.psum_scatter(
+            both_parts.astype(jnp.bfloat16), "wide", scatter_dimension=0, tiled=True
+        ).astype(jnp.float32)
+        activated = (jax.nn.silu(own_rows_parts[:, 0]) * own_rows_parts[:, 1]).astype(jnp.bfloat16)
         partial_down = jnp.dot(
-            gathered_copies(activated, "wide", 1), down_weight, preferred_element_type=jnp.float32
-        )
-        summed = summed_on_arrival(partial_down, "narrow", 0)
+            lax.all_gather(activated, "wide", axis=0, tiled=True),
+            down_weight,
+            preferred_element_type=jnp.float32,
+        )
+        summed = lax.psum_scatter(partial_down, "narrow", scatter_dimension=0, tiled=True)
         stream = (stream.astype(jnp.float32) + summed).astype(jnp.bfloat16)
     return (stream, jnp.stack(entries))
 

time: 351 us -> 798 us (2.27)
  waiting for transfers between devices: 35.3 us -> 389 us
  blocking collectives: 208 us -> 341 us
  starting transfers between devices: 30.3 us -> 0.33 us
  local copies, waits for them, and re-layouts: 32.9 us -> 4.74 us
  between operations: 1 us -> 14.4 us
    reduce_scatter x0 -> x6, waiting for transfers between devices: none -> 253 us  [the longest x2 135 us: on_device(): lax.psum_scatter(jnp.dot(normed, flat_qkv, preferred_element_type=jnp.flo...]
    all_to_all x14 -> x0, blocking collectives: 208 us -> none  [the longest x8 101 us: copy_for_each(): lax.all_to_all(jnp.broadcast_to(shard[None], (length, *shard.shape)), axi...]
    all_gather x0 -> x8, blocking collectives: none -> 192 us  [the longest x4 89.5 us: norm_rows(): lax.all_gather(scale_rows(floats, square_sum, gain), 'narrow', axis=0, ti...]
    psum x0 -> x4, blocking collectives: none -> 149 us  [norm_rows(): square_sum = lax.psum(jnp.sum(floats * floats, axis=1), 'wide')]
    unnamed x0 -> x10, waiting for transfers between devices: none -> 136 us
    all_to_all x6 -> x0, waiting for transfers between devices: 35.3 us -> none  [the longest x2 18.1 us: summed_on_arrival(): lax.all_to_all(parts, axis, split_axis=0, concat_axis=0, tiled=True)]
    all_to_all x6 -> x0, starting transfers between devices: 30.3 us -> none  [the longest x4 21.5 us: copy_for_each(): lax.all_to_all(jnp.broadcast_to(shard[None], (length, *shard.shape)), axi...]
    dot_general x3 -> x0, local copies, waits for them, and re-layouts: 14.1 us -> none  [the longest x1 10.4 us: on_device(): jnp.dot(normed, flat_gate, preferred_element_type=jnp.float32)]
  transfers between devices with their start and end apart: 6 -> 8, of which waited for: 5 -> 8; matrix products, arithmetic and copies ran while one was open for 6% -> 0% of each run, Pallas kernels for 0% -> 0%
where the time goes in v1:
time: 798 us; the launch traced here: 793 us
  waiting for transfers between devices  389 us (49%)
  blocking collectives  341 us (43%)
  matrix products  30.1 us (4%)
  between operations  14.4 us (2%)
  other arithmetic  12.5 us (2%)
    psum x4, blocking collectives, norm_rows(): square_sum = lax.psum(jnp.sum(floats * floats, axis=1), 'wide')  149 us
    unnamed x10, waiting for transfers between devices  136 us
    reduce_scatter x2, waiting for transfers between devices, on_device(): lax.psum_scatter(jnp.dot(normed, flat_qkv, preferred_element_type=jnp.flo...  135 us
    all_gather x4, blocking collectives, norm_rows(): lax.all_gather(scale_rows(floats, square_sum, gain), 'narrow', axis=0, ti...  89.5 us
    reduce_scatter x2, waiting for transfers between devices, on_device(): lax.psum_scatter(partial_down, 'narrow', scatter_dimension=0, tiled=True)  59.2 us
    reduce_scatter x2, waiting for transfers between devices, on_device(): lax.psum_scatter(jnp.dot(heads_all, o_weight, preferred_element_type=jnp....  59.1 us
    all_gather x2, blocking collectives, on_device(): lax.all_gather(activated, 'wide', axis=0, tiled=True)  53.3 us
    all_gather x2, blocking collectives, on_device(): heads_all = lax.all_gather(attended, 'wide', axis=0, tiled=True)  49.5 us
  transfers between devices with their start and end apart: 8, of which 8 were waited for; matrix products, arithmetic and copies ran while one was open for 0% of the time, Pallas kernels for 0%

profile of v1, /device:TPU:1, one launch (start us, length us, event | category | flops | bytes accessed | tf_op | source)
XLA Modules:
  0.0 792.7 jit_solution(17397242631848850265)
XLA Ops:
  8.2 34.1 %psum.28 = f32[16]{0:T(128)S(1)} all-reduce(f32[16]{0:T(128)S(1)} %fusion.91), channel_id=1, replica_groups=mesh['wide'=16,'narrow'=8] {'wide'}, use_global_device_ids=true, to_apply=%region_2.0 | all-reduce | flops 16 | bytes 128 | tf_op jit(solution)/shard_map/psum | solution.py:65
  43.8 23.7 %all_gather.24 = bf16[128,512]{1,0:T(8,128)(2,1)S(1)} all-gather(bf16[16,512]{1,0:T(8,128)(2,1)S(1)} %fusion.93), channel_id=1, replica_groups=mesh['wide'=16,'narrow'=8] {'narrow'}, dimensions={0}, use_global_device_ids=true | all-gather | bytes 147456 | tf_op jit(solution)/shard_map/all_gather | solution.py:66
  69.2 70.4 %reduce-scatter.13.cloned.1.call-done = f32[8,1280]{1,0:T(8,128)} async-done(((f32[128,1280]{1,0:T(8,128)}), f32[8,1280]{1,0:T(8,128)}) %reduce-scatter.13.cloned.1.call-update) | async-done | bytes 40976 | tf_op jit(solution)/shard_map/reduce_scatter | solution.py:155
  141.5 2.7 fusion.128
  144.9 2.4 fusion.70
  147.3 24.8 %all_gather.25 = bf16[128,1024]{1,0:T(8,128)(2,1)S(1)} all-gather(bf16[8,1024]{1,0:T(8,128)(2,1)S(1)} %bitcast.162), channel_id=1, replica_groups=mesh['wide'=16,'narrow'=8] {'wide'}, dimensions={0}, use_global_device_ids=true | all-gather | bytes 278528 | tf_op jit(solution)/shard_map/all_gather | solution.py:174
  173.2 29.5 %reduce-scatter.15.cloned.1.call-done = f32[16,512]{1,0:T(8,128)} async-done(((f32[128,512]{1,0:T(8,128)}), f32[16,512]{1,0:T(8,128)}) %reduce-scatter.15.cloned.1.call-update) | async-done | bytes 32784 | tf_op jit(solution)/shard_map/reduce_scatter | solution.py:175
  203.6 38.3 %psum.29 = f32[16]{0:T(128)S(1)} all-reduce(f32[16]{0:T(128)S(1)} %get-tuple-element.6), channel_id=1, replica_groups=mesh['wide'=16,'narrow'=8] {'wide'}, use_global_device_ids=true, to_apply=%region_8.9 | all-reduce | flops 16 | bytes 128 | tf_op jit(solution)/shard_map/psum | solution.py:65
  242.0 21.9 %all_gather.26 = bf16[128,512]{1,0:T(8,128)(2,1)S(1)} all-gather(bf16[16,512]{1,0:T(8,128)(2,1)S(1)} %fusion.97), channel_id=1, replica_groups=mesh['wide'=16,'narrow'=8] {'narrow'}, dimensions={0}, use_global_device_ids=true | all-gather | bytes 147456 | tf_op jit(solution)/shard_map/all_gather | solution.py:66
  263.9 4.2 fusion.15
  268.1 1.4 copy.60
  269.6 68.2 %reduce-scatter.25.cloned.1.call-done = bf16[8,7168]{1,0:T(8,128)(2,1)} async-done(((bf16[128,7168]{1,0:T(8,128)(2,1)}), bf16[8,7168]{1,0:T(8,128)(2,1)}) %reduce-scatter.25.cloned.1.call-update) | async-done | bytes 114704
  338.7 26.7 %all_gather.27 = bf16[128,3584]{1,0:T(8,128)(2,1)S(1)} all-gather(bf16[8,3584]{1,0:T(8,128)(2,1)S(1)} %fusion.86), channel_id=1, replica_groups=mesh['wide'=16,'narrow'=8] {'wide'}, dimensions={0}, use_global_device_ids=true | all-gather | bytes 974848 | tf_op jit(solution)/shard_map/all_gather | solution.py:191
  365.4 3.4 fusion.131
  368.8 29.9 %reduce-scatter.17.cloned.1.call-done = f32[16,512]{1,0:T(8,128)} async-done(((f32[128,512]{1,0:T(8,128)}), f32[16,512]{1,0:T(8,128)}) %reduce-scatter.17.cloned.1.call-update) | async-done | bytes 32784 | tf_op jit(solution)/shard_map/reduce_scatter | solution.py:195
  399.6 38.3 %psum.30 = f32[16]{0:T(128)S(1)} all-reduce(f32[16]{0:T(128)S(1)} %get-tuple-element.4), channel_id=1, replica_groups=mesh['wide'=16,'narrow'=8] {'wide'}, use_global_device_ids=true, to_apply=%region_12.13 | all-reduce | flops 16 | bytes 128 | tf_op jit(solution)/shard_map/psum | solution.py:65
  438.1 21.9 %all_gather.28 = bf16[128,512]{1,0:T(8,128)(2,1)S(1)} all-gather(bf16[16,512]{1,0:T(8,128)(2,1)S(1)} %fusion.101), channel_id=1, replica_groups=mesh['wide'=16,'narrow'=8] {'narrow'}, dimensions={0}, use_global_device_ids=true | all-gather | bytes 147456 | tf_op jit(solution)/shard_map/all_gather | solution.py:66
  460.0 1.2 fusion.32
  461.3 64.2 %reduce-scatter.19.cloned.1.call-done = f32[8,1280]{1,0:T(8,128)} async-done(((f32[128,1280]{1,0:T(8,128)}), f32[8,1280]{1,0:T(8,128)}) %reduce-scatter.19.cloned.1.call-update) | async-done | bytes 40976 | tf_op jit(solution)/shard_map/reduce_scatter | solution.py:155
  527.3 2.7 fusion.129
  530.7 2.3 fusion.75
  533.1 24.8 %all_gather.29 = bf16[128,1024]{1,0:T(8,128)(2,1)S(1)} all-gather(bf16[8,1024]{1,0:T(8,128)(2,1)S(1)} %bitcast.163), channel_id=1, replica_groups=mesh['wide'=16,'narrow'=8] {'wide'}, dimensions={0}, use_global_device_ids=true | all-gather | bytes 278528 | tf_op jit(solution)/shard_map/all_gather | solution.py:174
  558.9 29.5 %reduce-scatter.21.cloned.1.call-done = f32[16,512]{1,0:T(8,128)} async-done(((f32[128,512]{1,0:T(8,128)}), f32[16,512]{1,0:T(8,128)}) %reduce-scatter.21.cloned.1.call-update) | async-done | bytes 32784 | tf_op jit(solution)/shard_map/reduce_scatter | solution.py:175
  589.4 38.3 %psum.31 = f32[16]{0:T(128)S(1)} all-reduce(f32[16]{0:T(128)S(1)} %get-tuple-element.2), channel_id=1, replica_groups=mesh['wide'=16,'narrow'=8] {'wide'}, use_global_device_ids=true, to_apply=%region_18.19 | all-reduce | flops 16 | bytes 128 | tf_op jit(solution)/shard_map/psum | solution.py:65
  627.8 21.9 %all_gather.30 = bf16[128,512]{1,0:T(8,128)(2,1)S(1)} all-gather(bf16[16,512]{1,0:T(8,128)(2,1)S(1)} %fusion.105), channel_id=1, replica_groups=mesh['wide'=16,'narrow'=8] {'narrow'}, dimensions={0}, use_global_device_ids=true | all-gather | bytes 147456 | tf_op jit(solution)/shard_map/all_gather | solution.py:66
  649.7 4.2 fusion.12
  653.9 1.4 copy.61
  655.4 68.2 %reduce-scatter.27.cloned.1.call-done = bf16[8,7168]{1,0:T(8,128)(2,1)} async-done(((bf16[128,7168]{1,0:T(8,128)(2,1)}), bf16[8,7168]{1,0:T(8,128)(2,1)}) %reduce-scatter.27.cloned.1.call-update) | async-done | bytes 114704
  724.5 26.7 %all_gather.31 = bf16[128,3584]{1,0:T(8,128)(2,1)S(1)} all-gather(bf16[8,3584]{1,0:T(8,128)(2,1)S(1)} %fusion.84), channel_id=1, replica_groups=mesh['wide'=16,'narrow'=8] {'wide'}, dimensions={0}, use_global_device_ids=true | all-gather | bytes 974848 | tf_op jit(solution)/shard_map/all_gather | solution.py:191
  751.2 3.4 fusion.133
  755.2 29.3 %reduce-scatter.23.cloned.1.call-done = f32[16,512]{1,0:T(8,128)} async-done(((f32[128,512]{1,0:T(8,128)}), f32[16,512]{1,0:T(8,128)}) %reduce-scatter.23.cloned.1.call-update) | async-done | bytes 32784 | tf_op jit(solution)/shard_map/reduce_scatter | solution.py:195
  784.5 1.4 fusion.106
  (79 shorter events, 17.0 us)
Async XLA Ops:
  7.2 60.3 %copy-start = (bf16[512,1,1280]{2,0,1:T(8,128)(2,1)S(1)}, bf16[512,1,1280]{2,0,1:T(8,128)(2,1)}, u32[]{:S(2)}) copy-start(bf16[512,1,1280]{2,0,1:T(8,128)(2,1)} %param.12) | copy-start | bytes 3932164
  7.2 61.6 %copy-start.4 = (s32[8]{0:T(128)S(1)}, s32[8]{0:T(128)}, u32[]{:S(2)}) copy-start(s32[8]{0:T(128)} %param.10) | copy-start | bytes 100
  7.2 132.4 %reduce-scatter.13.cloned.1.call-start = ((), (), s32[]{:S(2)}) async-start(), calls=%async_computation.8 | async-start | bytes 696320 | tf_op jit(solution)/shard_map/reduce_scatter | solution.py:155
  68.7 134.0 %reduce-scatter.15.cloned.1.call-start = ((), (), s32[]{:S(2)}) async-start(), calls=%async_computation.9 | async-start | bytes 294912 | tf_op jit(solution)/shard_map/reduce_scatter | solution.py:175
  144.8 27.2 %copy-start.1 = (bf16[1024,512]{1,0:T(8,128)(2,1)S(1)}, bf16[1024,512]{1,0:T(8,128)(2,1)}, u32[]{:S(2)}) copy-start(bf16[1024,512]{1,0:T(8,128)(2,1)} %param.13) | copy-start | bytes 3145732
  144.8 28.3 %copy-start.3 = (bf16[512]{0:T(512)(128)(2,1)S(1)}, bf16[512]{0:T(512)(128)(2,1)}, u32[]{:S(2)}) copy-start(bf16[512]{0:T(512)(128)(2,1)} %param.17) | copy-start | bytes 3076
  144.8 57.8 %copy-start.2 = (bf16[16,512]{1,0:T(8,128)(2,1)S(1)}, bf16[16,512]{1,0:T(8,128)(2,1)}, u32[]{:S(2)}) copy-start(bf16[16,512]{1,0:T(8,128)(2,1)} %param.9) | copy-start | bytes 49156
  173.1 164.7 %reduce-scatter.25.cloned.1.call-start = ((), (), s32[]{:S(2)}) async-start(), calls=%async_computation.14 | async-start | bytes 1949696
  269.6 129.2 %reduce-scatter.17.cloned.1.call-start = ((), (), s32[]{:S(2)}) async-start(), calls=%async_computation.10 | async-start | bytes 294912 | tf_op jit(solution)/shard_map/reduce_scatter | solution.py:195
  368.8 156.7 %reduce-scatter.19.cloned.1.call-start = ((), (), s32[]{:S(2)}) async-start(), calls=%async_computation.11 | async-start | bytes 696320 | tf_op jit(solution)/shard_map/reduce_scatter | solution.py:155
  461.2 127.3 %reduce-scatter.21.cloned.1.call-start = ((), (), s32[]{:S(2)}) async-start(), calls=%async_computation.12 | async-start | bytes 294912 | tf_op jit(solution)/shard_map/reduce_scatter | solution.py:175
  558.9 164.7 %reduce-scatter.27.cloned.1.call-start = ((), (), s32[]{:S(2)}) async-start(), calls=%async_computation.15 | async-start | bytes 1949696
  655.4 129.2 %reduce-scatter.23.cloned.1.call-start = ((), (), s32[]{:S(2)}) async-start(), calls=%async_computation.13 | async-start | bytes 294912 | tf_op jit(solution)/shard_map/reduce_scatter | solution.py:195
Sparse Core Ops, SparseCore 0:
  68.8 70.7 reduce-scatter.12
  173.2 29.4 reduce-scatter.14
  269.7 68.0 reduce-scatter.24
  368.9 29.8 reduce-scatter.16
  461.3 64.1 reduce-scatter.18
  559.0 29.4 reduce-scatter.20
  655.5 68.0 reduce-scatter.26
  754.7 29.7 reduce-scatter.22

commit v2 on v0

--- a/solution.py
+++ b/solution.py
@@ -142,6 +142,28 @@
     )
 
 
+def split_hi_lo(values):
+    high = values.astype(jnp.bfloat16)
+    low = (values - high.astype(jnp.float32)).astype(jnp.bfloat16)
+    return high, low
+
+
+def gathered_rows(stream, gain):
+    floats = stream.astype(jnp.float32)
+    square_sum = jnp.sum(floats * floats, axis=1)
+    scaled = (floats * gain.astype(jnp.float32)[None, :]).astype(jnp.bfloat16)
+    high, low = split_hi_lo(square_sum)
+    packed = jnp.concatenate([scaled, high[:, None], low[:, None]], axis=1)
+    rows = gathered_copies(packed, "narrow", 0)
+    width = stream.shape[1]
+    partial_sum = rows[:, width].astype(jnp.float32) + rows[:, width + 1].astype(jnp.float32)
+    return rows[:, :width], partial_sum
+
+
+def row_scale(square_sum):
+    return lax.rsqrt(square_sum / D + EPSILON)
+
+
 def on_device(
     hidden_in, lengths, kv_cache, qkv_weight, o_weight, gate_up, down_weight, attn_gain, mlp_gain
 ):
@@ -149,13 +171,10 @@
     heads_kv = qkv_weight.shape[1]
     hidden_dev = down_weight.shape[0]
     flat_qkv = qkv_weight.reshape(width_dev, -1)
-    flat_gate = gate_up.reshape(width_dev, -1)
     stream = hidden_in
     entries = []
     for layer_index in range(LAYERS):
-        normed = norm_rows(stream, attn_gain)
-        total_rows = normed.shape[0]
-        rows_in = normed
+        rows_in = norm_rows(stream, attn_gain)
         own_qkv = summed_on_arrival(
             jnp.dot(rows_in, flat_qkv, preferred_element_type=jnp.float32), "wide", 0
         )
@@ -177,14 +196,29 @@
             jnp.dot(heads_all, o_weight, preferred_element_type=jnp.float32), "narrow", 0
         )
         stream = (stream.astype(jnp.float32) + summed).astype(jnp.bfloat16)
-        normed = norm_rows(stream, mlp_gain)
-        both_parts = jnp.dot(normed, flat_gate, preferred_element_type=jnp.float32).reshape(
-            total_rows, 2, hidden_dev
-        )
-        own_cols = sent_and_summed(both_parts.astype(jnp.bfloat16), "wide", 2)
-        activated = (jax.nn.silu(own_cols[:, 0]) * own_cols[:, 1]).astype(jnp.bfloat16)
+        rows_in, partial_sum = gathered_rows(stream, mlp_gain)
+        gate_part = jnp.dot(rows_in, gate_up[:, 0, :], preferred_element_type=jnp.float32)
+        up_part = jnp.dot(rows_in, gate_up[:, 1, :], preferred_element_type=jnp.float32)
+        high, low = split_hi_lo(partial_sum)
+        own = sent_and_summed(
+            jnp.concatenate(
+                [
+                    gate_part.astype(jnp.bfloat16),
+                    up_part.astype(jnp.bfloat16),
+                    high[:, None],
+                    low[:, None],
+                ],
+                axis=1,
+            ),
+            "wide",
+            0,
+        )
+        scale = row_scale(own[:, 2 * hidden_dev] + own[:, 2 * hidden_dev + 1])[:, None]
+        gate = own[:, :hidden_dev] * scale
+        up = own[:, hidden_dev : 2 * hidden_dev] * scale
+        activated = (jax.nn.silu(gate) * up).astype(jnp.bfloat16)
         partial_down = jnp.dot(
-            gathered_copies(activated, "wide", 1), down_weight, preferred_element_type=jnp.float32
+            gathered_copies(activated, "wide", 0), down_weight, preferred_element_type=jnp.float32
         )
         summed = summed_on_arrival(partial_down, "narrow", 0)
         stream = (stream.astype(jnp.float32) + summed).astype(jnp.bfloat16)

time: 351 us -> 325 us (0.926)
  blocking collectives: 208 us -> 190 us
  local copies, waits for them, and re-layouts: 32.9 us -> 24.6 us
    slice x0 -> x3, local copies, waits for them, and re-layouts: none -> 15.5 us  [the longest x1 15.3 us: on_device(): gate_up[:, 1, :]]
    dot_general x3 -> x0, local copies, waits for them, and re-layouts: 14.1 us -> none  [the longest x1 10.4 us: on_device(): jnp.dot(normed, flat_gate, preferred_element_type=jnp.float32)]
    all_to_all x8 -> x7, blocking collectives: 101 us -> 90.6 us  [copy_for_each(): lax.all_to_all(jnp.broadcast_to(shard[None], (length, *shard.shape)), axi...]
    all_to_all x4 -> x3, blocking collectives: 47.6 us -> 38.1 us  [summed_on_arrival(): lax.all_to_all(parts, axis, split_axis=0, concat_axis=0, tiled=True)]
    unnamed x15 -> x22, local copies, waits for them, and re-layouts: 7.91 us -> 0.38 us
    all_to_all x4 -> x3, waiting for transfers between devices: 17.3 us -> 10.3 us  [copy_for_each(): lax.all_to_all(jnp.broadcast_to(shard[None], (length, *shard.shape)), axi...]
    all_to_all x2 -> x3, waiting for transfers between devices: 18.1 us -> 24.9 us  [summed_on_arrival(): lax.all_to_all(parts, axis, split_axis=0, concat_axis=0, tiled=True)]
    concatenate x0 -> x6, local copies, waits for them, and re-layouts: none -> 6.06 us  [on_device(): jnp.concatenate([gate_part.astype(jnp.bfloat16), up_part.astype(jnp.bfloa...]
where the time goes in v2:
time: 325 us; the launch traced here: 323 us
  blocking collectives  190 us (58%)
  waiting for transfers between devices  35.2 us (11%)
  matrix products  34.1 us (10%)
  starting transfers between devices  29.2 us (9%)
  local copies, waits for them, and re-layouts  24.6 us (8%)
  other arithmetic  9.07 us (3%)
    all_to_all x7, blocking collectives, copy_for_each(): lax.all_to_all(jnp.broadcast_to(shard[None], (length, *shard.shape)), axi...  90.6 us
    all_to_all x2, blocking collectives, sent_and_summed(): lax.all_to_all(in_blocks(shard, dim, length), axis, 0, 0, tiled=True)  61.5 us
    all_to_all x3, blocking collectives, summed_on_arrival(): lax.all_to_all(parts, axis, split_axis=0, concat_axis=0, tiled=True)  38.1 us
    all_to_all x3, waiting for transfers between devices, summed_on_arrival(): lax.all_to_all(parts, axis, split_axis=0, concat_axis=0, tiled=True)  24.9 us
    all_to_all x3, starting transfers between devices, copy_for_each(): lax.all_to_all(jnp.broadcast_to(shard[None], (length, *shard.shape)), axi...  17 us
    slice x1, local copies, waits for them, and re-layouts, on_device(): gate_up[:, 1, :]  15.3 us
    all_to_all x3, starting transfers between devices, summed_on_arrival(): lax.all_to_all(parts, axis, split_axis=0, concat_axis=0, tiled=True)  12.3 us
    all_to_all x3, waiting for transfers between devices, copy_for_each(): lax.all_to_all(jnp.broadcast_to(shard[None], (length, *shard.shape)), axi...  10.3 us
  transfers between devices with their start and end apart: 6, of which 5 were waited for; matrix products, arithmetic and copies ran while one was open for 6% of the time, Pallas kernels for 0%

profile of v2, /device:TPU:1, one launch (start us, length us, event | category | flops | bytes accessed | tf_op | source)
XLA Modules:
  0.0 323.5 jit_solution(1275273491196581720)
XLA Ops:
  2.2 8.4 %all-to-all-start = ((f32[16,1,16]{2,1,0:T(1,128)}), f32[16,1,16]{2,1,0:T(1,128)S(1)}, u32[]{:S(2)}, u32[]{:S(2)}) async-start(f32[16,1,16]{2,1,0:T(1,128)} %broadcast_in_dim.41), calls=%async_computation | async-start | bytes 16384 | tf_op jit(solution)/shard_map/all_to_all | solution.py:19
  12.1 5.4 %all-to-all-done = f32[16,1,16]{2,1,0:T(1,128)S(1)} async-done(((f32[16,1,16]{2,1,0:T(1,128)}), f32[16,1,16]{2,1,0:T(1,128)S(1)}, u32[]{:S(2)}, u32[]{:S(2)}) %all-to-all-start) | async-done | bytes 1056 | tf_op jit(solution)/shard_map/all_to_all | solution.py:19
  19.0 5.1 %all-to-all-start.1 = ((bf16[8,16,512]{2,1,0:T(8,128)(2,1)}), bf16[8,16,512]{2,1,0:T(8,128)(2,1)S(1)}, u32[]{:S(2)}, u32[]{:S(2)}) async-start(bf16[8,16,512]{2,1,0:T(8,128)(2,1)} %broadcast_in_dim.42), calls=%async_computation.1 | async-start | bytes 262144 | tf_op jit(solution)/shard_map/all_to_all | solution.py:19
  24.9 4.8 %all-to-all-done.1 = bf16[8,16,512]{2,1,0:T(8,128)(2,1)S(1)} async-done(((bf16[8,16,512]{2,1,0:T(8,128)(2,1)}), bf16[8,16,512]{2,1,0:T(8,128)(2,1)S(1)}, u32[]{:S(2)}, u32[]{:S(2)}) %all-to-all-start.1) | async-done | bytes 131104 | tf_op jit(solution)/shard_map/all_to_all | solution.py:19
  31.0 5.4 %all-to-all-start.2 = ((f32[16,8,1280]{2,1,0:T(8,128)}), f32[16,8,1280]{2,1,0:T(8,128)S(1)}, u32[]{:S(2)}, u32[]{:S(2)}) async-start(f32[16,8,1280]{2,1,0:T(8,128)} %fusion.26), calls=%async_computation.2 | async-start | bytes 1310720 | tf_op jit(solution)/shard_map/all_to_all | solution.py:46
  36.7 12.0 %all-to-all-done.2 = f32[16,8,1280]{2,1,0:T(8,128)S(1)} async-done(((f32[16,8,1280]{2,1,0:T(8,128)}), f32[16,8,1280]{2,1,0:T(8,128)S(1)}, u32[]{:S(2)}, u32[]{:S(2)}) %all-to-all-start.2) | async-done | bytes 655392 | tf_op jit(solution)/shard_map/all_to_all | solution.py:46
  49.2 2.7 fusion.137
  55.0 13.0 %all_to_all.92 = bf16[16,8,1024]{2,1,0:T(8,128)(2,1)S(1)} all-to-all(bf16[16,8,1024]{2,1,0:T(8,128)(2,1)S(1)} %broadcast_in_dim.45), channel_id=1, replica_groups=mesh['wide'=16,'narrow'=8] {'wide'}, dimensions={0} | all-to-all | bytes 524288 | tf_op jit(solution)/shard_map/all_to_all | solution.py:19
  69.0 3.4 %all-to-all-start.4 = ((f32[8,16,512]{2,1,0:T(8,128)}), f32[8,16,512]{2,1,0:T(8,128)S(1)}, u32[]{:S(2)}, u32[]{:S(2)}) async-start(f32[8,16,512]{2,1,0:T(8,128)} %fusion.74), calls=%async_computation.4 | async-start | bytes 524288 | tf_op jit(solution)/shard_map/all_to_all | solution.py:46
  72.4 6.9 %all-to-all-done.4 = f32[8,16,512]{2,1,0:T(8,128)S(1)} async-done(((f32[8,16,512]{2,1,0:T(8,128)}), f32[8,16,512]{2,1,0:T(8,128)S(1)}, u32[]{:S(2)}, u32[]{:S(2)}) %all-to-all-start.4) | async-done | bytes 262176 | tf_op jit(solution)/shard_map/all_to_all | solution.py:46
  80.4 3.4 %all-to-all-start.5 = ((bf16[8,16,514]{2,1,0:T(8,128)(2,1)}), bf16[8,16,514]{2,1,0:T(8,128)(2,1)S(1)}, u32[]{:S(2)}, u32[]{:S(2)}) async-start(bf16[8,16,514]{2,1,0:T(8,128)(2,1)} %broadcast_in_dim.46), calls=%async_computation.5 | async-start | bytes 327680 | tf_op jit(solution)/shard_map/all_to_all | solution.py:19
  83.8 15.3 %fusion.132 = (bf16[512,1,3584]{2,1,0:T(2,128)(2,1)}, bf16[512,1,3584]{2,1,0:T(2,128)(2,1)}) fusion(bf16[512,2,3584]{2,1,0:T(2,128)(2,1)} %param.14), kind=kLoop, calls=%fused_computation.178 | loop fusion | bytes 14680064 | tf_op jit(solution)/shard_map/slice | solution.py:201
  99.9 4.7 %fusion.3 = bf16[16,8,3584]{2,1,0:T(8,128)(2,1)} fusion(bf16[512,1,3584]{2,1,0:T(2,128)(2,1)} %get-tuple-element.12, bf16[128,514]{1,0:T(8,128)(2,1)S(1)} %bitcast.176), kind=kOutput, calls=%fused_computation.9 | convolution fusion | flops 470220800 | bytes 4718592 | tf_op jit(solution)/shard_map/dot_general | solution.py:201
  104.6 4.7 %fusion.2 = bf16[16,8,3584]{2,1,0:T(8,128)(2,1)} fusion(bf16[512,1,3584]{2,1,0:T(2,128)(2,1)} %get-tuple-element.13, bf16[128,514]{1,0:T(8,128)(2,1)S(1)} %bitcast.177), kind=kOutput, calls=%fused_computation.8 | convolution fusion | flops 470220800 | bytes 4718592 | tf_op jit(solution)/shard_map/dot_general | solution.py:200
  109.3 2.6 concatenate.42
  111.8 29.9 %all_to_all.93 = bf16[16,8,7170]{2,1,0:T(8,128)(2,1)S(1)} all-to-all(bf16[16,8,7170]{2,1,0:T(8,128)(2,1)S(1)} %concatenate.42), channel_id=1, replica_groups=mesh['wide'=16,'narrow'=8] {'wide'}, dimensions={0} | all-to-all | bytes 3671040 | tf_op jit(solution)/shard_map/all_to_all | solution.py:52
  142.4 18.7 %all_to_all.94 = bf16[16,8,3584]{2,1,0:T(8,128)(2,1)S(1)} all-to-all(bf16[16,8,3584]{2,1,0:T(8,128)(2,1)S(1)} %broadcast_in_dim.47), channel_id=1, replica_groups=mesh['wide'=16,'narrow'=8] {'wide'}, dimensions={0} | all-to-all | bytes 1835008 | tf_op jit(solution)/shard_map/all_to_all | solution.py:19
  161.8 11.2 %all_to_all.95 = f32[8,16,512]{2,1,0:T(8,128)S(1)} all-to-all(f32[8,16,512]{2,1,0:T(8,128)S(1)} %fusion.8), channel_id=1, replica_groups=mesh['wide'=16,'narrow'=8] {'narrow'}, dimensions={0} | all-to-all | bytes 524288 | tf_op jit(solution)/shard_map/all_to_all | solution.py:46
  173.2 12.5 %all_to_all.96 = f32[16,1,16]{2,1,0:T(1,128)S(1)} all-to-all(f32[16,1,16]{2,1,0:T(1,128)S(1)} %broadcast_in_dim.48), channel_id=1, replica_groups=mesh['wide'=16,'narrow'=8] {'wide'}, dimensions={0} | all-to-all | bytes 2048 | tf_op jit(solution)/shard_map/all_to_all | solution.py:19
  185.8 7.9 %all_to_all.97 = bf16[8,16,512]{2,1,0:T(8,128)(2,1)S(1)} all-to-all(bf16[8,16,512]{2,1,0:T(8,128)(2,1)S(1)} %broadcast_in_dim.49), channel_id=1, replica_groups=mesh['wide'=16,'narrow'=8] {'narrow'}, dimensions={0} | all-to-all | bytes 262144 | tf_op jit(solution)/shard_map/all_to_all | solution.py:19
  194.1 17.5 %all_to_all.98 = f32[16,8,1280]{2,1,0:T(8,128)S(1)} all-to-all(f32[16,8,1280]{2,1,0:T(8,128)S(1)} %fusion.24), channel_id=1, replica_groups=mesh['wide'=16,'narrow'=8] {'wide'}, dimensions={0} | all-to-all | bytes 1310720 | tf_op jit(solution)/shard_map/all_to_all | solution.py:46
  212.0 2.7 fusion.138
  217.9 11.7 %all_to_all.99 = bf16[16,8,1024]{2,1,0:T(8,128)(2,1)S(1)} all-to-all(bf16[16,8,1024]{2,1,0:T(8,128)(2,1)S(1)} %broadcast_in_dim.51), channel_id=1, replica_groups=mesh['wide'=16,'narrow'=8] {'wide'}, dimensions={0} | all-to-all | bytes 524288 | tf_op jit(solution)/shard_map/all_to_all | solution.py:19
  229.9 9.4 %all_to_all.100 = f32[8,16,512]{2,1,0:T(8,128)S(1)} all-to-all(f32[8,16,512]{2,1,0:T(8,128)S(1)} %fusion.72), channel_id=1, replica_groups=mesh['wide'=16,'narrow'=8] {'narrow'}, dimensions={0} | all-to-all | bytes 524288 | tf_op jit(solution)/shard_map/all_to_all | solution.py:46
  239.8 8.1 %all_to_all.101 = bf16[8,16,514]{2,1,0:T(8,128)(2,1)S(1)} all-to-all(bf16[8,16,514]{2,1,0:T(8,128)(2,1)S(1)} %broadcast_in_dim.52), channel_id=1, replica_groups=mesh['wide'=16,'narrow'=8] {'narrow'}, dimensions={0} | all-to-all | bytes 263168 | tf_op jit(solution)/shard_map/all_to_all | solution.py:19
  247.9 4.7 %fusion.5 = bf16[16,8,3584]{2,1,0:T(8,128)(2,1)} fusion(bf16[512,1,3584]{2,1,0:T(2,128)(2,1)} %get-tuple-element.12, bf16[128,514]{1,0:T(8,128)(2,1)S(1)} %bitcast.178), kind=kOutput, calls=%fused_computation.11 | convolution fusion | flops 470220800 | bytes 4718592 | tf_op jit(solution)/shard_map/dot_general | solution.py:201
  252.5 4.7 %fusion.4 = bf16[16,8,3584]{2,1,0:T(8,128)(2,1)} fusion(bf16[512,1,3584]{2,1,0:T(2,128)(2,1)} %get-tuple-element.13, bf16[128,514]{1,0:T(8,128)(2,1)S(1)} %bitcast.179), kind=kOutput, calls=%fused_computation.10 | convolution fusion | flops 470220800 | bytes 4718592 | tf_op jit(solution)/shard_map/dot_general | solution.py:200
  257.9 2.6 concatenate.49
  260.5 31.5 %all_to_all.102 = bf16[16,8,7170]{2,1,0:T(8,128)(2,1)S(1)} all-to-all(bf16[16,8,7170]{2,1,0:T(8,128)(2,1)S(1)} %concatenate.49), channel_id=1, replica_groups=mesh['wide'=16,'narrow'=8] {'wide'}, dimensions={0} | all-to-all | bytes 3671040 | tf_op jit(solution)/shard_map/all_to_all | solution.py:52
  292.7 18.7 %all_to_all.103 = bf16[16,8,3584]{2,1,0:T(8,128)(2,1)S(1)} all-to-all(bf16[16,8,3584]{2,1,0:T(8,128)(2,1)S(1)} %broadcast_in_dim.53), channel_id=1, replica_groups=mesh['wide'=16,'narrow'=8] {'wide'}, dimensions={0} | all-to-all | bytes 1835008 | tf_op jit(solution)/shard_map/all_to_all | solution.py:19
  312.8 3.4 %all-to-all-start.17 = ((f32[8,16,512]{2,1,0:T(8,128)}), f32[8,16,512]{2,1,0:T(8,128)S(1)}, u32[]{:S(2)}, u32[]{:S(2)}) async-start(f32[8,16,512]{2,1,0:T(8,128)} %fusion.6), calls=%async_computation.17 | async-start | bytes 524288 | tf_op jit(solution)/shard_map/all_to_all | solution.py:46
  316.8 6.0 %all-to-all-done.17 = f32[8,16,512]{2,1,0:T(8,128)S(1)} async-done(((f32[8,16,512]{2,1,0:T(8,128)}), f32[8,16,512]{2,1,0:T(8,128)S(1)}, u32[]{:S(2)}, u32[]{:S(2)}) %all-to-all-start.17) | async-done | bytes 262176 | tf_op jit(solution)/shard_map/all_to_all | solution.py:46
  (113 shorter events, 23.2 us)
Async XLA Ops:
  0.6 29.1 %copy-start = (bf16[512,1,1280]{2,0,1:T(8,128)(2,1)S(1)}, bf16[512,1,1280]{2,0,1:T(8,128)(2,1)}, u32[]{:S(2)}) copy-start(bf16[512,1,1280]{2,0,1:T(8,128)(2,1)} %param.12) | copy-start | bytes 3932164
  2.2 15.4 %all-to-all-start = ((f32[16,1,16]{2,1,0:T(1,128)}), f32[16,1,16]{2,1,0:T(1,128)S(1)}, u32[]{:S(2)}, u32[]{:S(2)}) async-start(f32[16,1,16]{2,1,0:T(1,128)} %broadcast_in_dim.41), calls=%async_computation | async-start | bytes 16384 | tf_op jit(solution)/shard_map/all_to_all | solution.py:19
  19.0 10.7 %all-to-all-start.1 = ((bf16[8,16,512]{2,1,0:T(8,128)(2,1)}), bf16[8,16,512]{2,1,0:T(8,128)(2,1)S(1)}, u32[]{:S(2)}, u32[]{:S(2)}) async-start(bf16[8,16,512]{2,1,0:T(8,128)(2,1)} %broadcast_in_dim.42), calls=%async_computation.1 | async-start | bytes 262144 | tf_op jit(solution)/shard_map/all_to_all | solution.py:19
  31.0 17.8 %all-to-all-start.2 = ((f32[16,8,1280]{2,1,0:T(8,128)}), f32[16,8,1280]{2,1,0:T(8,128)S(1)}, u32[]{:S(2)}, u32[]{:S(2)}) async-start(f32[16,8,1280]{2,1,0:T(8,128)} %fusion.26), calls=%async_computation.2 | async-start | bytes 1310720 | tf_op jit(solution)/shard_map/all_to_all | solution.py:46
  52.5 15.5 %copy-start.3 = (bf16[1024,512]{1,0:T(8,128)(2,1)S(1)}, bf16[1024,512]{1,0:T(8,128)(2,1)}, u32[]{:S(2)}) copy-start(bf16[1024,512]{1,0:T(8,128)(2,1)} %param.13) | copy-start | bytes 3145732
  54.9 17.5 %copy-start.6 = (bf16[512]{0:T(512)(128)(2,1)S(1)}, bf16[512]{0:T(512)(128)(2,1)}, u32[]{:S(2)}) copy-start(bf16[512]{0:T(512)(128)(2,1)} %param.17) | copy-start | bytes 3076
  55.0 24.4 %copy-start.5 = (bf16[16,512]{1,0:T(8,128)(2,1)S(1)}, bf16[16,512]{1,0:T(8,128)(2,1)}, u32[]{:S(2)}) copy-start(bf16[16,512]{1,0:T(8,128)(2,1)} %param.9) | copy-start | bytes 49156
  69.0 10.3 %all-to-all-start.4 = ((f32[8,16,512]{2,1,0:T(8,128)}), f32[8,16,512]{2,1,0:T(8,128)S(1)}, u32[]{:S(2)}, u32[]{:S(2)}) async-start(f32[8,16,512]{2,1,0:T(8,128)} %fusion.74), calls=%async_computation.4 | async-start | bytes 524288 | tf_op jit(solution)/shard_map/all_to_all | solution.py:46
  80.4 18.7 %all-to-all-start.5 = ((bf16[8,16,514]{2,1,0:T(8,128)(2,1)}), bf16[8,16,514]{2,1,0:T(8,128)(2,1)S(1)}, u32[]{:S(2)}, u32[]{:S(2)}) async-start(bf16[8,16,514]{2,1,0:T(8,128)(2,1)} %broadcast_in_dim.46), calls=%async_computation.5 | async-start | bytes 327680 | tf_op jit(solution)/shard_map/all_to_all | solution.py:19
  141.8 19.4 %copy-start.1 = (bf16[3584,512]{1,0:T(8,128)(2,1)S(1)}, bf16[3584,512]{1,0:T(8,128)(2,1)}, u32[]{:S(2)}) copy-start(bf16[3584,512]{1,0:T(8,128)(2,1)} %param.15) | copy-start | bytes 11010052
  215.4 14.2 %copy-start.4 = (bf16[1024,512]{1,0:T(8,128)(2,1)S(1)}, bf16[1024,512]{1,0:T(8,128)(2,1)}, u32[]{:S(2)}) copy-start(bf16[1024,512]{1,0:T(8,128)(2,1)} %param.13) | copy-start | bytes 3145732
  292.0 19.4 %copy-start.2 = (bf16[3584,512]{1,0:T(8,128)(2,1)S(1)}, bf16[3584,512]{1,0:T(8,128)(2,1)}, u32[]{:S(2)}) copy-start(bf16[3584,512]{1,0:T(8,128)(2,1)} %param.15) | copy-start | bytes 11010052
  312.8 10.1 %all-to-all-start.17 = ((f32[8,16,512]{2,1,0:T(8,128)}), f32[8,16,512]{2,1,0:T(8,128)S(1)}, u32[]{:S(2)}, u32[]{:S(2)}) async-start(f32[8,16,512]{2,1,0:T(8,128)} %fusion.6), calls=%async_computation.17 | async-start | bytes 524288 | tf_op jit(solution)/shard_map/all_to_all | solution.py:46

commit v3 on v2

--- a/solution.py
+++ b/solution.py
@@ -197,25 +197,19 @@
         )
         stream = (stream.astype(jnp.float32) + summed).astype(jnp.bfloat16)
         rows_in, partial_sum = gathered_rows(stream, mlp_gain)
-        gate_part = jnp.dot(rows_in, gate_up[:, 0, :], preferred_element_type=jnp.float32)
-        up_part = jnp.dot(rows_in, gate_up[:, 1, :], preferred_element_type=jnp.float32)
+        both_parts = jnp.einsum(
+            "rd,dkh->krh", rows_in, gate_up, preferred_element_type=jnp.float32
+        ).astype(jnp.bfloat16)
         high, low = split_hi_lo(partial_sum)
-        own = sent_and_summed(
-            jnp.concatenate(
-                [
-                    gate_part.astype(jnp.bfloat16),
-                    up_part.astype(jnp.bfloat16),
-                    high[:, None],
-                    low[:, None],
-                ],
-                axis=1,
-            ),
-            "wide",
-            0,
-        )
-        scale = row_scale(own[:, 2 * hidden_dev] + own[:, 2 * hidden_dev + 1])[:, None]
-        gate = own[:, :hidden_dev] * scale
-        up = own[:, hidden_dev : 2 * hidden_dev] * scale
+        sums_col = jnp.stack([high, low])[:, :, None]
+        payload = jnp.concatenate([both_parts, sums_col], axis=2)
+        wide_size = lax.axis_size("wide")
+        payload = payload.reshape(2, wide_size, -1, hidden_dev + 1)
+        arrived = lax.all_to_all(payload, "wide", 1, 1, tiled=True)
+        own = jnp.sum(arrived.astype(jnp.float32), axis=1)
+        scale = row_scale(own[0, :, hidden_dev] + own[1, :, hidden_dev])[:, None]
+        gate = own[0, :, :hidden_dev] * scale
+        up = own[1, :, :hidden_dev] * scale
         activated = (jax.nn.silu(gate) * up).astype(jnp.bfloat16)
         partial_down = jnp.dot(
             gathered_copies(activated, "wide", 0), down_weight, preferred_element_type=jnp.float32

time: 325 us -> 297 us (0.914)
  local copies, waits for them, and re-layouts: 24.6 us -> 2.78 us
  matrix products: 34.1 us -> 23.8 us
  blocking collectives: 190 us -> 197 us
  starting transfers between devices: 29.2 us -> 25.8 us
    slice x3 -> x0, local copies, waits for them, and re-layouts: 15.5 us -> none  [the longest x1 15.3 us: on_device(): gate_up[:, 1, :]]
    dot_general x4 -> x2, matrix products: 18.7 us -> 8.43 us  [on_device(): jnp.einsum('rd,dkh->krh', rows_in, gate_up, preferred_element_type=jnp.fl...]
    all_to_all x7 -> x8, blocking collectives: 90.6 us -> 97.9 us  [copy_for_each(): lax.all_to_all(jnp.broadcast_to(shard[None], (length, *shard.shape)), axi...]
    concatenate x6 -> x0, local copies, waits for them, and re-layouts: 6.06 us -> none  [on_device(): jnp.concatenate([gate_part.astype(jnp.bfloat16), up_part.astype(jnp.bfloa...]
    all_to_all x3 -> x2, starting transfers between devices: 17 us -> 13.6 us  [copy_for_each(): lax.all_to_all(jnp.broadcast_to(shard[None], (length, *shard.shape)), axi...]
    all_to_all x3 -> x2, waiting for transfers between devices: 10.3 us -> 10.3 us  [copy_for_each(): lax.all_to_all(jnp.broadcast_to(shard[None], (length, *shard.shape)), axi...]
  transfers between devices with their start and end apart: 6 -> 5, of which waited for: 5 -> 5; matrix products, arithmetic and copies ran while one was open for 6% -> 1% of each run, Pallas kernels for 0% -> 0%
where the time goes in v3:
time: 297 us; the launch traced here: 295 us
  blocking collectives  197 us (66%)
  waiting for transfers between devices  35.2 us (12%)
  starting transfers between devices  25.8 us (9%)
  matrix products  23.8 us (8%)
  other arithmetic  9.48 us (3%)
    all_to_all x8, blocking collectives, copy_for_each(): lax.all_to_all(jnp.broadcast_to(shard[None], (length, *shard.shape)), axi...  97.9 us
    all_to_all x2, blocking collectives, on_device(): arrived = lax.all_to_all(payload, 'wide', 1, 1, tiled=True)  63.3 us
    all_to_all x3, blocking collectives, summed_on_arrival(): lax.all_to_all(parts, axis, split_axis=0, concat_axis=0, tiled=True)  36.1 us
    all_to_all x3, waiting for transfers between devices, summed_on_arrival(): lax.all_to_all(parts, axis, split_axis=0, concat_axis=0, tiled=True)  24.9 us
    all_to_all x2, starting transfers between devices, copy_for_each(): lax.all_to_all(jnp.broadcast_to(shard[None], (length, *shard.shape)), axi...  13.6 us
    all_to_all x3, starting transfers between devices, summed_on_arrival(): lax.all_to_all(parts, axis, split_axis=0, concat_axis=0, tiled=True)  12.3 us
    all_to_all x2, waiting for transfers between devices, copy_for_each(): lax.all_to_all(jnp.broadcast_to(shard[None], (length, *shard.shape)), axi...  10.3 us
    dot_general x2, matrix products, on_device(): jnp.einsum('rd,dkh->krh', rows_in, gate_up, preferred_element_type=jnp.fl...  8.43 us
  transfers between devices with their start and end apart: 5, of which 5 were waited for; matrix products, arithmetic and copies ran while one was open for 1% of the time, Pallas kernels for 0%

profile of v3, /device:TPU:1, one launch (start us, length us, event | category | flops | bytes accessed | tf_op | source)
XLA Modules:
  0.0 295.4 jit_solution(4781972823896606592)
XLA Ops:
  2.2 8.4 %all-to-all-start = ((f32[16,1,16]{2,1,0:T(1,128)}), f32[16,1,16]{2,1,0:T(1,128)S(1)}, u32[]{:S(2)}, u32[]{:S(2)}) async-start(f32[16,1,16]{2,1,0:T(1,128)} %broadcast_in_dim.45), calls=%async_computation | async-start | bytes 16384 | tf_op jit(solution)/shard_map/all_to_all | solution.py:19
  12.1 5.4 %all-to-all-done = f32[16,1,16]{2,1,0:T(1,128)S(1)} async-done(((f32[16,1,16]{2,1,0:T(1,128)}), f32[16,1,16]{2,1,0:T(1,128)S(1)}, u32[]{:S(2)}, u32[]{:S(2)}) %all-to-all-start) | async-done | bytes 1056 | tf_op jit(solution)/shard_map/all_to_all | solution.py:19
  19.0 5.1 %all-to-all-start.1 = ((bf16[8,16,512]{2,1,0:T(8,128)(2,1)}), bf16[8,16,512]{2,1,0:T(8,128)(2,1)S(1)}, u32[]{:S(2)}, u32[]{:S(2)}) async-start(bf16[8,16,512]{2,1,0:T(8,128)(2,1)} %broadcast_in_dim.46), calls=%async_computation.1 | async-start | bytes 262144 | tf_op jit(solution)/shard_map/all_to_all | solution.py:19
  24.9 4.8 %all-to-all-done.1 = bf16[8,16,512]{2,1,0:T(8,128)(2,1)S(1)} async-done(((bf16[8,16,512]{2,1,0:T(8,128)(2,1)}), bf16[8,16,512]{2,1,0:T(8,128)(2,1)S(1)}, u32[]{:S(2)}, u32[]{:S(2)}) %all-to-all-start.1) | async-done | bytes 131104 | tf_op jit(solution)/shard_map/all_to_all | solution.py:19
  29.8 1.2 fusion.38
  31.0 5.4 %all-to-all-start.2 = ((f32[16,8,1280]{2,1,0:T(8,128)}), f32[16,8,1280]{2,1,0:T(8,128)S(1)}, u32[]{:S(2)}, u32[]{:S(2)}) async-start(f32[16,8,1280]{2,1,0:T(8,128)} %fusion.38), calls=%async_computation.2 | async-start | bytes 1310720 | tf_op jit(solution)/shard_map/all_to_all | solution.py:46
  36.7 12.0 %all-to-all-done.2 = f32[16,8,1280]{2,1,0:T(8,128)S(1)} async-done(((f32[16,8,1280]{2,1,0:T(8,128)}), f32[16,8,1280]{2,1,0:T(8,128)S(1)}, u32[]{:S(2)}, u32[]{:S(2)}) %all-to-all-start.2) | async-done | bytes 655392 | tf_op jit(solution)/shard_map/all_to_all | solution.py:46
  49.2 2.7 fusion.144
  52.5 2.4 fusion.74
  55.0 13.0 %all_to_all.92 = bf16[16,8,1024]{2,1,0:T(8,128)(2,1)S(1)} all-to-all(bf16[16,8,1024]{2,1,0:T(8,128)(2,1)S(1)} %broadcast_in_dim.49), channel_id=1, replica_groups=mesh['wide'=16,'narrow'=8] {'wide'}, dimensions={0} | all-to-all | bytes 524288 | tf_op jit(solution)/shard_map/all_to_all | solution.py:19
  68.0 1.0 fusion.86
  69.0 3.4 %all-to-all-start.4 = ((f32[8,16,512]{2,1,0:T(8,128)}), f32[8,16,512]{2,1,0:T(8,128)S(1)}, u32[]{:S(2)}, u32[]{:S(2)}) async-start(f32[8,16,512]{2,1,0:T(8,128)} %fusion.86), calls=%async_computation.4 | async-start | bytes 524288 | tf_op jit(solution)/shard_map/all_to_all | solution.py:46
  72.4 6.9 %all-to-all-done.4 = f32[8,16,512]{2,1,0:T(8,128)S(1)} async-done(((f32[8,16,512]{2,1,0:T(8,128)}), f32[8,16,512]{2,1,0:T(8,128)S(1)}, u32[]{:S(2)}, u32[]{:S(2)}) %all-to-all-start.4) | async-done | bytes 262176 | tf_op jit(solution)/shard_map/all_to_all | solution.py:46
  79.8 8.1 %all_to_all.93 = bf16[8,16,514]{2,1,0:T(8,128)(2,1)S(1)} all-to-all(bf16[8,16,514]{2,1,0:T(8,128)(2,1)S(1)} %broadcast_in_dim.50), channel_id=1, replica_groups=mesh['wide'=16,'narrow'=8] {'narrow'}, dimensions={0} | all-to-all | bytes 263168 | tf_op jit(solution)/shard_map/all_to_all | solution.py:19
  88.4 4.2 %fusion.15 = bf16[2,16,8,3584]{3,2,1,0:T(8,128)(2,1)S(1)} fusion(bf16[512,2,3584]{2,1,0:T(2,128)(2,1)} %param.14, bf16[128,514]{1,0:T(8,128)(2,1)S(1)} %bitcast.172), kind=kOutput, calls=%fused_computation.11 | convolution fusion | flops 940441600 | bytes 9306112 | tf_op jit(solution)/shard_map/rd,dkh->krh/dot_general | solution.py:200
  92.8 31.5 %all_to_all.94 = bf16[2,16,8,3585]{3,2,0,1:T(8,128)(2,1)S(1)} all-to-all(bf16[2,16,8,3585]{3,2,0,1:T(8,128)(2,1)S(1)} %pad_maximum_fusion), channel_id=1, replica_groups=mesh['wide'=16,'narrow'=8] {'wide'}, dimensions={1} | all-to-all | bytes 3671040 | tf_op jit(solution)/shard_map/all_to_all | solution.py:208
  124.9 18.8 %all_to_all.95 = bf16[16,8,3584]{2,1,0:T(8,128)(2,1)S(1)} all-to-all(bf16[16,8,3584]{2,1,0:T(8,128)(2,1)S(1)} %broadcast_in_dim.52), channel_id=1, replica_groups=mesh['wide'=16,'narrow'=8] {'wide'}, dimensions={0} | all-to-all | bytes 1835008 | tf_op jit(solution)/shard_map/all_to_all | solution.py:19
  144.3 9.2 %all_to_all.96 = f32[8,16,512]{2,1,0:T(8,128)S(1)} all-to-all(f32[8,16,512]{2,1,0:T(8,128)S(1)} %fusion.20), channel_id=1, replica_groups=mesh['wide'=16,'narrow'=8] {'narrow'}, dimensions={0} | all-to-all | bytes 524288 | tf_op jit(solution)/shard_map/all_to_all | solution.py:46
  153.6 11.6 %all_to_all.97 = f32[16,1,16]{2,1,0:T(1,128)S(1)} all-to-all(f32[16,1,16]{2,1,0:T(1,128)S(1)} %broadcast_in_dim.53), channel_id=1, replica_groups=mesh['wide'=16,'narrow'=8] {'wide'}, dimensions={0} | all-to-all | bytes 2048 | tf_op jit(solution)/shard_map/all_to_all | solution.py:19
  165.3 7.9 %all_to_all.98 = bf16[8,16,512]{2,1,0:T(8,128)(2,1)S(1)} all-to-all(bf16[8,16,512]{2,1,0:T(8,128)(2,1)S(1)} %broadcast_in_dim.54), channel_id=1, replica_groups=mesh['wide'=16,'narrow'=8] {'narrow'}, dimensions={0} | all-to-all | bytes 262144 | tf_op jit(solution)/shard_map/all_to_all | solution.py:19
  173.6 17.5 %all_to_all.99 = f32[16,8,1280]{2,1,0:T(8,128)S(1)} all-to-all(f32[16,8,1280]{2,1,0:T(8,128)S(1)} %fusion.36), channel_id=1, replica_groups=mesh['wide'=16,'narrow'=8] {'wide'}, dimensions={0} | all-to-all | bytes 1310720 | tf_op jit(solution)/shard_map/all_to_all | solution.py:46
  191.5 2.7 fusion.145
  194.9 2.4 fusion.79
  197.3 11.7 %all_to_all.100 = bf16[16,8,1024]{2,1,0:T(8,128)(2,1)S(1)} all-to-all(bf16[16,8,1024]{2,1,0:T(8,128)(2,1)S(1)} %broadcast_in_dim.56), channel_id=1, replica_groups=mesh['wide'=16,'narrow'=8] {'wide'}, dimensions={0} | all-to-all | bytes 524288 | tf_op jit(solution)/shard_map/all_to_all | solution.py:19
  209.4 9.4 %all_to_all.101 = f32[8,16,512]{2,1,0:T(8,128)S(1)} all-to-all(f32[8,16,512]{2,1,0:T(8,128)S(1)} %fusion.84), channel_id=1, replica_groups=mesh['wide'=16,'narrow'=8] {'narrow'}, dimensions={0} | all-to-all | bytes 524288 | tf_op jit(solution)/shard_map/all_to_all | solution.py:46
  219.2 8.1 %all_to_all.102 = bf16[8,16,514]{2,1,0:T(8,128)(2,1)S(1)} all-to-all(bf16[8,16,514]{2,1,0:T(8,128)(2,1)S(1)} %broadcast_in_dim.57), channel_id=1, replica_groups=mesh['wide'=16,'narrow'=8] {'narrow'}, dimensions={0} | all-to-all | bytes 263168 | tf_op jit(solution)/shard_map/all_to_all | solution.py:19
  227.5 4.2 %fusion.12 = bf16[2,16,8,3584]{3,2,1,0:T(8,128)(2,1)S(1)} fusion(bf16[512,2,3584]{2,1,0:T(2,128)(2,1)} %param.14, bf16[128,514]{1,0:T(8,128)(2,1)S(1)} %bitcast.174), kind=kOutput, calls=%fused_computation.10 | convolution fusion | flops 940441600 | bytes 9306112 | tf_op jit(solution)/shard_map/rd,dkh->krh/dot_general | solution.py:200
  232.2 31.8 %all_to_all.103 = bf16[2,16,8,3585]{3,2,0,1:T(8,128)(2,1)S(1)} all-to-all(bf16[2,16,8,3585]{3,2,0,1:T(8,128)(2,1)S(1)} %pad_maximum_fusion.1), channel_id=1, replica_groups=mesh['wide'=16,'narrow'=8] {'wide'}, dimensions={1} | all-to-all | bytes 3671040 | tf_op jit(solution)/shard_map/all_to_all | solution.py:208
  264.6 18.8 %all_to_all.104 = bf16[16,8,3584]{2,1,0:T(8,128)(2,1)S(1)} all-to-all(bf16[16,8,3584]{2,1,0:T(8,128)(2,1)S(1)} %broadcast_in_dim.59), channel_id=1, replica_groups=mesh['wide'=16,'narrow'=8] {'wide'}, dimensions={0} | all-to-all | bytes 1835008 | tf_op jit(solution)/shard_map/all_to_all | solution.py:19
  283.4 1.3 fusion.18
  284.7 3.4 %all-to-all-start.17 = ((f32[8,16,512]{2,1,0:T(8,128)}), f32[8,16,512]{2,1,0:T(8,128)S(1)}, u32[]{:S(2)}, u32[]{:S(2)}) async-start(f32[8,16,512]{2,1,0:T(8,128)} %fusion.18), calls=%async_computation.17 | async-start | bytes 524288 | tf_op jit(solution)/shard_map/all_to_all | solution.py:46
  288.7 6.0 %all-to-all-done.17 = f32[8,16,512]{2,1,0:T(8,128)S(1)} async-done(((f32[8,16,512]{2,1,0:T(8,128)}), f32[8,16,512]{2,1,0:T(8,128)S(1)}, u32[]{:S(2)}, u32[]{:S(2)}) %all-to-all-start.17) | async-done | bytes 262176 | tf_op jit(solution)/shard_map/all_to_all | solution.py:46
  (105 shorter events, 13.8 us)
Async XLA Ops:
  0.6 29.1 %copy-start = (bf16[512,1,1280]{2,0,1:T(8,128)(2,1)S(1)}, bf16[512,1,1280]{2,0,1:T(8,128)(2,1)}, u32[]{:S(2)}) copy-start(bf16[512,1,1280]{2,0,1:T(8,128)(2,1)} %param.12) | copy-start | bytes 3932164
  2.2 15.4 %all-to-all-start = ((f32[16,1,16]{2,1,0:T(1,128)}), f32[16,1,16]{2,1,0:T(1,128)S(1)}, u32[]{:S(2)}, u32[]{:S(2)}) async-start(f32[16,1,16]{2,1,0:T(1,128)} %broadcast_in_dim.45), calls=%async_computation | async-start | bytes 16384 | tf_op jit(solution)/shard_map/all_to_all | solution.py:19
  19.0 10.7 %all-to-all-start.1 = ((bf16[8,16,512]{2,1,0:T(8,128)(2,1)}), bf16[8,16,512]{2,1,0:T(8,128)(2,1)S(1)}, u32[]{:S(2)}, u32[]{:S(2)}) async-start(bf16[8,16,512]{2,1,0:T(8,128)(2,1)} %broadcast_in_dim.46), calls=%async_computation.1 | async-start | bytes 262144 | tf_op jit(solution)/shard_map/all_to_all | solution.py:19
  31.0 17.8 %all-to-all-start.2 = ((f32[16,8,1280]{2,1,0:T(8,128)}), f32[16,8,1280]{2,1,0:T(8,128)S(1)}, u32[]{:S(2)}, u32[]{:S(2)}) async-start(f32[16,8,1280]{2,1,0:T(8,128)} %fusion.38), calls=%async_computation.2 | async-start | bytes 1310720 | tf_op jit(solution)/shard_map/all_to_all | solution.py:46
  52.5 15.5 %copy-start.3 = (bf16[1024,512]{1,0:T(8,128)(2,1)S(1)}, bf16[1024,512]{1,0:T(8,128)(2,1)}, u32[]{:S(2)}) copy-start(bf16[1024,512]{1,0:T(8,128)(2,1)} %param.13) | copy-start | bytes 3145732
  54.9 17.5 %copy-start.5 = (bf16[512]{0:T(512)(128)(2,1)S(1)}, bf16[512]{0:T(512)(128)(2,1)}, u32[]{:S(2)}) copy-start(bf16[512]{0:T(512)(128)(2,1)} %param.17) | copy-start | bytes 3076
  55.0 24.4 %copy-start.4 = (bf16[16,512]{1,0:T(8,128)(2,1)S(1)}, bf16[16,512]{1,0:T(8,128)(2,1)}, u32[]{:S(2)}) copy-start(bf16[16,512]{1,0:T(8,128)(2,1)} %param.9) | copy-start | bytes 49156
  69.0 10.3 %all-to-all-start.4 = ((f32[8,16,512]{2,1,0:T(8,128)}), f32[8,16,512]{2,1,0:T(8,128)S(1)}, u32[]{:S(2)}, u32[]{:S(2)}) async-start(f32[8,16,512]{2,1,0:T(8,128)} %fusion.86), calls=%async_computation.4 | async-start | bytes 524288 | tf_op jit(solution)/shard_map/all_to_all | solution.py:46
  124.3 19.3 %copy-start.1 = (bf16[3584,512]{1,0:T(8,128)(2,1)S(1)}, bf16[3584,512]{1,0:T(8,128)(2,1)}, u32[]{:S(2)}) copy-start(bf16[3584,512]{1,0:T(8,128)(2,1)} %param.15) | copy-start | bytes 11010052
  264.0 19.3 %copy-start.2 = (bf16[3584,512]{1,0:T(8,128)(2,1)S(1)}, bf16[3584,512]{1,0:T(8,128)(2,1)}, u32[]{:S(2)}) copy-start(bf16[3584,512]{1,0:T(8,128)(2,1)} %param.15) | copy-start | bytes 11010052
  284.7 10.1 %all-to-all-start.17 = ((f32[8,16,512]{2,1,0:T(8,128)}), f32[8,16,512]{2,1,0:T(8,128)S(1)}, u32[]{:S(2)}, u32[]{:S(2)}) async-start(f32[8,16,512]{2,1,0:T(8,128)} %fusion.18), calls=%async_computation.17 | async-start | bytes 524288 | tf_op jit(solution)/shard_map/all_to_all | solution.py:46

commit v4 on v3

--- a/solution.py
+++ b/solution.py
@@ -174,10 +174,19 @@
     stream = hidden_in
     entries = []
     for layer_index in range(LAYERS):
-        rows_in = norm_rows(stream, attn_gain)
-        own_qkv = summed_on_arrival(
-            jnp.dot(rows_in, flat_qkv, preferred_element_type=jnp.float32), "wide", 0
-        )
+        if layer_index == 0:
+            rows_in = norm_rows(stream, attn_gain)
+            own_qkv = summed_on_arrival(
+                jnp.dot(rows_in, flat_qkv, preferred_element_type=jnp.float32), "wide", 0
+            )
+        else:
+            rows_in, partial_sum = gathered_rows(stream, attn_gain)
+            projected = jnp.dot(rows_in, flat_qkv, preferred_element_type=jnp.float32)
+            own = summed_on_arrival(
+                jnp.concatenate([projected, partial_sum[:, None]], axis=1), "wide", 0
+            )
+            qkv_cols = flat_qkv.shape[1]
+            own_qkv = own[:, :qkv_cols] * row_scale(own[:, qkv_cols])[:, None]
         queries, key_new, value_new = split_heads(own_qkv, lengths, heads_kv, HD)
         own_rows = key_new.shape[0]
         entries.append(

time: 297 us -> 288 us (0.970)
  blocking collectives: 197 us -> 188 us
    all_to_all x8 -> x7, blocking collectives: 97.9 us -> 86.7 us  [copy_for_each(): lax.all_to_all(jnp.broadcast_to(shard[None], (length, *shard.shape)), axi...]
where the time goes in v4:
time: 288 us; the launch traced here: 286 us
  blocking collectives  188 us (65%)
  waiting for transfers between devices  35.2 us (12%)
  starting transfers between devices  25.8 us (9%)
  matrix products  23.8 us (8%)
  other arithmetic  9.81 us (3%)
  local copies, waits for them, and re-layouts  2.96 us (1%)
    all_to_all x7, blocking collectives, copy_for_each(): lax.all_to_all(jnp.broadcast_to(shard[None], (length, *shard.shape)), axi...  86.7 us
    all_to_all x2, blocking collectives, on_device(): arrived = lax.all_to_all(payload, 'wide', 1, 1, tiled=True)  63 us
    all_to_all x3, blocking collectives, summed_on_arrival(): lax.all_to_all(parts, axis, split_axis=0, concat_axis=0, tiled=True)  38 us
    all_to_all x3, waiting for transfers between devices, summed_on_arrival(): lax.all_to_all(parts, axis, split_axis=0, concat_axis=0, tiled=True)  24.9 us
    all_to_all x2, starting transfers between devices, copy_for_each(): lax.all_to_all(jnp.broadcast_to(shard[None], (length, *shard.shape)), axi...  13.6 us
    all_to_all x3, starting transfers between devices, summed_on_arrival(): lax.all_to_all(parts, axis, split_axis=0, concat_axis=0, tiled=True)  12.3 us
    all_to_all x2, waiting for transfers between devices, copy_for_each(): lax.all_to_all(jnp.broadcast_to(shard[None], (length, *shard.shape)), axi...  10.3 us
    dot_general x2, matrix products, on_device(): jnp.einsum('rd,dkh->krh', rows_in, gate_up, preferred_element_type=jnp.fl...  8.43 us
  transfers between devices with their start and end apart: 5, of which 5 were waited for; matrix products, arithmetic and copies ran while one was open for 1% of the time, Pallas kernels for 0%

profile of v4, /device:TPU:1, one launch (start us, length us, event | category | flops | bytes accessed | tf_op | source)
XLA Modules:
  0.0 286.4 jit_solution(3496743124981372936)
XLA Ops:
  0.6 0.9 fusion.100
  2.2 8.4 %all-to-all-start = ((f32[16,1,16]{2,1,0:T(1,128)}), f32[16,1,16]{2,1,0:T(1,128)S(1)}, u32[]{:S(2)}, u32[]{:S(2)}) async-start(f32[16,1,16]{2,1,0:T(1,128)} %broadcast_in_dim.43), calls=%async_computation | async-start | bytes 16384 | tf_op jit(solution)/shard_map/all_to_all | solution.py:19
  12.1 5.4 %all-to-all-done = f32[16,1,16]{2,1,0:T(1,128)S(1)} async-done(((f32[16,1,16]{2,1,0:T(1,128)}), f32[16,1,16]{2,1,0:T(1,128)S(1)}, u32[]{:S(2)}, u32[]{:S(2)}) %all-to-all-start) | async-done | bytes 1056 | tf_op jit(solution)/shard_map/all_to_all | solution.py:19
  19.0 5.1 %all-to-all-start.1 = ((bf16[8,16,512]{2,1,0:T(8,128)(2,1)}), bf16[8,16,512]{2,1,0:T(8,128)(2,1)S(1)}, u32[]{:S(2)}, u32[]{:S(2)}) async-start(bf16[8,16,512]{2,1,0:T(8,128)(2,1)} %broadcast_in_dim.44), calls=%async_computation.1 | async-start | bytes 262144 | tf_op jit(solution)/shard_map/all_to_all | solution.py:19
  24.9 4.8 %all-to-all-done.1 = bf16[8,16,512]{2,1,0:T(8,128)(2,1)S(1)} async-done(((bf16[8,16,512]{2,1,0:T(8,128)(2,1)}), bf16[8,16,512]{2,1,0:T(8,128)(2,1)S(1)}, u32[]{:S(2)}, u32[]{:S(2)}) %all-to-all-start.1) | async-done | bytes 131104 | tf_op jit(solution)/shard_map/all_to_all | solution.py:19
  29.8 1.2 fusion.38
  31.0 5.4 %all-to-all-start.2 = ((f32[16,8,1280]{2,1,0:T(8,128)}), f32[16,8,1280]{2,1,0:T(8,128)S(1)}, u32[]{:S(2)}, u32[]{:S(2)}) async-start(f32[16,8,1280]{2,1,0:T(8,128)} %fusion.38), calls=%async_computation.2 | async-start | bytes 1310720 | tf_op jit(solution)/shard_map/all_to_all | solution.py:46
  36.7 12.0 %all-to-all-done.2 = f32[16,8,1280]{2,1,0:T(8,128)S(1)} async-done(((f32[16,8,1280]{2,1,0:T(8,128)}), f32[16,8,1280]{2,1,0:T(8,128)S(1)}, u32[]{:S(2)}, u32[]{:S(2)}) %all-to-all-start.2) | async-done | bytes 655392 | tf_op jit(solution)/shard_map/all_to_all | solution.py:46
  49.2 2.7 fusion.148
  52.5 2.4 fusion.74
  55.0 13.0 %all_to_all.86 = bf16[16,8,1024]{2,1,0:T(8,128)(2,1)S(1)} all-to-all(bf16[16,8,1024]{2,1,0:T(8,128)(2,1)S(1)} %broadcast_in_dim.47), channel_id=1, replica_groups=mesh['wide'=16,'narrow'=8] {'wide'}, dimensions={0} | all-to-all | bytes 524288 | tf_op jit(solution)/shard_map/all_to_all | solution.py:19
  68.0 1.0 fusion.86
  69.0 3.4 %all-to-all-start.4 = ((f32[8,16,512]{2,1,0:T(8,128)}), f32[8,16,512]{2,1,0:T(8,128)S(1)}, u32[]{:S(2)}, u32[]{:S(2)}) async-start(f32[8,16,512]{2,1,0:T(8,128)} %fusion.86), calls=%async_computation.4 | async-start | bytes 524288 | tf_op jit(solution)/shard_map/all_to_all | solution.py:46
  72.4 6.9 %all-to-all-done.4 = f32[8,16,512]{2,1,0:T(8,128)S(1)} async-done(((f32[8,16,512]{2,1,0:T(8,128)}), f32[8,16,512]{2,1,0:T(8,128)S(1)}, u32[]{:S(2)}, u32[]{:S(2)}) %all-to-all-start.4) | async-done | bytes 262176 | tf_op jit(solution)/shard_map/all_to_all | solution.py:46
  79.8 8.1 %all_to_all.87 = bf16[8,16,514]{2,1,0:T(8,128)(2,1)S(1)} all-to-all(bf16[8,16,514]{2,1,0:T(8,128)(2,1)S(1)} %broadcast_in_dim.48), channel_id=1, replica_groups=mesh['wide'=16,'narrow'=8] {'narrow'}, dimensions={0} | all-to-all | bytes 263168 | tf_op jit(solution)/shard_map/all_to_all | solution.py:19
  88.4 4.2 %fusion.15 = bf16[2,16,8,3584]{3,2,1,0:T(8,128)(2,1)S(1)} fusion(bf16[512,2,3584]{2,1,0:T(2,128)(2,1)} %param.14, bf16[128,514]{1,0:T(8,128)(2,1)S(1)} %bitcast.183), kind=kOutput, calls=%fused_computation.11 | convolution fusion | flops 940441600 | bytes 9306112 | tf_op jit(solution)/shard_map/rd,dkh->krh/dot_general | solution.py:209
  92.8 31.5 %all_to_all.88 = bf16[2,16,8,3585]{3,2,0,1:T(8,128)(2,1)S(1)} all-to-all(bf16[2,16,8,3585]{3,2,0,1:T(8,128)(2,1)S(1)} %pad_maximum_fusion), channel_id=1, replica_groups=mesh['wide'=16,'narrow'=8] {'wide'}, dimensions={1} | all-to-all | bytes 3671040 | tf_op jit(solution)/shard_map/all_to_all | solution.py:217
  124.9 18.8 %all_to_all.89 = bf16[16,8,3584]{2,1,0:T(8,128)(2,1)S(1)} all-to-all(bf16[16,8,3584]{2,1,0:T(8,128)(2,1)S(1)} %broadcast_in_dim.50), channel_id=1, replica_groups=mesh['wide'=16,'narrow'=8] {'wide'}, dimensions={0} | all-to-all | bytes 1835008 | tf_op jit(solution)/shard_map/all_to_all | solution.py:19
  144.3 9.2 %all_to_all.90 = f32[8,16,512]{2,1,0:T(8,128)S(1)} all-to-all(f32[8,16,512]{2,1,0:T(8,128)S(1)} %fusion.20), channel_id=1, replica_groups=mesh['wide'=16,'narrow'=8] {'narrow'}, dimensions={0} | all-to-all | bytes 524288 | tf_op jit(solution)/shard_map/all_to_all | solution.py:46
  153.9 8.3 %all_to_all.91 = bf16[8,16,514]{2,1,0:T(8,128)(2,1)S(1)} all-to-all(bf16[8,16,514]{2,1,0:T(8,128)(2,1)S(1)} %broadcast_in_dim.51), channel_id=1, replica_groups=mesh['wide'=16,'narrow'=8] {'narrow'}, dimensions={0} | all-to-all | bytes 263168 | tf_op jit(solution)/shard_map/all_to_all | solution.py:19
  162.7 19.5 %all_to_all.92 = f32[16,8,1281]{2,1,0:T(8,128)S(1)} all-to-all(f32[16,8,1281]{2,1,0:T(8,128)S(1)} %pad_maximum_fusion.2), channel_id=1, replica_groups=mesh['wide'=16,'narrow'=8] {'wide'}, dimensions={0} | all-to-all | bytes 1311744 | tf_op jit(solution)/shard_map/all_to_all | solution.py:46
  182.7 2.7 fusion.149
  186.2 2.4 fusion.79
  188.6 11.8 %all_to_all.93 = bf16[16,8,1024]{2,1,0:T(8,128)(2,1)S(1)} all-to-all(bf16[16,8,1024]{2,1,0:T(8,128)(2,1)S(1)} %broadcast_in_dim.53), channel_id=1, replica_groups=mesh['wide'=16,'narrow'=8] {'wide'}, dimensions={0} | all-to-all | bytes 524288 | tf_op jit(solution)/shard_map/all_to_all | solution.py:19
  200.6 9.4 %all_to_all.94 = f32[8,16,512]{2,1,0:T(8,128)S(1)} all-to-all(f32[8,16,512]{2,1,0:T(8,128)S(1)} %fusion.84), channel_id=1, replica_groups=mesh['wide'=16,'narrow'=8] {'narrow'}, dimensions={0} | all-to-all | bytes 524288 | tf_op jit(solution)/shard_map/all_to_all | solution.py:46
  210.5 8.1 %all_to_all.95 = bf16[8,16,514]{2,1,0:T(8,128)(2,1)S(1)} all-to-all(bf16[8,16,514]{2,1,0:T(8,128)(2,1)S(1)} %broadcast_in_dim.54), channel_id=1, replica_groups=mesh['wide'=16,'narrow'=8] {'narrow'}, dimensions={0} | all-to-all | bytes 263168 | tf_op jit(solution)/shard_map/all_to_all | solution.py:19
  218.7 4.2 %fusion.12 = bf16[2,16,8,3584]{3,2,1,0:T(8,128)(2,1)S(1)} fusion(bf16[512,2,3584]{2,1,0:T(2,128)(2,1)} %param.14, bf16[128,514]{1,0:T(8,128)(2,1)S(1)} %bitcast.185), kind=kOutput, calls=%fused_computation.10 | convolution fusion | flops 940441600 | bytes 9306112 | tf_op jit(solution)/shard_map/rd,dkh->krh/dot_general | solution.py:209
  223.5 31.5 %all_to_all.96 = bf16[2,16,8,3585]{3,2,0,1:T(8,128)(2,1)S(1)} all-to-all(bf16[2,16,8,3585]{3,2,0,1:T(8,128)(2,1)S(1)} %pad_maximum_fusion.1), channel_id=1, replica_groups=mesh['wide'=16,'narrow'=8] {'wide'}, dimensions={1} | all-to-all | bytes 3671040 | tf_op jit(solution)/shard_map/all_to_all | solution.py:217
  255.6 18.8 %all_to_all.97 = bf16[16,8,3584]{2,1,0:T(8,128)(2,1)S(1)} all-to-all(bf16[16,8,3584]{2,1,0:T(8,128)(2,1)S(1)} %broadcast_in_dim.56), channel_id=1, replica_groups=mesh['wide'=16,'narrow'=8] {'wide'}, dimensions={0} | all-to-all | bytes 1835008 | tf_op jit(solution)/shard_map/all_to_all | solution.py:19
  274.3 1.3 fusion.18
  275.7 3.4 %all-to-all-start.16 = ((f32[8,16,512]{2,1,0:T(8,128)}), f32[8,16,512]{2,1,0:T(8,128)S(1)}, u32[]{:S(2)}, u32[]{:S(2)}) async-start(f32[8,16,512]{2,1,0:T(8,128)} %fusion.18), calls=%async_computation.16 | async-start | bytes 524288 | tf_op jit(solution)/shard_map/all_to_all | solution.py:46
  279.7 6.0 %all-to-all-done.16 = f32[8,16,512]{2,1,0:T(8,128)S(1)} async-done(((f32[8,16,512]{2,1,0:T(8,128)}), f32[8,16,512]{2,1,0:T(8,128)S(1)}, u32[]{:S(2)}, u32[]{:S(2)}) %all-to-all-start.16) | async-done | bytes 262176 | tf_op jit(solution)/shard_map/all_to_all | solution.py:46
  (110 shorter events, 13.4 us)
Async XLA Ops:
  0.6 29.1 %copy-start = (bf16[512,1,1280]{2,0,1:T(8,128)(2,1)S(1)}, bf16[512,1,1280]{2,0,1:T(8,128)(2,1)}, u32[]{:S(2)}) copy-start(bf16[512,1,1280]{2,0,1:T(8,128)(2,1)} %param.12) | copy-start | bytes 3932164
  2.2 15.4 %all-to-all-start = ((f32[16,1,16]{2,1,0:T(1,128)}), f32[16,1,16]{2,1,0:T(1,128)S(1)}, u32[]{:S(2)}, u32[]{:S(2)}) async-start(f32[16,1,16]{2,1,0:T(1,128)} %broadcast_in_dim.43), calls=%async_computation | async-start | bytes 16384 | tf_op jit(solution)/shard_map/all_to_all | solution.py:19
  19.0 10.7 %all-to-all-start.1 = ((bf16[8,16,512]{2,1,0:T(8,128)(2,1)}), bf16[8,16,512]{2,1,0:T(8,128)(2,1)S(1)}, u32[]{:S(2)}, u32[]{:S(2)}) async-start(bf16[8,16,512]{2,1,0:T(8,128)(2,1)} %broadcast_in_dim.44), calls=%async_computation.1 | async-start | bytes 262144 | tf_op jit(solution)/shard_map/all_to_all | solution.py:19
  31.0 17.8 %all-to-all-start.2 = ((f32[16,8,1280]{2,1,0:T(8,128)}), f32[16,8,1280]{2,1,0:T(8,128)S(1)}, u32[]{:S(2)}, u32[]{:S(2)}) async-start(f32[16,8,1280]{2,1,0:T(8,128)} %fusion.38), calls=%async_computation.2 | async-start | bytes 1310720 | tf_op jit(solution)/shard_map/all_to_all | solution.py:46
  52.5 15.5 %copy-start.3 = (bf16[1024,512]{1,0:T(8,128)(2,1)S(1)}, bf16[1024,512]{1,0:T(8,128)(2,1)}, u32[]{:S(2)}) copy-start(bf16[1024,512]{1,0:T(8,128)(2,1)} %param.13) | copy-start | bytes 3145732
  54.9 17.5 %copy-start.5 = (bf16[512]{0:T(512)(128)(2,1)S(1)}, bf16[512]{0:T(512)(128)(2,1)}, u32[]{:S(2)}) copy-start(bf16[512]{0:T(512)(128)(2,1)} %param.17) | copy-start | bytes 3076
  55.0 24.4 %copy-start.4 = (bf16[16,512]{1,0:T(8,128)(2,1)S(1)}, bf16[16,512]{1,0:T(8,128)(2,1)}, u32[]{:S(2)}) copy-start(bf16[16,512]{1,0:T(8,128)(2,1)} %param.9) | copy-start | bytes 49156
  69.0 10.3 %all-to-all-start.4 = ((f32[8,16,512]{2,1,0:T(8,128)}), f32[8,16,512]{2,1,0:T(8,128)S(1)}, u32[]{:S(2)}, u32[]{:S(2)}) async-start(f32[8,16,512]{2,1,0:T(8,128)} %fusion.86), calls=%async_computation.4 | async-start | bytes 524288 | tf_op jit(solution)/shard_map/all_to_all | solution.py:46
  124.3 19.3 %copy-start.1 = (bf16[3584,512]{1,0:T(8,128)(2,1)S(1)}, bf16[3584,512]{1,0:T(8,128)(2,1)}, u32[]{:S(2)}) copy-start(bf16[3584,512]{1,0:T(8,128)(2,1)} %param.15) | copy-start | bytes 11010052
  255.0 19.3 %copy-start.2 = (bf16[3584,512]{1,0:T(8,128)(2,1)S(1)}, bf16[3584,512]{1,0:T(8,128)(2,1)}, u32[]{:S(2)}) copy-start(bf16[3584,512]{1,0:T(8,128)(2,1)} %param.15) | copy-start | bytes 11010052
  275.7 10.1 %all-to-all-start.16 = ((f32[8,16,512]{2,1,0:T(8,128)}), f32[8,16,512]{2,1,0:T(8,128)S(1)}, u32[]{:S(2)}, u32[]{:S(2)}) async-start(f32[8,16,512]{2,1,0:T(8,128)} %fusion.18), calls=%async_computation.16 | async-start | bytes 524288 | tf_op jit(solution)/shard_map/all_to_all | solution.py:46

commit v5 on v4

--- a/solution.py
+++ b/solution.py
@@ -3,19 +3,62 @@
 import jax
 import jax.numpy as jnp
 from jax import lax
+from jax.sharding import Mesh
 from jax.sharding import PartitionSpec as P
 
 D = 8192
 HD = 128
 LAYERS = 2
+CHIPS = "chips"
+CORES = "cores"
+WIDE = (CHIPS, CORES)
 
 
 EPSILON = 1e-05
 ROPE_BASE = 500000.0
 
 
+def axis_length(axis):
+    if isinstance(axis, tuple):
+        return math.prod(lax.axis_size(name) for name in axis)
+    return lax.axis_size(axis)
+
+
+def swap_cores(shard):
+    return lax.ppermute(shard, CORES, [(0, 1), (1, 0)])
+
+
+def reduced_rows(partial, row_dim, wire_type):
+    chips = lax.axis_size(CHIPS)
+    shape = partial.shape
+    split = shape[:row_dim] + (chips, 2, shape[row_dim] // (chips * 2)) + shape[row_dim + 1 :]
+    blocks = partial.reshape(split)
+    core = lax.axis_index(CORES)
+    mine = lax.dynamic_index_in_dim(blocks, core, row_dim + 1, keepdims=False)
+    other = lax.dynamic_index_in_dim(blocks, 1 - core, row_dim + 1, keepdims=False)
+    pair_sum = mine.astype(jnp.float32) + swap_cores(other).astype(jnp.float32)
+    return pair_sum, row_dim
+
+
+def chip_sum(pair_sum, row_dim, wire_type):
+    arrived = lax.all_to_all(pair_sum.astype(wire_type), CHIPS, row_dim, row_dim, tiled=True)
+    return jnp.sum(arrived.astype(jnp.float32), axis=row_dim)
+
+
+def gathered_rows_wide(shard):
+    chips = lax.axis_size(CHIPS)
+    from_chips = lax.all_to_all(
+        jnp.broadcast_to(shard[None], (chips, *shard.shape)), CHIPS, 0, 0, tiled=True
+    )
+    from_partner = swap_cores(from_chips)
+    first = lax.axis_index(CORES) == 0
+    low_core = jnp.where(first, from_chips, from_partner)
+    high_core = jnp.where(first, from_partner, from_chips)
+    return jnp.stack([low_core, high_core], axis=1).reshape(-1, *shard.shape[1:])
+
+
 def copy_for_each(shard, axis):
-    length = lax.axis_size(axis)
+    length = axis_length(axis)
     return lax.all_to_all(
         jnp.broadcast_to(shard[None], (length, *shard.shape)), axis, 0, 0, tiled=True
     )
@@ -42,13 +85,13 @@
 
 
 def summed_on_arrival(shard, axis, dim):
-    parts = in_blocks(shard, dim, lax.axis_size(axis))
+    parts = in_blocks(shard, dim, axis_length(axis))
     arrived = lax.all_to_all(parts, axis, split_axis=0, concat_axis=0, tiled=True)
     return arrived.sum(axis=0)
 
 
 def sent_and_summed(shard, axis, dim):
-    length = lax.axis_size(axis)
+    length = axis_length(axis)
     parts = lax.all_to_all(in_blocks(shard, dim, length), axis, 0, 0, tiled=True)
     return jnp.sum(parts.astype(jnp.float32), axis=0)
 
@@ -62,7 +105,7 @@
 
 def norm_rows(stream, gain):
     floats = stream.astype(jnp.float32)
-    square_sum = of_everyone(jnp.sum(floats * floats, axis=1), "wide")
+    square_sum = of_everyone(jnp.sum(floats * floats, axis=1), WIDE)
     return gathered_copies(scale_rows(floats, square_sum, gain), "narrow", 0)
 
 
@@ -176,15 +219,17 @@
     for layer_index in range(LAYERS):
         if layer_index == 0:
             rows_in = norm_rows(stream, attn_gain)
-            own_qkv = summed_on_arrival(
-                jnp.dot(rows_in, flat_qkv, preferred_element_type=jnp.float32), "wide", 0
+            pair_sum, row_dim = reduced_rows(
+                jnp.dot(rows_in, flat_qkv, preferred_element_type=jnp.float32), 0, jnp.float32
             )
+            own_qkv = chip_sum(pair_sum, row_dim, jnp.float32)
         else:
             rows_in, partial_sum = gathered_rows(stream, attn_gain)
             projected = jnp.dot(rows_in, flat_qkv, preferred_element_type=jnp.float32)
-            own = summed_on_arrival(
-                jnp.concatenate([projected, partial_sum[:, None]], axis=1), "wide", 0
+            pair_sum, row_dim = reduced_rows(
+                jnp.concatenate([projected, partial_sum[:, None]], axis=1), 0, jnp.float32
             )
+            own = chip_sum(pair_sum, row_dim, jnp.float32)
             qkv_cols = flat_qkv.shape[1]
             own_qkv = own[:, :qkv_cols] * row_scale(own[:, qkv_cols])[:, None]
         queries, key_new, value_new = split_heads(own_qkv, lengths, heads_kv, HD)
@@ -200,7 +245,7 @@
         attended = attend(
             queries, key_new, value_new, kv_cache[layer_index, 0], kv_cache[layer_index, 1], lengths
         )
-        heads_all = gathered_copies(attended, "wide", 0)
+        heads_all = gathered_rows_wide(attended)
         summed = summed_on_arrival(
             jnp.dot(heads_all, o_weight, preferred_element_type=jnp.float32), "narrow", 0
         )
@@ -212,16 +257,18 @@
         high, low = split_hi_lo(partial_sum)
         sums_col = jnp.stack([high, low])[:, :, None]
         payload = jnp.concatenate([both_parts, sums_col], axis=2)
-        wide_size = lax.axis_size("wide")
-        payload = payload.reshape(2, wide_size, -1, hidden_dev + 1)
-        arrived = lax.all_to_all(payload, "wide", 1, 1, tiled=True)
-        own = jnp.sum(arrived.astype(jnp.float32), axis=1)
+        pair_sum, row_dim = reduced_rows(payload, 1, jnp.bfloat16)
+        pair_squares = pair_sum[0, :, :, hidden_dev] + pair_sum[1, :, :, hidden_dev]
+        high, low = split_hi_lo(pair_squares)
+        pair_sum = pair_sum.astype(jnp.bfloat16)
+        pair_sum = pair_sum.at[0, :, :, hidden_dev].set(high).at[1, :, :, hidden_dev].set(low)
+        own = chip_sum(pair_sum, row_dim, jnp.bfloat16)
         scale = row_scale(own[0, :, hidden_dev] + own[1, :, hidden_dev])[:, None]
         gate = own[0, :, :hidden_dev] * scale
         up = own[1, :, :hidden_dev] * scale
         activated = (jax.nn.silu(gate) * up).astype(jnp.bfloat16)
         partial_down = jnp.dot(
-            gathered_copies(activated, "wide", 0), down_weight, preferred_element_type=jnp.float32
+            gathered_rows_wide(activated), down_weight, preferred_element_type=jnp.float32
         )
         summed = summed_on_arrival(partial_down, "narrow", 0)
         stream = (stream.astype(jnp.float32) + summed).astype(jnp.bfloat16)
@@ -229,20 +276,24 @@
 
 
 def solution(mesh):
+    wide_size, narrow_size = mesh.devices.shape
+    split_mesh = Mesh(
+        mesh.devices.reshape(wide_size // 2, 2, narrow_size), (CHIPS, CORES, "narrow")
+    )
     return jax.shard_map(
         on_device,
-        mesh=mesh,
+        mesh=split_mesh,
         in_specs=(
-            P("narrow", "wide"),
-            P("wide"),
-            P(None, None, "wide", "narrow"),
-            P("wide", "narrow", None),
-            P("narrow", "wide"),
-            P("wide", None, "narrow"),
-            P("narrow", "wide"),
-            P("wide"),
-            P("wide"),
+            P("narrow", WIDE),
+            P(WIDE),
+            P(None, None, WIDE, "narrow"),
+            P(WIDE, "narrow", None),
+            P("narrow", WIDE),
+            P(WIDE, None, "narrow"),
+            P("narrow", WIDE),
+            P(WIDE),
+            P(WIDE),
         ),
-        out_specs=(P("narrow", "wide"), P(None, None, "wide", "narrow")),
+        out_specs=(P("narrow", WIDE), P(None, None, WIDE, "narrow")),
         check_vma=False,
     )

time: 288 us -> 275 us (0.955)
  blocking collectives: 188 us -> 135 us
  starting transfers between devices: 25.8 us -> 44 us
  other arithmetic: 9.81 us -> 21.3 us
  waiting for transfers between devices: 35.2 us -> 41.7 us
  local copies, waits for them, and re-layouts: 2.96 us -> 7.55 us
    all_to_all x7 -> x3, blocking collectives: 86.7 us -> 24.6 us  [copy_for_each(): lax.all_to_all(jnp.broadcast_to(shard[None], (length, *shard.shape)), axi...]
    all_to_all x2 -> x7, blocking collectives: 63 us -> 91.5 us  [the longest x3 48 us: chip_sum(): lax.all_to_all(pair_sum.astype(wire_type), CHIPS, row_dim, row_dim, tiled...]
    ppermute x0 -> x8, starting transfers between devices: none -> 20.2 us  [swap_cores(): return lax.ppermute(shard, CORES, [(0, 1), (1, 0)])]
    all_to_all x3 -> x2, blocking collectives: 38 us -> 18.4 us  [summed_on_arrival(): lax.all_to_all(parts, axis, split_axis=0, concat_axis=0, tiled=True)]
    all_to_all x3 -> x2, waiting for transfers between devices: 24.9 us -> 13.2 us  [summed_on_arrival(): lax.all_to_all(parts, axis, split_axis=0, concat_axis=0, tiled=True)]
    ppermute x0 -> x8, waiting for transfers between devices: none -> 9.43 us  [swap_cores(): return lax.ppermute(shard, CORES, [(0, 1), (1, 0)])]
    all_to_all x0 -> x1, waiting for transfers between devices: none -> 8.74 us  [chip_sum(): lax.all_to_all(pair_sum.astype(wire_type), CHIPS, row_dim, row_dim, tiled...]
    another operation x3 -> x11, other arithmetic: 0.99 us -> 7.79 us
  transfers between devices with their start and end apart: 5 -> 13, of which waited for: 5 -> 12; matrix products, arithmetic and copies ran while one was open for 1% -> 2% of each run, Pallas kernels for 0% -> 0%
where the time goes in v5:
time: 275 us; the launch traced here: 273 us
  blocking collectives  135 us (49%)
  starting transfers between devices  44 us (16%)
  waiting for transfers between devices  41.7 us (15%)
  matrix products  23 us (8%)
  other arithmetic  21.3 us (8%)
  local copies, waits for them, and re-layouts  7.55 us (3%)
    all_to_all x3, blocking collectives, chip_sum(): lax.all_to_all(pair_sum.astype(wire_type), CHIPS, row_dim, row_dim, tiled...  48 us
    all_to_all x4, blocking collectives, gathered_rows_wide(): lax.all_to_all(jnp.broadcast_to(shard[None], (chips, *shard.shape)), CHIP...  43.6 us
    all_to_all x3, blocking collectives, copy_for_each(): lax.all_to_all(jnp.broadcast_to(shard[None], (length, *shard.shape)), axi...  24.6 us
    ppermute x8, starting transfers between devices, swap_cores(): return lax.ppermute(shard, CORES, [(0, 1), (1, 0)])  20.2 us
    all_to_all x2, blocking collectives, summed_on_arrival(): lax.all_to_all(parts, axis, split_axis=0, concat_axis=0, tiled=True)  18.4 us
    all_to_all x2, starting transfers between devices, copy_for_each(): lax.all_to_all(jnp.broadcast_to(shard[None], (length, *shard.shape)), axi...  13.6 us
    all_to_all x2, waiting for transfers between devices, summed_on_arrival(): lax.all_to_all(parts, axis, split_axis=0, concat_axis=0, tiled=True)  13.2 us
    all_to_all x2, waiting for transfers between devices, copy_for_each(): lax.all_to_all(jnp.broadcast_to(shard[None], (length, *shard.shape)), axi...  10.3 us
  transfers between devices with their start and end apart: 13, of which 12 were waited for; matrix products, arithmetic and copies ran while one was open for 2% of the time, Pallas kernels for 0%

profile of v5, /device:TPU:1, one launch (start us, length us, event | category | flops | bytes accessed | tf_op | source)
XLA Modules:
  0.0 273.2 jit_solution(11121338816553449535)
XLA Ops:
  2.2 8.4 %all-to-all-start = ((f32[16,1,16]{2,1,0:T(1,128)}), f32[16,1,16]{2,1,0:T(1,128)S(1)}, u32[]{:S(2)}, u32[]{:S(2)}) async-start(f32[16,1,16]{2,1,0:T(1,128)} %broadcast_in_dim.43), calls=%async_computation | async-start | bytes 16384 | tf_op jit(solution)/shard_map/all_to_all | solution.py:62
  12.1 5.4 %all-to-all-done = f32[16,1,16]{2,1,0:T(1,128)S(1)} async-done(((f32[16,1,16]{2,1,0:T(1,128)}), f32[16,1,16]{2,1,0:T(1,128)S(1)}, u32[]{:S(2)}, u32[]{:S(2)}) %all-to-all-start) | async-done | bytes 1056 | tf_op jit(solution)/shard_map/all_to_all | solution.py:62
  19.0 5.1 %all-to-all-start.1 = ((bf16[8,16,512]{2,1,0:T(8,128)(2,1)}), bf16[8,16,512]{2,1,0:T(8,128)(2,1)S(1)}, u32[]{:S(2)}, u32[]{:S(2)}) async-start(bf16[8,16,512]{2,1,0:T(8,128)(2,1)} %broadcast_in_dim.44), calls=%async_computation.1 | async-start | bytes 262144 | tf_op jit(solution)/shard_map/all_to_all | solution.py:62
  24.9 4.8 %all-to-all-done.1 = bf16[8,16,512]{2,1,0:T(8,128)(2,1)S(1)} async-done(((bf16[8,16,512]{2,1,0:T(8,128)(2,1)}), bf16[8,16,512]{2,1,0:T(8,128)(2,1)S(1)}, u32[]{:S(2)}, u32[]{:S(2)}) %all-to-all-start.1) | async-done | bytes 131104 | tf_op jit(solution)/shard_map/all_to_all | solution.py:62
  34.3 3.4 %all-to-all-start.2 = ((f32[8,8,1280]{2,1,0:T(8,128)}), f32[8,8,1280]{2,1,0:T(8,128)S(1)}, u32[]{:S(2)}, u32[]{:S(2)}) async-start(f32[8,8,1280]{2,1,0:T(8,128)} %bitcast_add_fusion), calls=%async_computation.2 | async-start | bytes 655360 | tf_op jit(solution)/shard_map/all_to_all | solution.py:44
  37.9 8.7 %all-to-all-done.2 = f32[8,8,1280]{2,1,0:T(8,128)S(1)} async-done(((f32[8,8,1280]{2,1,0:T(8,128)}), f32[8,8,1280]{2,1,0:T(8,128)S(1)}, u32[]{:S(2)}, u32[]{:S(2)}) %all-to-all-start.2) | async-done | bytes 327712 | tf_op jit(solution)/shard_map/all_to_all | solution.py:44
  47.1 2.7 %fusion.175 = (f32[8,8]{1,0:T(8,128)S(1)}, f32[8,8,9536]{2,1,0:T(8,128)S(1)}) fusion(bf16[8,8,128]{2,1,0:T(8,128)(2,1)S(1)} %fusion.135, bf16[2,2,9536,128]{3,2,1,0:T(8,128)(2,1)} %param.19, pred[8,9536]{1,0:T(8,128)(4,1)S(1)} %fusion.99), kind=kOutput, calls=%fused_computation.252 | convolution fusion | flops 158068672 | bytes 4975360 | tf_op jit(solution)/shard_map/rkgd,tkd->krgt/dot_general | solution.py:160
  52.9 9.3 %all_to_all.86 = bf16[8,8,1024]{2,1,0:T(8,128)(2,1)S(1)} all-to-all(bf16[8,8,1024]{2,1,0:T(8,128)(2,1)S(1)} %broadcast_in_dim.47), channel_id=1, replica_groups=mesh['chips'=8,'cores'=2,'narrow'=8] {'chips'}, dimensions={0} | all-to-all | bytes 262144 | tf_op jit(solution)/shard_map/all_to_all | solution.py:50
  62.2 2.6 collective-permute-start.1
  66.9 3.4 %all-to-all-start.4 = ((f32[8,16,512]{2,1,0:T(8,128)}), f32[8,16,512]{2,1,0:T(8,128)S(1)}, u32[]{:S(2)}, u32[]{:S(2)}) async-start(f32[8,16,512]{2,1,0:T(8,128)} %fusion.80), calls=%async_computation.4 | async-start | bytes 524288 | tf_op jit(solution)/shard_map/all_to_all | solution.py:89
  70.3 6.9 %all-to-all-done.4 = f32[8,16,512]{2,1,0:T(8,128)S(1)} async-done(((f32[8,16,512]{2,1,0:T(8,128)}), f32[8,16,512]{2,1,0:T(8,128)S(1)}, u32[]{:S(2)}, u32[]{:S(2)}) %all-to-all-start.4) | async-done | bytes 262176 | tf_op jit(solution)/shard_map/all_to_all | solution.py:89
  77.7 8.1 %all_to_all.87 = bf16[8,16,514]{2,1,0:T(8,128)(2,1)S(1)} all-to-all(bf16[8,16,514]{2,1,0:T(8,128)(2,1)S(1)} %broadcast_in_dim.48), channel_id=1, replica_groups=mesh['chips'=8,'cores'=2,'narrow'=8] {'narrow'}, dimensions={0} | all-to-all | bytes 263168 | tf_op jit(solution)/shard_map/all_to_all | solution.py:62
  86.4 4.2 %fusion.6 = bf16[128,2,3584]{2,0,1:T(8,128)(2,1)S(1)} fusion(bf16[512,2,3584]{2,1,0:T(2,128)(2,1)} %param.22, bf16[128,514]{1,0:T(8,128)(2,1)S(1)} %bitcast.235), kind=kOutput, calls=%fused_computation.8 | convolution fusion | flops 940441600 | bytes 9306112 | tf_op jit(solution)/shard_map/rd,dkh->krh/dot_general | solution.py:254
  100.2 17.7 %all_to_all.88 = bf16[2,8,8,3585]{3,2,0,1:T(8,128)(2,1)S(1)} all-to-all(bf16[2,8,8,3585]{3,2,0,1:T(8,128)(2,1)S(1)} %fusion.133), channel_id=1, replica_groups=mesh['chips'=8,'cores'=2,'narrow'=8] {'chips'}, dimensions={1} | all-to-all | bytes 1835520 | tf_op jit(solution)/shard_map/all_to_all | solution.py:44
  118.3 12.4 %all_to_all.89 = bf16[8,8,3584]{2,1,0:T(8,128)(2,1)S(1)} all-to-all(bf16[8,8,3584]{2,1,0:T(8,128)(2,1)S(1)} %broadcast_in_dim.50), channel_id=1, replica_groups=mesh['chips'=8,'cores'=2,'narrow'=8] {'chips'}, dimensions={0} | all-to-all | bytes 917504 | tf_op jit(solution)/shard_map/all_to_all | solution.py:50
  135.2 9.0 %all_to_all.90 = f32[8,16,512]{2,1,0:T(8,128)S(1)} all-to-all(f32[8,16,512]{2,1,0:T(8,128)S(1)} %fusion.14), channel_id=1, replica_groups=mesh['chips'=8,'cores'=2,'narrow'=8] {'narrow'}, dimensions={0} | all-to-all | bytes 524288 | tf_op jit(solution)/shard_map/all_to_all | solution.py:89
  144.7 8.5 %all_to_all.91 = bf16[8,16,514]{2,1,0:T(8,128)(2,1)S(1)} all-to-all(bf16[8,16,514]{2,1,0:T(8,128)(2,1)S(1)} %broadcast_in_dim.51), channel_id=1, replica_groups=mesh['chips'=8,'cores'=2,'narrow'=8] {'narrow'}, dimensions={0} | all-to-all | bytes 263168 | tf_op jit(solution)/shard_map/all_to_all | solution.py:62
  153.6 2.6 collective-permute-start.4
  157.6 11.6 %all_to_all.92 = f32[8,8,1281]{2,1,0:T(8,128)S(1)} all-to-all(f32[8,8,1281]{2,1,0:T(8,128)S(1)} %fusion.98), channel_id=1, replica_groups=mesh['chips'=8,'cores'=2,'narrow'=8] {'chips'}, dimensions={0} | all-to-all | bytes 655872 | tf_op jit(solution)/shard_map/all_to_all | solution.py:44
  169.7 2.7 %fusion.176 = (f32[8,8]{1,0:T(8,128)S(1)}, f32[8,8,9536]{2,1,0:T(8,128)S(1)}) fusion(bf16[8,8,128]{2,1,0:T(8,128)(2,1)S(1)} %fusion.136, bf16[2,2,9536,128]{3,2,1,0:T(8,128)(2,1)} %param.19, pred[8,9536]{1,0:T(8,128)(4,1)S(1)} %fusion.99), kind=kOutput, calls=%fused_computation.253 | convolution fusion | flops 158068672 | bytes 4975360 | tf_op jit(solution)/shard_map/rkgd,tkd->krgt/dot_general | solution.py:160
  175.6 9.8 %all_to_all.93 = bf16[8,8,1024]{2,1,0:T(8,128)(2,1)S(1)} all-to-all(bf16[8,8,1024]{2,1,0:T(8,128)(2,1)S(1)} %broadcast_in_dim.53), channel_id=1, replica_groups=mesh['chips'=8,'cores'=2,'narrow'=8] {'chips'}, dimensions={0} | all-to-all | bytes 262144 | tf_op jit(solution)/shard_map/all_to_all | solution.py:50
  185.3 2.8 %collective-permute-start.5 = (bf16[8,8,1024]{2,1,0:T(8,128)(2,1)S(1)}, bf16[8,8,1024]{2,1,0:T(8,128)(2,1)S(1)}, u32[]{:S(2)}, u32[]{:S(2)}) collective-permute-start(bf16[8,8,1024]{2,1,0:T(8,128)(2,1)S(1)} %all_to_all.93), channel_id=1, source_target_pairs={{0,8},{8,0},{1,9},{9,1},{2,10},{10,2},{3,11},{11,3},{4,12},{12,4},... | collective-permute-start | bytes 393224 | tf_op jit(solution)/shard_map/ppermute | solution.py:28
  189.5 9.4 %all_to_all.94 = f32[8,16,512]{2,1,0:T(8,128)S(1)} all-to-all(f32[8,16,512]{2,1,0:T(8,128)S(1)} %fusion.78), channel_id=1, replica_groups=mesh['chips'=8,'cores'=2,'narrow'=8] {'narrow'}, dimensions={0} | all-to-all | bytes 524288 | tf_op jit(solution)/shard_map/all_to_all | solution.py:89
  199.4 8.1 %all_to_all.95 = bf16[8,16,514]{2,1,0:T(8,128)(2,1)S(1)} all-to-all(bf16[8,16,514]{2,1,0:T(8,128)(2,1)S(1)} %broadcast_in_dim.54), channel_id=1, replica_groups=mesh['chips'=8,'cores'=2,'narrow'=8] {'narrow'}, dimensions={0} | all-to-all | bytes 263168 | tf_op jit(solution)/shard_map/all_to_all | solution.py:62
  207.6 4.2 %fusion.9 = bf16[128,2,3584]{2,0,1:T(8,128)(2,1)S(1)} fusion(bf16[512,2,3584]{2,1,0:T(2,128)(2,1)} %param.22, bf16[128,514]{1,0:T(8,128)(2,1)S(1)} %bitcast.237), kind=kOutput, calls=%fused_computation.9 | convolution fusion | flops 940441600 | bytes 9306112 | tf_op jit(solution)/shard_map/rd,dkh->krh/dot_general | solution.py:254
  212.3 2.6 collective-permute-start.6
  218.9 2.7 dynamic-slice_select_fusion
  221.6 2.6 scatter.16
  225.6 18.7 %all_to_all.96 = bf16[2,8,8,3585]{3,2,0,1:T(8,128)(2,1)S(1)} all-to-all(bf16[2,8,8,3585]{3,2,0,1:T(8,128)(2,1)} %fusion.134), channel_id=1, replica_groups=mesh['chips'=8,'cores'=2,'narrow'=8] {'chips'}, dimensions={1} | all-to-all | bytes 1835520 | tf_op jit(solution)/shard_map/all_to_all | solution.py:44
  244.8 12.2 %all_to_all.97 = bf16[8,8,3584]{2,1,0:T(8,128)(2,1)S(1)} all-to-all(bf16[8,8,3584]{2,1,0:T(8,128)(2,1)S(1)} %broadcast_in_dim.56), channel_id=1, replica_groups=mesh['chips'=8,'cores'=2,'narrow'=8] {'chips'}, dimensions={0} | all-to-all | bytes 917504 | tf_op jit(solution)/shard_map/all_to_all | solution.py:50
  262.2 3.4 %all-to-all-start.16 = ((f32[8,16,512]{2,1,0:T(8,128)}), f32[8,16,512]{2,1,0:T(8,128)S(1)}, u32[]{:S(2)}, u32[]{:S(2)}) async-start(f32[8,16,512]{2,1,0:T(8,128)} %fusion.12), calls=%async_computation.16 | async-start | bytes 524288 | tf_op jit(solution)/shard_map/all_to_all | solution.py:89
  266.3 6.3 %all-to-all-done.16 = f32[8,16,512]{2,1,0:T(8,128)S(1)} async-done(((f32[8,16,512]{2,1,0:T(8,128)}), f32[8,16,512]{2,1,0:T(8,128)S(1)}, u32[]{:S(2)}, u32[]{:S(2)}) %all-to-all-start.16) | async-done | bytes 262176 | tf_op jit(solution)/shard_map/all_to_all | solution.py:89
  (149 shorter events, 51.5 us)
Async XLA Ops:
  0.6 29.1 %copy-start = (bf16[512,1,1280]{2,0,1:T(8,128)(2,1)S(1)}, bf16[512,1,1280]{2,0,1:T(8,128)(2,1)}, u32[]{:S(2)}) copy-start(bf16[512,1,1280]{2,0,1:T(8,128)(2,1)} %param.20) | copy-start | bytes 3932164
  2.2 15.4 %all-to-all-start = ((f32[16,1,16]{2,1,0:T(1,128)}), f32[16,1,16]{2,1,0:T(1,128)S(1)}, u32[]{:S(2)}, u32[]{:S(2)}) async-start(f32[16,1,16]{2,1,0:T(1,128)} %broadcast_in_dim.43), calls=%async_computation | async-start | bytes 16384 | tf_op jit(solution)/shard_map/all_to_all | solution.py:62
  19.0 10.7 %all-to-all-start.1 = ((bf16[8,16,512]{2,1,0:T(8,128)(2,1)}), bf16[8,16,512]{2,1,0:T(8,128)(2,1)S(1)}, u32[]{:S(2)}, u32[]{:S(2)}) async-start(bf16[8,16,512]{2,1,0:T(8,128)(2,1)} %broadcast_in_dim.44), calls=%async_computation.1 | async-start | bytes 262144 | tf_op jit(solution)/shard_map/all_to_all | solution.py:62
  30.2 3.4 %collective-permute-start = (f32[8,8,1280]{2,1,0:T(8,128)S(1)}, f32[8,8,1280]{2,1,0:T(8,128)S(1)}, u32[]{:S(2)}, u32[]{:S(2)}) collective-permute-start(f32[8,8,1280]{2,1,0:T(8,128)S(1)} %dynamic-slice_bitcast_fusion), channel_id=1, source_target_pairs={{0,8},{8,0},{1,9},{9,1},{2,10},{10,2},{3,11},{11,3},{4,12},{12,4},... | collective-permute-start | bytes 983048 | tf_op jit(solution)/shard_map/ppermute | solution.py:28
  34.3 12.3 %all-to-all-start.2 = ((f32[8,8,1280]{2,1,0:T(8,128)}), f32[8,8,1280]{2,1,0:T(8,128)S(1)}, u32[]{:S(2)}, u32[]{:S(2)}) async-start(f32[8,8,1280]{2,1,0:T(8,128)} %bitcast_add_fusion), calls=%async_computation.2 | async-start | bytes 655360 | tf_op jit(solution)/shard_map/all_to_all | solution.py:44
  50.4 15.4 %copy-start.1 = (bf16[1024,512]{1,0:T(8,128)(2,1)S(1)}, bf16[1024,512]{1,0:T(8,128)(2,1)}, u32[]{:S(2)}) copy-start(bf16[1024,512]{1,0:T(8,128)(2,1)} %param.21) | copy-start | bytes 3145732
  52.9 17.4 %copy-start.4 = (bf16[512]{0:T(512)(128)(2,1)S(1)}, bf16[512]{0:T(512)(128)(2,1)}, u32[]{:S(2)}) copy-start(bf16[512]{0:T(512)(128)(2,1)} %param.25) | copy-start | bytes 3076
  52.9 24.4 %copy-start.3 = (bf16[16,512]{1,0:T(8,128)(2,1)S(1)}, bf16[16,512]{1,0:T(8,128)(2,1)}, u32[]{:S(2)}) copy-start(bf16[16,512]{1,0:T(8,128)(2,1)} %param.17) | copy-start | bytes 49156
  62.2 3.6 %collective-permute-start.1 = (bf16[8,8,1024]{2,1,0:T(8,128)(2,1)S(1)}, bf16[8,8,1024]{2,1,0:T(8,128)(2,1)S(1)}, u32[]{:S(2)}, u32[]{:S(2)}) collective-permute-start(bf16[8,8,1024]{2,1,0:T(8,128)(2,1)S(1)} %all_to_all.86), channel_id=1, source_target_pairs={{0,8},{8,0},{1,9},{9,1},{2,10},{10,2},{3,11},{11,3},{4,12},{12,4},... | collective-permute-start | bytes 393224 | tf_op jit(solution)/shard_map/ppermute | solution.py:28
  66.9 10.4 %all-to-all-start.4 = ((f32[8,16,512]{2,1,0:T(8,128)}), f32[8,16,512]{2,1,0:T(8,128)S(1)}, u32[]{:S(2)}, u32[]{:S(2)}) async-start(f32[8,16,512]{2,1,0:T(8,128)} %fusion.80), calls=%async_computation.4 | async-start | bytes 524288 | tf_op jit(solution)/shard_map/all_to_all | solution.py:89
  90.6 3.2 %copy-start.5 = (s32[4]{0:T(128)S(1)}, s32[4]{0:T(128)}, u32[]{:S(2)}) copy-start(s32[4]{0:T(128)} %constant.159.clone.1) | copy-start | bytes 52
  90.7 5.1 %collective-permute-start.2 = (bf16[2,8,8,3585]{3,2,0,1:T(8,128)(2,1)S(1)}, bf16[2,8,8,3585]{3,2,0,1:T(8,128)(2,1)S(1)}, u32[]{:S(2)}, u32[]{:S(2)}) collective-permute-start(bf16[2,8,8,3585]{3,2,0,1:T(8,128)(2,1)S(1)} %fusion.87), channel_id=1, source_target_pairs={{0,8},{8,0},{1,9},{9,1},{2,10},{10,2},{3,11},{11,3},{4,12},{12,4},... | collective-permute-start | bytes 2753288 | tf_op jit(solution)/shard_map/ppermute | solution.py:28
  96.1 2.0 copy-start.2
  117.8 16.7 %copy-start.6 = (bf16[3584,512]{1,0:T(8,128)(2,1)S(1)}, bf16[3584,512]{1,0:T(8,128)(2,1)}, u32[]{:S(2)}) copy-start(bf16[3584,512]{1,0:T(8,128)(2,1)} %param.23) | copy-start | bytes 11010052
  130.7 3.8 %collective-permute-start.3 = (bf16[8,8,3584]{2,1,0:T(8,128)(2,1)S(1)}, bf16[8,8,3584]{2,1,0:T(8,128)(2,1)S(1)}, u32[]{:S(2)}, u32[]{:S(2)}) collective-permute-start(bf16[8,8,3584]{2,1,0:T(8,128)(2,1)S(1)} %all_to_all.89), channel_id=1, source_target_pairs={{0,8},{8,0},{1,9},{9,1},{2,10},{10,2},{3,11},{11,3},{4,12},{12,4},... | collective-permute-start | bytes 1376264 | tf_op jit(solution)/shard_map/ppermute | solution.py:28
  153.6 3.9 %collective-permute-start.4 = (f32[8,8,1281]{2,1,0:T(8,128)S(1)}, f32[8,8,1281]{2,1,0:T(8,128)S(1)}, u32[]{:S(2)}, u32[]{:S(2)}) collective-permute-start(f32[8,8,1281]{2,1,0:T(8,128)S(1)} %fusion.95), channel_id=1, source_target_pairs={{0,8},{8,0},{1,9},{9,1},{2,10},{10,2},{3,11},{11,3},{4,12},{12,4},... | collective-permute-start | bytes 983816 | tf_op jit(solution)/shard_map/ppermute | solution.py:28
  185.3 3.8 %collective-permute-start.5 = (bf16[8,8,1024]{2,1,0:T(8,128)(2,1)S(1)}, bf16[8,8,1024]{2,1,0:T(8,128)(2,1)S(1)}, u32[]{:S(2)}, u32[]{:S(2)}) collective-permute-start(bf16[8,8,1024]{2,1,0:T(8,128)(2,1)S(1)} %all_to_all.93), channel_id=1, source_target_pairs={{0,8},{8,0},{1,9},{9,1},{2,10},{10,2},{3,11},{11,3},{4,12},{12,4},... | collective-permute-start | bytes 393224 | tf_op jit(solution)/shard_map/ppermute | solution.py:28
  212.3 4.7 %collective-permute-start.6 = (bf16[2,8,8,3585]{3,2,0,1:T(8,128)(2,1)S(1)}, bf16[2,8,8,3585]{3,2,0,1:T(8,128)(2,1)S(1)}, u32[]{:S(2)}, u32[]{:S(2)}) collective-permute-start(bf16[2,8,8,3585]{3,2,0,1:T(8,128)(2,1)S(1)} %fusion.83), channel_id=1, source_target_pairs={{0,8},{8,0},{1,9},{9,1},{2,10},{10,2},{3,11},{11,3},{4,12},{12,4},... | collective-permute-start | bytes 2753288 | tf_op jit(solution)/shard_map/ppermute | solution.py:28
  244.3 16.6 %copy-start.7 = (bf16[3584,512]{1,0:T(8,128)(2,1)S(1)}, bf16[3584,512]{1,0:T(8,128)(2,1)}, u32[]{:S(2)}) copy-start(bf16[3584,512]{1,0:T(8,128)(2,1)} %param.23) | copy-start | bytes 11010052
  256.9 3.9 %collective-permute-start.7 = (bf16[8,8,3584]{2,1,0:T(8,128)(2,1)S(1)}, bf16[8,8,3584]{2,1,0:T(8,128)(2,1)S(1)}, u32[]{:S(2)}, u32[]{:S(2)}) collective-permute-start(bf16[8,8,3584]{2,1,0:T(8,128)(2,1)S(1)} %all_to_all.97), channel_id=1, source_target_pairs={{0,8},{8,0},{1,9},{9,1},{2,10},{10,2},{3,11},{11,3},{4,12},{12,4},... | collective-permute-start | bytes 1376264 | tf_op jit(solution)/shard_map/ppermute | solution.py:28
  262.2 10.4 %all-to-all-start.16 = ((f32[8,16,512]{2,1,0:T(8,128)}), f32[8,16,512]{2,1,0:T(8,128)S(1)}, u32[]{:S(2)}, u32[]{:S(2)}) async-start(f32[8,16,512]{2,1,0:T(8,128)} %fusion.12), calls=%async_computation.16 | async-start | bytes 524288 | tf_op jit(solution)/shard_map/all_to_all | solution.py:89

commit v6 on v5

--- a/solution.py
+++ b/solution.py
@@ -251,18 +251,48 @@
         )
         stream = (stream.astype(jnp.float32) + summed).astype(jnp.bfloat16)
         rows_in, partial_sum = gathered_rows(stream, mlp_gain)
+        chips = lax.axis_size(CHIPS)
+        core = lax.axis_index(CORES)
+        by_core = rows_in.reshape(chips, 2, -1, rows_in.shape[1])
+        sums_by_core = partial_sum.reshape(chips, 2, -1)
+        reordered = jnp.concatenate(
+            [
+                lax.dynamic_index_in_dim(by_core, 1 - core, 1, keepdims=False),
+                lax.dynamic_index_in_dim(by_core, core, 1, keepdims=False),
+            ]
+        ).reshape(rows_in.shape)
+        reordered_sums = jnp.concatenate(
+            [
+                lax.dynamic_index_in_dim(sums_by_core, 1 - core, 1, keepdims=False),
+                lax.dynamic_index_in_dim(sums_by_core, core, 1, keepdims=False),
+            ]
+        ).reshape(partial_sum.shape)
         both_parts = jnp.einsum(
-            "rd,dkh->krh", rows_in, gate_up, preferred_element_type=jnp.float32
+            "rd,dkh->krh", reordered, gate_up, preferred_element_type=jnp.float32
         ).astype(jnp.bfloat16)
-        high, low = split_hi_lo(partial_sum)
+        high, low = split_hi_lo(reordered_sums)
         sums_col = jnp.stack([high, low])[:, :, None]
         payload = jnp.concatenate([both_parts, sums_col], axis=2)
-        pair_sum, row_dim = reduced_rows(payload, 1, jnp.bfloat16)
-        pair_squares = pair_sum[0, :, :, hidden_dev] + pair_sum[1, :, :, hidden_dev]
+        half = payload.shape[1] // 2
+        block_shape = (2, chips, half // chips, hidden_dev + 1)
+        to_partner = payload[:, :half].reshape(block_shape)
+        kept = payload[:, half:].reshape(block_shape)
+        from_partner = swap_cores(to_partner)
+        pair_squares = (
+            kept[0, :, :, hidden_dev].astype(jnp.float32)
+            + kept[1, :, :, hidden_dev].astype(jnp.float32)
+            + from_partner[0, :, :, hidden_dev].astype(jnp.float32)
+            + from_partner[1, :, :, hidden_dev].astype(jnp.float32)
+        )
         high, low = split_hi_lo(pair_squares)
-        pair_sum = pair_sum.astype(jnp.bfloat16)
-        pair_sum = pair_sum.at[0, :, :, hidden_dev].set(high).at[1, :, :, hidden_dev].set(low)
-        own = chip_sum(pair_sum, row_dim, jnp.bfloat16)
+        resplit = jnp.stack([high, low]).astype(jnp.float32)[..., None]
+        column = lax.broadcasted_iota(jnp.int32, block_shape, 3)
+        pair_sum = jnp.where(
+            column == hidden_dev,
+            resplit,
+            kept.astype(jnp.float32) + from_partner.astype(jnp.float32),
+        ).astype(jnp.bfloat16)
+        own = chip_sum(pair_sum, 1, jnp.bfloat16)
         scale = row_scale(own[0, :, hidden_dev] + own[1, :, hidden_dev])[:, None]
         gate = own[0, :, :hidden_dev] * scale
         up = own[1, :, :hidden_dev] * scale

time: 275 us -> 265 us (0.964)
  other arithmetic: 21.3 us -> 14.3 us
  blocking collectives: 135 us -> 132 us
    another operation x9 -> x5, other arithmetic: 7.65 us -> 1.01 us
    scatter x2 -> x0, local copies, waits for them, and re-layouts: 4.01 us -> none  [on_device(): pair_sum.at[0, :, :, hidden_dev].set(high).at[1, :, :, hidden_dev].set(low)]
  transfers between devices with their start and end apart: 13 -> 13, of which waited for: 12 -> 13; matrix products, arithmetic and copies ran while one was open for 2% -> 1% of each run, Pallas kernels for 0% -> 0%
where the time goes in v6:
time: 265 us; the launch traced here: 264 us
  blocking collectives  132 us (50%)
  starting transfers between devices  44.9 us (17%)
  waiting for transfers between devices  43.8 us (17%)
  matrix products  23 us (9%)
  other arithmetic  14.3 us (5%)
  local copies, waits for them, and re-layouts  4.86 us (2%)
    all_to_all x3, blocking collectives, chip_sum(): lax.all_to_all(pair_sum.astype(wire_type), CHIPS, row_dim, row_dim, tiled...  46.3 us
    all_to_all x4, blocking collectives, gathered_rows_wide(): lax.all_to_all(jnp.broadcast_to(shard[None], (chips, *shard.shape)), CHIP...  42.5 us
    all_to_all x3, blocking collectives, copy_for_each(): lax.all_to_all(jnp.broadcast_to(shard[None], (length, *shard.shape)), axi...  24.6 us
    ppermute x8, starting transfers between devices, swap_cores(): return lax.ppermute(shard, CORES, [(0, 1), (1, 0)])  21.1 us
    all_to_all x2, blocking collectives, summed_on_arrival(): lax.all_to_all(parts, axis, split_axis=0, concat_axis=0, tiled=True)  18.4 us
    all_to_all x2, starting transfers between devices, copy_for_each(): lax.all_to_all(jnp.broadcast_to(shard[None], (length, *shard.shape)), axi...  13.6 us
    all_to_all x2, waiting for transfers between devices, summed_on_arrival(): lax.all_to_all(parts, axis, split_axis=0, concat_axis=0, tiled=True)  13.2 us
    ppermute x8, waiting for transfers between devices, swap_cores(): return lax.ppermute(shard, CORES, [(0, 1), (1, 0)])  11.6 us
  transfers between devices with their start and end apart: 13, of which 13 were waited for; matrix products, arithmetic and copies ran while one was open for 1% of the time, Pallas kernels for 0%

profile of v6, /device:TPU:1, one launch (start us, length us, event | category | flops | bytes accessed | tf_op | source)
XLA Modules:
  0.0 263.9 jit_solution(11755723838342849104)
XLA Ops:
  2.2 8.4 %all-to-all-start = ((f32[16,1,16]{2,1,0:T(1,128)}), f32[16,1,16]{2,1,0:T(1,128)S(1)}, u32[]{:S(2)}, u32[]{:S(2)}) async-start(f32[16,1,16]{2,1,0:T(1,128)} %broadcast_in_dim.60), calls=%async_computation | async-start | bytes 16384 | tf_op jit(solution)/shard_map/all_to_all | solution.py:62
  12.1 5.4 %all-to-all-done = f32[16,1,16]{2,1,0:T(1,128)S(1)} async-done(((f32[16,1,16]{2,1,0:T(1,128)}), f32[16,1,16]{2,1,0:T(1,128)S(1)}, u32[]{:S(2)}, u32[]{:S(2)}) %all-to-all-start) | async-done | bytes 1056 | tf_op jit(solution)/shard_map/all_to_all | solution.py:62
  19.0 5.1 %all-to-all-start.1 = ((bf16[8,16,512]{2,1,0:T(8,128)(2,1)}), bf16[8,16,512]{2,1,0:T(8,128)(2,1)S(1)}, u32[]{:S(2)}, u32[]{:S(2)}) async-start(bf16[8,16,512]{2,1,0:T(8,128)(2,1)} %broadcast_in_dim.61), calls=%async_computation.1 | async-start | bytes 262144 | tf_op jit(solution)/shard_map/all_to_all | solution.py:62
  24.9 4.8 %all-to-all-done.1 = bf16[8,16,512]{2,1,0:T(8,128)(2,1)S(1)} async-done(((bf16[8,16,512]{2,1,0:T(8,128)(2,1)}), bf16[8,16,512]{2,1,0:T(8,128)(2,1)S(1)}, u32[]{:S(2)}, u32[]{:S(2)}) %all-to-all-start.1) | async-done | bytes 131104 | tf_op jit(solution)/shard_map/all_to_all | solution.py:62
  34.3 3.4 %all-to-all-start.2 = ((f32[8,8,1280]{2,1,0:T(8,128)}), f32[8,8,1280]{2,1,0:T(8,128)S(1)}, u32[]{:S(2)}, u32[]{:S(2)}) async-start(f32[8,8,1280]{2,1,0:T(8,128)} %bitcast_add_fusion), calls=%async_computation.2 | async-start | bytes 655360 | tf_op jit(solution)/shard_map/all_to_all | solution.py:44
  37.9 8.7 %all-to-all-done.2 = f32[8,8,1280]{2,1,0:T(8,128)S(1)} async-done(((f32[8,8,1280]{2,1,0:T(8,128)}), f32[8,8,1280]{2,1,0:T(8,128)S(1)}, u32[]{:S(2)}, u32[]{:S(2)}) %all-to-all-start.2) | async-done | bytes 327712 | tf_op jit(solution)/shard_map/all_to_all | solution.py:44
  47.1 2.7 %fusion.188 = (f32[8,8]{1,0:T(8,128)S(1)}, f32[8,8,9536]{2,1,0:T(8,128)S(1)}) fusion(bf16[8,8,128]{2,1,0:T(8,128)(2,1)S(1)} %fusion.141, bf16[2,2,9536,128]{3,2,1,0:T(8,128)(2,1)} %param.11, pred[8,9536]{1,0:T(8,128)(4,1)S(1)} %fusion.103), kind=kOutput, calls=%fused_computation.270 | convolution fusion | flops 158068672 | bytes 4975360 | tf_op jit(solution)/shard_map/rkgd,tkd->krgt/dot_general | solution.py:160
  52.9 9.3 %all_to_all.86 = bf16[8,8,1024]{2,1,0:T(8,128)(2,1)S(1)} all-to-all(bf16[8,8,1024]{2,1,0:T(8,128)(2,1)S(1)} %broadcast_in_dim.64), channel_id=1, replica_groups=mesh['chips'=8,'cores'=2,'narrow'=8] {'chips'}, dimensions={0} | all-to-all | bytes 262144 | tf_op jit(solution)/shard_map/all_to_all | solution.py:50
  62.2 2.6 collective-permute-start.1
  66.8 3.4 %all-to-all-start.4 = ((f32[8,16,512]{2,1,0:T(8,128)}), f32[8,16,512]{2,1,0:T(8,128)S(1)}, u32[]{:S(2)}, u32[]{:S(2)}) async-start(f32[8,16,512]{2,1,0:T(8,128)} %fusion.86), calls=%async_computation.4 | async-start | bytes 524288 | tf_op jit(solution)/shard_map/all_to_all | solution.py:89
  70.3 6.9 %all-to-all-done.4 = f32[8,16,512]{2,1,0:T(8,128)S(1)} async-done(((f32[8,16,512]{2,1,0:T(8,128)}), f32[8,16,512]{2,1,0:T(8,128)S(1)}, u32[]{:S(2)}, u32[]{:S(2)}) %all-to-all-start.4) | async-done | bytes 262176 | tf_op jit(solution)/shard_map/all_to_all | solution.py:89
  77.7 8.1 %all_to_all.87 = bf16[8,16,514]{2,1,0:T(8,128)(2,1)S(1)} all-to-all(bf16[8,16,514]{2,1,0:T(8,128)(2,1)S(1)} %broadcast_in_dim.65), channel_id=1, replica_groups=mesh['chips'=8,'cores'=2,'narrow'=8] {'narrow'}, dimensions={0} | all-to-all | bytes 263168 | tf_op jit(solution)/shard_map/all_to_all | solution.py:62
  86.4 4.2 %fusion.15 = bf16[2,128,3584]{2,1,0:T(8,128)(2,1)S(1)} fusion(bf16[512,2,3584]{2,1,0:T(2,128)(2,1)} %param.14, bf16[8,8,512]{2,1,0:T(8,128)(2,1)S(1)} %get-tuple-element.31, bf16[8,8,512]{2,1,0:T(8,128)(2,1)S(1)} %get-tuple-element.30), kind=kOutput, calls=%fused_computation.11 | convolution fusion | flops 940703744 | bytes 9306112 | tf_op jit(solution)/shard_map/rd,dkh->krh/dot_general | solution.py:270
  99.2 17.4 %all_to_all.88 = bf16[2,8,8,3585]{3,2,0,1:T(8,128)(2,1)S(1)} all-to-all(bf16[2,8,8,3585]{3,2,0,1:T(8,128)(2,1)S(1)} %copy.264), channel_id=1, replica_groups=mesh['chips'=8,'cores'=2,'narrow'=8] {'chips'}, dimensions={1} | all-to-all | bytes 1835520 | tf_op jit(solution)/shard_map/all_to_all | solution.py:44
  117.0 11.7 %all_to_all.89 = bf16[8,8,3584]{2,1,0:T(8,128)(2,1)S(1)} all-to-all(bf16[8,8,3584]{2,1,0:T(8,128)(2,1)S(1)} %broadcast_in_dim.69), channel_id=1, replica_groups=mesh['chips'=8,'cores'=2,'narrow'=8] {'chips'}, dimensions={0} | all-to-all | bytes 917504 | tf_op jit(solution)/shard_map/all_to_all | solution.py:50
  128.8 3.0 %collective-permute-start.3 = (bf16[8,8,3584]{2,1,0:T(8,128)(2,1)S(1)}, bf16[8,8,3584]{2,1,0:T(8,128)(2,1)S(1)}, u32[]{:S(2)}, u32[]{:S(2)}) collective-permute-start(bf16[8,8,3584]{2,1,0:T(8,128)(2,1)S(1)} %all_to_all.89), channel_id=1, source_target_pairs={{0,8},{8,0},{1,9},{9,1},{2,10},{10,2},{3,11},{11,3},{4,12},{12,4},... | collective-permute-start | bytes 1376264 | tf_op jit(solution)/shard_map/ppermute | solution.py:28
  133.9 9.0 %all_to_all.90 = f32[8,16,512]{2,1,0:T(8,128)S(1)} all-to-all(f32[8,16,512]{2,1,0:T(8,128)S(1)} %fusion.20), channel_id=1, replica_groups=mesh['chips'=8,'cores'=2,'narrow'=8] {'narrow'}, dimensions={0} | all-to-all | bytes 524288 | tf_op jit(solution)/shard_map/all_to_all | solution.py:89
  143.4 8.4 %all_to_all.91 = bf16[8,16,514]{2,1,0:T(8,128)(2,1)S(1)} all-to-all(bf16[8,16,514]{2,1,0:T(8,128)(2,1)S(1)} %broadcast_in_dim.70), channel_id=1, replica_groups=mesh['chips'=8,'cores'=2,'narrow'=8] {'narrow'}, dimensions={0} | all-to-all | bytes 263168 | tf_op jit(solution)/shard_map/all_to_all | solution.py:62
  152.3 2.6 collective-permute-start.4
  156.3 11.6 %all_to_all.92 = f32[8,8,1281]{2,1,0:T(8,128)S(1)} all-to-all(f32[8,8,1281]{2,1,0:T(8,128)S(1)} %fusion.102), channel_id=1, replica_groups=mesh['chips'=8,'cores'=2,'narrow'=8] {'chips'}, dimensions={0} | all-to-all | bytes 655872 | tf_op jit(solution)/shard_map/all_to_all | solution.py:44
  168.4 2.7 %fusion.189 = (f32[8,8]{1,0:T(8,128)S(1)}, f32[8,8,9536]{2,1,0:T(8,128)S(1)}) fusion(bf16[8,8,128]{2,1,0:T(8,128)(2,1)S(1)} %fusion.142, bf16[2,2,9536,128]{3,2,1,0:T(8,128)(2,1)} %param.11, pred[8,9536]{1,0:T(8,128)(4,1)S(1)} %fusion.103), kind=kOutput, calls=%fused_computation.271 | convolution fusion | flops 158068672 | bytes 4975360 | tf_op jit(solution)/shard_map/rkgd,tkd->krgt/dot_general | solution.py:160
  174.2 9.8 %all_to_all.93 = bf16[8,8,1024]{2,1,0:T(8,128)(2,1)S(1)} all-to-all(bf16[8,8,1024]{2,1,0:T(8,128)(2,1)S(1)} %broadcast_in_dim.72), channel_id=1, replica_groups=mesh['chips'=8,'cores'=2,'narrow'=8] {'chips'}, dimensions={0} | all-to-all | bytes 262144 | tf_op jit(solution)/shard_map/all_to_all | solution.py:50
  184.0 2.8 %collective-permute-start.5 = (bf16[8,8,1024]{2,1,0:T(8,128)(2,1)S(1)}, bf16[8,8,1024]{2,1,0:T(8,128)(2,1)S(1)}, u32[]{:S(2)}, u32[]{:S(2)}) collective-permute-start(bf16[8,8,1024]{2,1,0:T(8,128)(2,1)S(1)} %all_to_all.93), channel_id=1, source_target_pairs={{0,8},{8,0},{1,9},{9,1},{2,10},{10,2},{3,11},{11,3},{4,12},{12,4},... | collective-permute-start | bytes 393224 | tf_op jit(solution)/shard_map/ppermute | solution.py:28
  188.1 9.4 %all_to_all.94 = f32[8,16,512]{2,1,0:T(8,128)S(1)} all-to-all(f32[8,16,512]{2,1,0:T(8,128)S(1)} %fusion.84), channel_id=1, replica_groups=mesh['chips'=8,'cores'=2,'narrow'=8] {'narrow'}, dimensions={0} | all-to-all | bytes 524288 | tf_op jit(solution)/shard_map/all_to_all | solution.py:89
  198.0 8.1 %all_to_all.95 = bf16[8,16,514]{2,1,0:T(8,128)(2,1)S(1)} all-to-all(bf16[8,16,514]{2,1,0:T(8,128)(2,1)S(1)} %broadcast_in_dim.73), channel_id=1, replica_groups=mesh['chips'=8,'cores'=2,'narrow'=8] {'narrow'}, dimensions={0} | all-to-all | bytes 263168 | tf_op jit(solution)/shard_map/all_to_all | solution.py:62
  206.7 4.2 %fusion.12 = bf16[2,128,3584]{2,1,0:T(8,128)(2,1)S(1)} fusion(bf16[512,2,3584]{2,1,0:T(2,128)(2,1)} %param.14, bf16[8,8,512]{2,1,0:T(8,128)(2,1)S(1)} %get-tuple-element.29, bf16[8,8,512]{2,1,0:T(8,128)(2,1)S(1)} %get-tuple-element.28), kind=kOutput, calls=%fused_computation.10 | convolution fusion | flops 940703744 | bytes 9306112 | tf_op jit(solution)/shard_map/rd,dkh->krh/dot_general | solution.py:270
  212.0 2.5 collective-permute-start.6
  217.5 17.4 %all_to_all.96 = bf16[2,8,8,3585]{3,2,0,1:T(8,128)(2,1)S(1)} all-to-all(bf16[2,8,8,3585]{3,2,0,1:T(8,128)(2,1)S(1)} %copy.280), channel_id=1, replica_groups=mesh['chips'=8,'cores'=2,'narrow'=8] {'chips'}, dimensions={1} | all-to-all | bytes 1835520 | tf_op jit(solution)/shard_map/all_to_all | solution.py:44
  235.3 11.7 %all_to_all.97 = bf16[8,8,3584]{2,1,0:T(8,128)(2,1)S(1)} all-to-all(bf16[8,8,3584]{2,1,0:T(8,128)(2,1)S(1)} %broadcast_in_dim.77), channel_id=1, replica_groups=mesh['chips'=8,'cores'=2,'narrow'=8] {'chips'}, dimensions={0} | all-to-all | bytes 917504 | tf_op jit(solution)/shard_map/all_to_all | solution.py:50
  247.1 3.0 %collective-permute-start.7 = (bf16[8,8,3584]{2,1,0:T(8,128)(2,1)S(1)}, bf16[8,8,3584]{2,1,0:T(8,128)(2,1)S(1)}, u32[]{:S(2)}, u32[]{:S(2)}) collective-permute-start(bf16[8,8,3584]{2,1,0:T(8,128)(2,1)S(1)} %all_to_all.97), channel_id=1, source_target_pairs={{0,8},{8,0},{1,9},{9,1},{2,10},{10,2},{3,11},{11,3},{4,12},{12,4},... | collective-permute-start | bytes 1376264 | tf_op jit(solution)/shard_map/ppermute | solution.py:28
  252.9 3.4 %all-to-all-start.16 = ((f32[8,16,512]{2,1,0:T(8,128)}), f32[8,16,512]{2,1,0:T(8,128)S(1)}, u32[]{:S(2)}, u32[]{:S(2)}) async-start(f32[8,16,512]{2,1,0:T(8,128)} %fusion.18), calls=%async_computation.16 | async-start | bytes 524288 | tf_op jit(solution)/shard_map/all_to_all | solution.py:89
  257.0 6.3 %all-to-all-done.16 = f32[8,16,512]{2,1,0:T(8,128)S(1)} async-done(((f32[8,16,512]{2,1,0:T(8,128)}), f32[8,16,512]{2,1,0:T(8,128)S(1)}, u32[]{:S(2)}, u32[]{:S(2)}) %all-to-all-start.16) | async-done | bytes 262176 | tf_op jit(solution)/shard_map/all_to_all | solution.py:89
  (165 shorter events, 44.3 us)
Async XLA Ops:
  0.6 29.1 %copy-start = (bf16[512,1,1280]{2,0,1:T(8,128)(2,1)S(1)}, bf16[512,1,1280]{2,0,1:T(8,128)(2,1)}, u32[]{:S(2)}) copy-start(bf16[512,1,1280]{2,0,1:T(8,128)(2,1)} %param.12) | copy-start | bytes 3932164
  2.2 15.4 %all-to-all-start = ((f32[16,1,16]{2,1,0:T(1,128)}), f32[16,1,16]{2,1,0:T(1,128)S(1)}, u32[]{:S(2)}, u32[]{:S(2)}) async-start(f32[16,1,16]{2,1,0:T(1,128)} %broadcast_in_dim.60), calls=%async_computation | async-start | bytes 16384 | tf_op jit(solution)/shard_map/all_to_all | solution.py:62
  19.0 10.7 %all-to-all-start.1 = ((bf16[8,16,512]{2,1,0:T(8,128)(2,1)}), bf16[8,16,512]{2,1,0:T(8,128)(2,1)S(1)}, u32[]{:S(2)}, u32[]{:S(2)}) async-start(bf16[8,16,512]{2,1,0:T(8,128)(2,1)} %broadcast_in_dim.61), calls=%async_computation.1 | async-start | bytes 262144 | tf_op jit(solution)/shard_map/all_to_all | solution.py:62
  30.2 3.4 %collective-permute-start = (f32[8,8,1280]{2,1,0:T(8,128)S(1)}, f32[8,8,1280]{2,1,0:T(8,128)S(1)}, u32[]{:S(2)}, u32[]{:S(2)}) collective-permute-start(f32[8,8,1280]{2,1,0:T(8,128)S(1)} %dynamic-slice_bitcast_fusion), channel_id=1, source_target_pairs={{0,8},{8,0},{1,9},{9,1},{2,10},{10,2},{3,11},{11,3},{4,12},{12,4},... | collective-permute-start | bytes 983048 | tf_op jit(solution)/shard_map/ppermute | solution.py:28
  34.3 12.3 %all-to-all-start.2 = ((f32[8,8,1280]{2,1,0:T(8,128)}), f32[8,8,1280]{2,1,0:T(8,128)S(1)}, u32[]{:S(2)}, u32[]{:S(2)}) async-start(f32[8,8,1280]{2,1,0:T(8,128)} %bitcast_add_fusion), calls=%async_computation.2 | async-start | bytes 655360 | tf_op jit(solution)/shard_map/all_to_all | solution.py:44
  50.4 15.4 %copy-start.1 = (bf16[1024,512]{1,0:T(8,128)(2,1)S(1)}, bf16[1024,512]{1,0:T(8,128)(2,1)}, u32[]{:S(2)}) copy-start(bf16[1024,512]{1,0:T(8,128)(2,1)} %param.13) | copy-start | bytes 3145732
  52.8 17.4 %copy-start.3 = (bf16[512]{0:T(512)(128)(2,1)S(1)}, bf16[512]{0:T(512)(128)(2,1)}, u32[]{:S(2)}) copy-start(bf16[512]{0:T(512)(128)(2,1)} %param.17) | copy-start | bytes 3076
  52.9 24.4 %copy-start.2 = (bf16[16,512]{1,0:T(8,128)(2,1)S(1)}, bf16[16,512]{1,0:T(8,128)(2,1)}, u32[]{:S(2)}) copy-start(bf16[16,512]{1,0:T(8,128)(2,1)} %param.9) | copy-start | bytes 49156
  62.2 3.6 %collective-permute-start.1 = (bf16[8,8,1024]{2,1,0:T(8,128)(2,1)S(1)}, bf16[8,8,1024]{2,1,0:T(8,128)(2,1)S(1)}, u32[]{:S(2)}, u32[]{:S(2)}) collective-permute-start(bf16[8,8,1024]{2,1,0:T(8,128)(2,1)S(1)} %all_to_all.86), channel_id=1, source_target_pairs={{0,8},{8,0},{1,9},{9,1},{2,10},{10,2},{3,11},{11,3},{4,12},{12,4},... | collective-permute-start | bytes 393224 | tf_op jit(solution)/shard_map/ppermute | solution.py:28
  66.8 10.4 %all-to-all-start.4 = ((f32[8,16,512]{2,1,0:T(8,128)}), f32[8,16,512]{2,1,0:T(8,128)S(1)}, u32[]{:S(2)}, u32[]{:S(2)}) async-start(f32[8,16,512]{2,1,0:T(8,128)} %fusion.86), calls=%async_computation.4 | async-start | bytes 524288 | tf_op jit(solution)/shard_map/all_to_all | solution.py:89
  91.7 5.0 %collective-permute-start.2 = (bf16[2,8,8,3585]{3,2,1,0:T(8,128)(2,1)}, bf16[2,8,8,3585]{3,2,1,0:T(8,128)(2,1)}, u32[]{:S(2)}, u32[]{:S(2)}) collective-permute-start(bf16[2,8,8,3585]{3,2,1,0:T(8,128)(2,1)} %get-tuple-element.11), channel_id=1, source_target_pairs={{0,8},{8,0},{1,9},{9,1},{2,10},{10,2},{3,11},{11,3},{4,12},{12,4},... | collective-permute-start | bytes 2753288 | tf_op jit(solution)/shard_map/ppermute | solution.py:28
  116.6 16.6 %copy-start.4 = (bf16[3584,512]{1,0:T(8,128)(2,1)S(1)}, bf16[3584,512]{1,0:T(8,128)(2,1)}, u32[]{:S(2)}) copy-start(bf16[3584,512]{1,0:T(8,128)(2,1)} %param.15) | copy-start | bytes 11010052
  128.8 4.4 %collective-permute-start.3 = (bf16[8,8,3584]{2,1,0:T(8,128)(2,1)S(1)}, bf16[8,8,3584]{2,1,0:T(8,128)(2,1)S(1)}, u32[]{:S(2)}, u32[]{:S(2)}) collective-permute-start(bf16[8,8,3584]{2,1,0:T(8,128)(2,1)S(1)} %all_to_all.89), channel_id=1, source_target_pairs={{0,8},{8,0},{1,9},{9,1},{2,10},{10,2},{3,11},{11,3},{4,12},{12,4},... | collective-permute-start | bytes 1376264 | tf_op jit(solution)/shard_map/ppermute | solution.py:28
  152.3 3.9 %collective-permute-start.4 = (f32[8,8,1281]{2,1,0:T(8,128)S(1)}, f32[8,8,1281]{2,1,0:T(8,128)S(1)}, u32[]{:S(2)}, u32[]{:S(2)}) collective-permute-start(f32[8,8,1281]{2,1,0:T(8,128)S(1)} %fusion.99), channel_id=1, source_target_pairs={{0,8},{8,0},{1,9},{9,1},{2,10},{10,2},{3,11},{11,3},{4,12},{12,4},... | collective-permute-start | bytes 983816 | tf_op jit(solution)/shard_map/ppermute | solution.py:28
  184.0 3.8 %collective-permute-start.5 = (bf16[8,8,1024]{2,1,0:T(8,128)(2,1)S(1)}, bf16[8,8,1024]{2,1,0:T(8,128)(2,1)S(1)}, u32[]{:S(2)}, u32[]{:S(2)}) collective-permute-start(bf16[8,8,1024]{2,1,0:T(8,128)(2,1)S(1)} %all_to_all.93), channel_id=1, source_target_pairs={{0,8},{8,0},{1,9},{9,1},{2,10},{10,2},{3,11},{11,3},{4,12},{12,4},... | collective-permute-start | bytes 393224 | tf_op jit(solution)/shard_map/ppermute | solution.py:28
  212.0 4.9 %collective-permute-start.6 = (bf16[2,8,8,3585]{3,2,1,0:T(8,128)(2,1)}, bf16[2,8,8,3585]{3,2,1,0:T(8,128)(2,1)S(1)}, u32[]{:S(2)}, u32[]{:S(2)}) collective-permute-start(bf16[2,8,8,3585]{3,2,1,0:T(8,128)(2,1)} %get-tuple-element.9), channel_id=1, source_target_pairs={{0,8},{8,0},{1,9},{9,1},{2,10},{10,2},{3,11},{11,3},{4,12},{12,4},... | collective-permute-start | bytes 2753288 | tf_op jit(solution)/shard_map/ppermute | solution.py:28
  234.9 16.6 %copy-start.5 = (bf16[3584,512]{1,0:T(8,128)(2,1)S(1)}, bf16[3584,512]{1,0:T(8,128)(2,1)}, u32[]{:S(2)}) copy-start(bf16[3584,512]{1,0:T(8,128)(2,1)} %param.15) | copy-start | bytes 11010052
  247.1 4.4 %collective-permute-start.7 = (bf16[8,8,3584]{2,1,0:T(8,128)(2,1)S(1)}, bf16[8,8,3584]{2,1,0:T(8,128)(2,1)S(1)}, u32[]{:S(2)}, u32[]{:S(2)}) collective-permute-start(bf16[8,8,3584]{2,1,0:T(8,128)(2,1)S(1)} %all_to_all.97), channel_id=1, source_target_pairs={{0,8},{8,0},{1,9},{9,1},{2,10},{10,2},{3,11},{11,3},{4,12},{12,4},... | collective-permute-start | bytes 1376264 | tf_op jit(solution)/shard_map/ppermute | solution.py:28
  252.9 10.3 %all-to-all-start.16 = ((f32[8,16,512]{2,1,0:T(8,128)}), f32[8,16,512]{2,1,0:T(8,128)S(1)}, u32[]{:S(2)}, u32[]{:S(2)}) async-start(f32[8,16,512]{2,1,0:T(8,128)} %fusion.18), calls=%async_computation.16 | async-start | bytes 524288 | tf_op jit(solution)/shard_map/all_to_all | solution.py:89

commit v7 on v6

--- a/solution.py
+++ b/solution.py
@@ -105,7 +105,8 @@
 
 def norm_rows(stream, gain):
     floats = stream.astype(jnp.float32)
-    square_sum = of_everyone(jnp.sum(floats * floats, axis=1), WIDE)
+    own_sum = jnp.sum(floats * floats, axis=1)
+    square_sum = of_everyone(own_sum + swap_cores(own_sum), CHIPS)
     return gathered_copies(scale_rows(floats, square_sum, gain), "narrow", 0)
 
 

time: 265 us -> 266 us (level)
    ppermute x8 -> x9, starting transfers between devices: 21.1 us -> 23.7 us  [swap_cores(): return lax.ppermute(shard, CORES, [(0, 1), (1, 0)])]
    ppermute x8 -> x9, waiting for transfers between devices: 11.6 us -> 12.4 us  [swap_cores(): return lax.ppermute(shard, CORES, [(0, 1), (1, 0)])]
  transfers between devices with their start and end apart: 13 -> 14, of which waited for: 13 -> 14; matrix products, arithmetic and copies ran while one was open for 1% -> 1% of each run, Pallas kernels for 0% -> 0%
where the time goes in v7:
time: 266 us; the launch traced here: 265 us
  blocking collectives  132 us (50%)
  starting transfers between devices  45.8 us (17%)
  waiting for transfers between devices  44.1 us (17%)
  matrix products  22.9 us (9%)
  other arithmetic  14.3 us (5%)
  local copies, waits for them, and re-layouts  4.85 us (2%)
    all_to_all x3, blocking collectives, chip_sum(): lax.all_to_all(pair_sum.astype(wire_type), CHIPS, row_dim, row_dim, tiled...  46.3 us
    all_to_all x4, blocking collectives, gathered_rows_wide(): lax.all_to_all(jnp.broadcast_to(shard[None], (chips, *shard.shape)), CHIP...  42.5 us
    all_to_all x3, blocking collectives, copy_for_each(): lax.all_to_all(jnp.broadcast_to(shard[None], (length, *shard.shape)), axi...  24.6 us
    ppermute x9, starting transfers between devices, swap_cores(): return lax.ppermute(shard, CORES, [(0, 1), (1, 0)])  23.7 us
    all_to_all x2, blocking collectives, summed_on_arrival(): lax.all_to_all(parts, axis, split_axis=0, concat_axis=0, tiled=True)  18.4 us
    all_to_all x2, waiting for transfers between devices, summed_on_arrival(): lax.all_to_all(parts, axis, split_axis=0, concat_axis=0, tiled=True)  13.2 us
    ppermute x9, waiting for transfers between devices, swap_cores(): return lax.ppermute(shard, CORES, [(0, 1), (1, 0)])  12.4 us
    all_to_all x2, starting transfers between devices, copy_for_each(): lax.all_to_all(jnp.broadcast_to(shard[None], (length, *shard.shape)), axi...  11.9 us
  transfers between devices with their start and end apart: 14, of which 14 were waited for; matrix products, arithmetic and copies ran while one was open for 1% of the time, Pallas kernels for 0%

profile of v7, /device:TPU:1, one launch (start us, length us, event | category | flops | bytes accessed | tf_op | source)
XLA Modules:
  0.0 265.1 jit_solution(10249579826892880844)
XLA Ops:
  4.5 6.8 %all-to-all-start = ((f32[8,1,16]{2,1,0:T(1,128)}), f32[8,1,16]{2,1,0:T(1,128)S(1)}, u32[]{:S(2)}, u32[]{:S(2)}) async-start(f32[8,1,16]{2,1,0:T(1,128)} %broadcast_in_dim.60), calls=%async_computation | async-start | bytes 8192 | tf_op jit(solution)/shard_map/all_to_all | solution.py:62
  12.7 4.9 %all-to-all-done = f32[8,1,16]{2,1,0:T(1,128)S(1)} async-done(((f32[8,1,16]{2,1,0:T(1,128)}), f32[8,1,16]{2,1,0:T(1,128)S(1)}, u32[]{:S(2)}, u32[]{:S(2)}) %all-to-all-start) | async-done | bytes 544 | tf_op jit(solution)/shard_map/all_to_all | solution.py:62
  19.1 5.1 %all-to-all-start.1 = ((bf16[8,16,512]{2,1,0:T(8,128)(2,1)}), bf16[8,16,512]{2,1,0:T(8,128)(2,1)S(1)}, u32[]{:S(2)}, u32[]{:S(2)}) async-start(bf16[8,16,512]{2,1,0:T(8,128)(2,1)} %broadcast_in_dim.61), calls=%async_computation.1 | async-start | bytes 262144 | tf_op jit(solution)/shard_map/all_to_all | solution.py:62
  25.0 4.8 %all-to-all-done.1 = bf16[8,16,512]{2,1,0:T(8,128)(2,1)S(1)} async-done(((bf16[8,16,512]{2,1,0:T(8,128)(2,1)}), bf16[8,16,512]{2,1,0:T(8,128)(2,1)S(1)}, u32[]{:S(2)}, u32[]{:S(2)}) %all-to-all-start.1) | async-done | bytes 131104 | tf_op jit(solution)/shard_map/all_to_all | solution.py:62
  30.2 3.3 %collective-permute-start.1 = (f32[8,8,1280]{2,1,0:T(8,128)S(1)}, f32[8,8,1280]{2,1,0:T(8,128)S(1)}, u32[]{:S(2)}, u32[]{:S(2)}) collective-permute-start(f32[8,8,1280]{2,1,0:T(8,128)S(1)} %dynamic-slice_bitcast_fusion), channel_id=1, source_target_pairs={{0,8},{8,0},{1,9},{9,1},{2,10},{10,2},{3,11},{11,3},{4,12},{12,4},... | collective-permute-start | bytes 983048 | tf_op jit(solution)/shard_map/ppermute | solution.py:28
  35.5 3.4 %all-to-all-start.2 = ((f32[8,8,1280]{2,1,0:T(8,128)}), f32[8,8,1280]{2,1,0:T(8,128)S(1)}, u32[]{:S(2)}, u32[]{:S(2)}) async-start(f32[8,8,1280]{2,1,0:T(8,128)} %bitcast_add_fusion), calls=%async_computation.2 | async-start | bytes 655360 | tf_op jit(solution)/shard_map/all_to_all | solution.py:44
  39.1 8.7 %all-to-all-done.2 = f32[8,8,1280]{2,1,0:T(8,128)S(1)} async-done(((f32[8,8,1280]{2,1,0:T(8,128)}), f32[8,8,1280]{2,1,0:T(8,128)S(1)}, u32[]{:S(2)}, u32[]{:S(2)}) %all-to-all-start.2) | async-done | bytes 327712 | tf_op jit(solution)/shard_map/all_to_all | solution.py:44
  48.3 2.7 %fusion.188 = (f32[8,8]{1,0:T(8,128)S(1)}, f32[8,8,9536]{2,1,0:T(8,128)S(1)}) fusion(bf16[8,8,128]{2,1,0:T(8,128)(2,1)S(1)} %fusion.141, bf16[2,2,9536,128]{3,2,1,0:T(8,128)(2,1)} %param.11, pred[8,9536]{1,0:T(8,128)(4,1)S(1)} %fusion.103), kind=kOutput, calls=%fused_computation.270 | convolution fusion | flops 158068672 | bytes 4975360 | tf_op jit(solution)/shard_map/rkgd,tkd->krgt/dot_general | solution.py:161
  54.1 9.3 %all_to_all.86 = bf16[8,8,1024]{2,1,0:T(8,128)(2,1)S(1)} all-to-all(bf16[8,8,1024]{2,1,0:T(8,128)(2,1)S(1)} %broadcast_in_dim.64), channel_id=1, replica_groups=mesh['chips'=8,'cores'=2,'narrow'=8] {'chips'}, dimensions={0} | all-to-all | bytes 262144 | tf_op jit(solution)/shard_map/all_to_all | solution.py:50
  63.4 2.6 collective-permute-start.2
  68.0 3.4 %all-to-all-start.4 = ((f32[8,16,512]{2,1,0:T(8,128)}), f32[8,16,512]{2,1,0:T(8,128)S(1)}, u32[]{:S(2)}, u32[]{:S(2)}) async-start(f32[8,16,512]{2,1,0:T(8,128)} %fusion.86), calls=%async_computation.4 | async-start | bytes 524288 | tf_op jit(solution)/shard_map/all_to_all | solution.py:89
  71.5 6.9 %all-to-all-done.4 = f32[8,16,512]{2,1,0:T(8,128)S(1)} async-done(((f32[8,16,512]{2,1,0:T(8,128)}), f32[8,16,512]{2,1,0:T(8,128)S(1)}, u32[]{:S(2)}, u32[]{:S(2)}) %all-to-all-start.4) | async-done | bytes 262176 | tf_op jit(solution)/shard_map/all_to_all | solution.py:89
  78.9 8.1 %all_to_all.87 = bf16[8,16,514]{2,1,0:T(8,128)(2,1)S(1)} all-to-all(bf16[8,16,514]{2,1,0:T(8,128)(2,1)S(1)} %broadcast_in_dim.65), channel_id=1, replica_groups=mesh['chips'=8,'cores'=2,'narrow'=8] {'narrow'}, dimensions={0} | all-to-all | bytes 263168 | tf_op jit(solution)/shard_map/all_to_all | solution.py:62
  87.6 4.2 %fusion.15 = bf16[2,128,3584]{2,1,0:T(8,128)(2,1)S(1)} fusion(bf16[512,2,3584]{2,1,0:T(2,128)(2,1)} %param.14, bf16[8,8,512]{2,1,0:T(8,128)(2,1)S(1)} %get-tuple-element.31, bf16[8,8,512]{2,1,0:T(8,128)(2,1)S(1)} %get-tuple-element.30), kind=kOutput, calls=%fused_computation.11 | convolution fusion | flops 940703744 | bytes 9306112 | tf_op jit(solution)/shard_map/rd,dkh->krh/dot_general | solution.py:271
  100.4 17.4 %all_to_all.88 = bf16[2,8,8,3585]{3,2,0,1:T(8,128)(2,1)S(1)} all-to-all(bf16[2,8,8,3585]{3,2,0,1:T(8,128)(2,1)S(1)} %copy.264), channel_id=1, replica_groups=mesh['chips'=8,'cores'=2,'narrow'=8] {'chips'}, dimensions={1} | all-to-all | bytes 1835520 | tf_op jit(solution)/shard_map/all_to_all | solution.py:44
  118.2 11.7 %all_to_all.89 = bf16[8,8,3584]{2,1,0:T(8,128)(2,1)S(1)} all-to-all(bf16[8,8,3584]{2,1,0:T(8,128)(2,1)S(1)} %broadcast_in_dim.69), channel_id=1, replica_groups=mesh['chips'=8,'cores'=2,'narrow'=8] {'chips'}, dimensions={0} | all-to-all | bytes 917504 | tf_op jit(solution)/shard_map/all_to_all | solution.py:50
  130.0 3.0 %collective-permute-start.4 = (bf16[8,8,3584]{2,1,0:T(8,128)(2,1)S(1)}, bf16[8,8,3584]{2,1,0:T(8,128)(2,1)S(1)}, u32[]{:S(2)}, u32[]{:S(2)}) collective-permute-start(bf16[8,8,3584]{2,1,0:T(8,128)(2,1)S(1)} %all_to_all.89), channel_id=1, source_target_pairs={{0,8},{8,0},{1,9},{9,1},{2,10},{10,2},{3,11},{11,3},{4,12},{12,4},... | collective-permute-start | bytes 1376264 | tf_op jit(solution)/shard_map/ppermute | solution.py:28
  135.1 9.0 %all_to_all.90 = f32[8,16,512]{2,1,0:T(8,128)S(1)} all-to-all(f32[8,16,512]{2,1,0:T(8,128)S(1)} %fusion.20), channel_id=1, replica_groups=mesh['chips'=8,'cores'=2,'narrow'=8] {'narrow'}, dimensions={0} | all-to-all | bytes 524288 | tf_op jit(solution)/shard_map/all_to_all | solution.py:89
  144.6 8.5 %all_to_all.91 = bf16[8,16,514]{2,1,0:T(8,128)(2,1)S(1)} all-to-all(bf16[8,16,514]{2,1,0:T(8,128)(2,1)S(1)} %broadcast_in_dim.70), channel_id=1, replica_groups=mesh['chips'=8,'cores'=2,'narrow'=8] {'narrow'}, dimensions={0} | all-to-all | bytes 263168 | tf_op jit(solution)/shard_map/all_to_all | solution.py:62
  153.5 2.6 collective-permute-start.5
  157.5 11.6 %all_to_all.92 = f32[8,8,1281]{2,1,0:T(8,128)S(1)} all-to-all(f32[8,8,1281]{2,1,0:T(8,128)S(1)} %fusion.102), channel_id=1, replica_groups=mesh['chips'=8,'cores'=2,'narrow'=8] {'chips'}, dimensions={0} | all-to-all | bytes 655872 | tf_op jit(solution)/shard_map/all_to_all | solution.py:44
  169.6 2.7 %fusion.189 = (f32[8,8]{1,0:T(8,128)S(1)}, f32[8,8,9536]{2,1,0:T(8,128)S(1)}) fusion(bf16[8,8,128]{2,1,0:T(8,128)(2,1)S(1)} %fusion.142, bf16[2,2,9536,128]{3,2,1,0:T(8,128)(2,1)} %param.11, pred[8,9536]{1,0:T(8,128)(4,1)S(1)} %fusion.103), kind=kOutput, calls=%fused_computation.271 | convolution fusion | flops 158068672 | bytes 4975360 | tf_op jit(solution)/shard_map/rkgd,tkd->krgt/dot_general | solution.py:161
  175.4 9.8 %all_to_all.93 = bf16[8,8,1024]{2,1,0:T(8,128)(2,1)S(1)} all-to-all(bf16[8,8,1024]{2,1,0:T(8,128)(2,1)S(1)} %broadcast_in_dim.72), channel_id=1, replica_groups=mesh['chips'=8,'cores'=2,'narrow'=8] {'chips'}, dimensions={0} | all-to-all | bytes 262144 | tf_op jit(solution)/shard_map/all_to_all | solution.py:50
  185.2 2.8 %collective-permute-start.6 = (bf16[8,8,1024]{2,1,0:T(8,128)(2,1)S(1)}, bf16[8,8,1024]{2,1,0:T(8,128)(2,1)S(1)}, u32[]{:S(2)}, u32[]{:S(2)}) collective-permute-start(bf16[8,8,1024]{2,1,0:T(8,128)(2,1)S(1)} %all_to_all.93), channel_id=1, source_target_pairs={{0,8},{8,0},{1,9},{9,1},{2,10},{10,2},{3,11},{11,3},{4,12},{12,4},... | collective-permute-start | bytes 393224 | tf_op jit(solution)/shard_map/ppermute | solution.py:28
  189.3 9.4 %all_to_all.94 = f32[8,16,512]{2,1,0:T(8,128)S(1)} all-to-all(f32[8,16,512]{2,1,0:T(8,128)S(1)} %fusion.84), channel_id=1, replica_groups=mesh['chips'=8,'cores'=2,'narrow'=8] {'narrow'}, dimensions={0} | all-to-all | bytes 524288 | tf_op jit(solution)/shard_map/all_to_all | solution.py:89
  199.2 8.1 %all_to_all.95 = bf16[8,16,514]{2,1,0:T(8,128)(2,1)S(1)} all-to-all(bf16[8,16,514]{2,1,0:T(8,128)(2,1)S(1)} %broadcast_in_dim.73), channel_id=1, replica_groups=mesh['chips'=8,'cores'=2,'narrow'=8] {'narrow'}, dimensions={0} | all-to-all | bytes 263168 | tf_op jit(solution)/shard_map/all_to_all | solution.py:62
  207.9 4.2 %fusion.12 = bf16[2,128,3584]{2,1,0:T(8,128)(2,1)S(1)} fusion(bf16[512,2,3584]{2,1,0:T(2,128)(2,1)} %param.14, bf16[8,8,512]{2,1,0:T(8,128)(2,1)S(1)} %get-tuple-element.29, bf16[8,8,512]{2,1,0:T(8,128)(2,1)S(1)} %get-tuple-element.28), kind=kOutput, calls=%fused_computation.10 | convolution fusion | flops 940703744 | bytes 9306112 | tf_op jit(solution)/shard_map/rd,dkh->krh/dot_general | solution.py:271
  218.8 17.4 %all_to_all.96 = bf16[2,8,8,3585]{3,2,0,1:T(8,128)(2,1)S(1)} all-to-all(bf16[2,8,8,3585]{3,2,0,1:T(8,128)(2,1)S(1)} %copy.280), channel_id=1, replica_groups=mesh['chips'=8,'cores'=2,'narrow'=8] {'chips'}, dimensions={1} | all-to-all | bytes 1835520 | tf_op jit(solution)/shard_map/all_to_all | solution.py:44
  236.6 11.7 %all_to_all.97 = bf16[8,8,3584]{2,1,0:T(8,128)(2,1)S(1)} all-to-all(bf16[8,8,3584]{2,1,0:T(8,128)(2,1)S(1)} %broadcast_in_dim.77), channel_id=1, replica_groups=mesh['chips'=8,'cores'=2,'narrow'=8] {'chips'}, dimensions={0} | all-to-all | bytes 917504 | tf_op jit(solution)/shard_map/all_to_all | solution.py:50
  248.3 3.0 %collective-permute-start.8 = (bf16[8,8,3584]{2,1,0:T(8,128)(2,1)S(1)}, bf16[8,8,3584]{2,1,0:T(8,128)(2,1)S(1)}, u32[]{:S(2)}, u32[]{:S(2)}) collective-permute-start(bf16[8,8,3584]{2,1,0:T(8,128)(2,1)S(1)} %all_to_all.97), channel_id=1, source_target_pairs={{0,8},{8,0},{1,9},{9,1},{2,10},{10,2},{3,11},{11,3},{4,12},{12,4},... | collective-permute-start | bytes 1376264 | tf_op jit(solution)/shard_map/ppermute | solution.py:28
  254.1 3.4 %all-to-all-start.16 = ((f32[8,16,512]{2,1,0:T(8,128)}), f32[8,16,512]{2,1,0:T(8,128)S(1)}, u32[]{:S(2)}, u32[]{:S(2)}) async-start(f32[8,16,512]{2,1,0:T(8,128)} %fusion.18), calls=%async_computation.16 | async-start | bytes 524288 | tf_op jit(solution)/shard_map/all_to_all | solution.py:89
  258.2 6.3 %all-to-all-done.16 = f32[8,16,512]{2,1,0:T(8,128)S(1)} async-done(((f32[8,16,512]{2,1,0:T(8,128)}), f32[8,16,512]{2,1,0:T(8,128)S(1)}, u32[]{:S(2)}, u32[]{:S(2)}) %all-to-all-start.16) | async-done | bytes 262176 | tf_op jit(solution)/shard_map/all_to_all | solution.py:89
  (168 shorter events, 47.0 us)
Async XLA Ops:
  0.6 29.2 %copy-start = (bf16[512,1,1280]{2,0,1:T(8,128)(2,1)S(1)}, bf16[512,1,1280]{2,0,1:T(8,128)(2,1)}, u32[]{:S(2)}) copy-start(bf16[512,1,1280]{2,0,1:T(8,128)(2,1)} %param.12) | copy-start | bytes 3932164
  1.6 2.3 collective-permute-start
  4.5 13.2 %all-to-all-start = ((f32[8,1,16]{2,1,0:T(1,128)}), f32[8,1,16]{2,1,0:T(1,128)S(1)}, u32[]{:S(2)}, u32[]{:S(2)}) async-start(f32[8,1,16]{2,1,0:T(1,128)} %broadcast_in_dim.60), calls=%async_computation | async-start | bytes 8192 | tf_op jit(solution)/shard_map/all_to_all | solution.py:62
  19.1 10.7 %all-to-all-start.1 = ((bf16[8,16,512]{2,1,0:T(8,128)(2,1)}), bf16[8,16,512]{2,1,0:T(8,128)(2,1)S(1)}, u32[]{:S(2)}, u32[]{:S(2)}) async-start(bf16[8,16,512]{2,1,0:T(8,128)(2,1)} %broadcast_in_dim.61), calls=%async_computation.1 | async-start | bytes 262144 | tf_op jit(solution)/shard_map/all_to_all | solution.py:62
  30.2 4.5 %collective-permute-start.1 = (f32[8,8,1280]{2,1,0:T(8,128)S(1)}, f32[8,8,1280]{2,1,0:T(8,128)S(1)}, u32[]{:S(2)}, u32[]{:S(2)}) collective-permute-start(f32[8,8,1280]{2,1,0:T(8,128)S(1)} %dynamic-slice_bitcast_fusion), channel_id=1, source_target_pairs={{0,8},{8,0},{1,9},{9,1},{2,10},{10,2},{3,11},{11,3},{4,12},{12,4},... | collective-permute-start | bytes 983048 | tf_op jit(solution)/shard_map/ppermute | solution.py:28
  35.5 12.3 %all-to-all-start.2 = ((f32[8,8,1280]{2,1,0:T(8,128)}), f32[8,8,1280]{2,1,0:T(8,128)S(1)}, u32[]{:S(2)}, u32[]{:S(2)}) async-start(f32[8,8,1280]{2,1,0:T(8,128)} %bitcast_add_fusion), calls=%async_computation.2 | async-start | bytes 655360 | tf_op jit(solution)/shard_map/all_to_all | solution.py:44
  51.6 15.4 %copy-start.1 = (bf16[1024,512]{1,0:T(8,128)(2,1)S(1)}, bf16[1024,512]{1,0:T(8,128)(2,1)}, u32[]{:S(2)}) copy-start(bf16[1024,512]{1,0:T(8,128)(2,1)} %param.13) | copy-start | bytes 3145732
  54.0 17.4 %copy-start.3 = (bf16[512]{0:T(512)(128)(2,1)S(1)}, bf16[512]{0:T(512)(128)(2,1)}, u32[]{:S(2)}) copy-start(bf16[512]{0:T(512)(128)(2,1)} %param.17) | copy-start | bytes 3076
  54.1 24.4 %copy-start.2 = (bf16[16,512]{1,0:T(8,128)(2,1)S(1)}, bf16[16,512]{1,0:T(8,128)(2,1)}, u32[]{:S(2)}) copy-start(bf16[16,512]{1,0:T(8,128)(2,1)} %param.9) | copy-start | bytes 49156
  63.4 3.6 %collective-permute-start.2 = (bf16[8,8,1024]{2,1,0:T(8,128)(2,1)S(1)}, bf16[8,8,1024]{2,1,0:T(8,128)(2,1)S(1)}, u32[]{:S(2)}, u32[]{:S(2)}) collective-permute-start(bf16[8,8,1024]{2,1,0:T(8,128)(2,1)S(1)} %all_to_all.86), channel_id=1, source_target_pairs={{0,8},{8,0},{1,9},{9,1},{2,10},{10,2},{3,11},{11,3},{4,12},{12,4},... | collective-permute-start | bytes 393224 | tf_op jit(solution)/shard_map/ppermute | solution.py:28
  68.0 10.4 %all-to-all-start.4 = ((f32[8,16,512]{2,1,0:T(8,128)}), f32[8,16,512]{2,1,0:T(8,128)S(1)}, u32[]{:S(2)}, u32[]{:S(2)}) async-start(f32[8,16,512]{2,1,0:T(8,128)} %fusion.86), calls=%async_computation.4 | async-start | bytes 524288 | tf_op jit(solution)/shard_map/all_to_all | solution.py:89
  92.9 5.0 %collective-permute-start.3 = (bf16[2,8,8,3585]{3,2,1,0:T(8,128)(2,1)}, bf16[2,8,8,3585]{3,2,1,0:T(8,128)(2,1)}, u32[]{:S(2)}, u32[]{:S(2)}) collective-permute-start(bf16[2,8,8,3585]{3,2,1,0:T(8,128)(2,1)} %get-tuple-element.11), channel_id=1, source_target_pairs={{0,8},{8,0},{1,9},{9,1},{2,10},{10,2},{3,11},{11,3},{4,12},{12,4},... | collective-permute-start | bytes 2753288 | tf_op jit(solution)/shard_map/ppermute | solution.py:28
  117.8 16.6 %copy-start.4 = (bf16[3584,512]{1,0:T(8,128)(2,1)S(1)}, bf16[3584,512]{1,0:T(8,128)(2,1)}, u32[]{:S(2)}) copy-start(bf16[3584,512]{1,0:T(8,128)(2,1)} %param.15) | copy-start | bytes 11010052
  130.0 4.4 %collective-permute-start.4 = (bf16[8,8,3584]{2,1,0:T(8,128)(2,1)S(1)}, bf16[8,8,3584]{2,1,0:T(8,128)(2,1)S(1)}, u32[]{:S(2)}, u32[]{:S(2)}) collective-permute-start(bf16[8,8,3584]{2,1,0:T(8,128)(2,1)S(1)} %all_to_all.89), channel_id=1, source_target_pairs={{0,8},{8,0},{1,9},{9,1},{2,10},{10,2},{3,11},{11,3},{4,12},{12,4},... | collective-permute-start | bytes 1376264 | tf_op jit(solution)/shard_map/ppermute | solution.py:28
  153.5 3.9 %collective-permute-start.5 = (f32[8,8,1281]{2,1,0:T(8,128)S(1)}, f32[8,8,1281]{2,1,0:T(8,128)S(1)}, u32[]{:S(2)}, u32[]{:S(2)}) collective-permute-start(f32[8,8,1281]{2,1,0:T(8,128)S(1)} %fusion.99), channel_id=1, source_target_pairs={{0,8},{8,0},{1,9},{9,1},{2,10},{10,2},{3,11},{11,3},{4,12},{12,4},... | collective-permute-start | bytes 983816 | tf_op jit(solution)/shard_map/ppermute | solution.py:28
  185.2 3.8 %collective-permute-start.6 = (bf16[8,8,1024]{2,1,0:T(8,128)(2,1)S(1)}, bf16[8,8,1024]{2,1,0:T(8,128)(2,1)S(1)}, u32[]{:S(2)}, u32[]{:S(2)}) collective-permute-start(bf16[8,8,1024]{2,1,0:T(8,128)(2,1)S(1)} %all_to_all.93), channel_id=1, source_target_pairs={{0,8},{8,0},{1,9},{9,1},{2,10},{10,2},{3,11},{11,3},{4,12},{12,4},... | collective-permute-start | bytes 393224 | tf_op jit(solution)/shard_map/ppermute | solution.py:28
  213.2 4.9 %collective-permute-start.7 = (bf16[2,8,8,3585]{3,2,1,0:T(8,128)(2,1)}, bf16[2,8,8,3585]{3,2,1,0:T(8,128)(2,1)S(1)}, u32[]{:S(2)}, u32[]{:S(2)}) collective-permute-start(bf16[2,8,8,3585]{3,2,1,0:T(8,128)(2,1)} %get-tuple-element.9), channel_id=1, source_target_pairs={{0,8},{8,0},{1,9},{9,1},{2,10},{10,2},{3,11},{11,3},{4,12},{12,4},... | collective-permute-start | bytes 2753288 | tf_op jit(solution)/shard_map/ppermute | solution.py:28
  236.1 16.6 %copy-start.5 = (bf16[3584,512]{1,0:T(8,128)(2,1)S(1)}, bf16[3584,512]{1,0:T(8,128)(2,1)}, u32[]{:S(2)}) copy-start(bf16[3584,512]{1,0:T(8,128)(2,1)} %param.15) | copy-start | bytes 11010052
  248.3 4.4 %collective-permute-start.8 = (bf16[8,8,3584]{2,1,0:T(8,128)(2,1)S(1)}, bf16[8,8,3584]{2,1,0:T(8,128)(2,1)S(1)}, u32[]{:S(2)}, u32[]{:S(2)}) collective-permute-start(bf16[8,8,3584]{2,1,0:T(8,128)(2,1)S(1)} %all_to_all.97), channel_id=1, source_target_pairs={{0,8},{8,0},{1,9},{9,1},{2,10},{10,2},{3,11},{11,3},{4,12},{12,4},... | collective-permute-start | bytes 1376264 | tf_op jit(solution)/shard_map/ppermute | solution.py:28
  254.1 10.3 %all-to-all-start.16 = ((f32[8,16,512]{2,1,0:T(8,128)}), f32[8,16,512]{2,1,0:T(8,128)S(1)}, u32[]{:S(2)}, u32[]{:S(2)}) async-start(f32[8,16,512]{2,1,0:T(8,128)} %fusion.18), calls=%async_computation.16 | async-start | bytes 524288 | tf_op jit(solution)/shard_map/all_to_all | solution.py:89

commit v8 on v6

--- a/solution.py
+++ b/solution.py
@@ -3,6 +3,7 @@
 import jax
 import jax.numpy as jnp
 from jax import lax
+from jax.experimental import pallas as pl
 from jax.sharding import Mesh
 from jax.sharding import PartitionSpec as P
 
@@ -183,6 +184,65 @@
     return jnp.transpose(normalized, (1, 0, 2, 3)).reshape(
         row_count, heads_kv * group_size * head_dim
     )
+
+
+def attention_kernel(q_ref, kn_ref, vn_ref, lo_ref, hi_ref, k_ref, v_ref, out_ref):
+    score_scale = 1.0 / math.sqrt(HD)
+    queries = q_ref[...]
+    keys = k_ref[...]
+    scores = lax.dot_general(
+        queries, keys, (((1,), (1,)), ((), ())), preferred_element_type=jnp.float32
+    ) * score_scale
+    position = lax.broadcasted_iota(jnp.int32, scores.shape, 1)
+    owned = (position >= lo_ref[...]) & (position < hi_ref[...])
+    scores = jnp.where(owned, scores, -jnp.inf)
+    query_floats = queries.astype(jnp.float32)
+    own_score = (
+        jnp.sum(query_floats * kn_ref[...].astype(jnp.float32), axis=1, keepdims=True)
+        * score_scale
+    )
+    peak = jnp.maximum(jnp.max(scores, axis=1, keepdims=True), own_score)
+    weights = jnp.exp(scores - peak)
+    own_weight = jnp.exp(own_score - peak)
+    weight_sum = jnp.sum(weights, axis=1, keepdims=True) + own_weight
+    blended = jnp.dot(
+        weights.astype(jnp.bfloat16), v_ref[...], preferred_element_type=jnp.float32
+    )
+    own_rounded = own_weight.astype(jnp.bfloat16).astype(jnp.float32)
+    blended = blended + own_rounded * vn_ref[...].astype(jnp.float32)
+    out_ref[...] = (blended / weight_sum).astype(out_ref.dtype)
+
+
+def attend_kernel(queries, key_new, value_new, kv_cache, layer_index, lengths):
+    row_count, heads_kv, group_size, head_dim = queries.shape
+    slot_count = kv_cache.shape[2]
+    rows = row_count * group_size
+    starts = jnp.cumsum(lengths) - lengths
+    lo = jnp.repeat(starts, group_size)[:, None].astype(jnp.int32)
+    hi = jnp.repeat(starts + lengths, group_size)[:, None].astype(jnp.int32)
+    q_rows = queries.reshape(rows, head_dim)
+    kn_rows = jnp.repeat(key_new.reshape(row_count, head_dim), group_size, axis=0)
+    vn_rows = jnp.repeat(value_new.reshape(row_count, head_dim), group_size, axis=0)
+    whole = lambda shape: pl.BlockSpec(shape, lambda i: (0,) * len(shape))
+    cache_spec = lambda which: pl.BlockSpec(
+        (None, None, slot_count, head_dim), lambda i: (layer_index, which, 0, 0)
+    )
+    out = pl.pallas_call(
+        attention_kernel,
+        grid=(1,),
+        in_specs=[
+            whole((rows, head_dim)),
+            whole((rows, head_dim)),
+            whole((rows, head_dim)),
+            whole((rows, 1)),
+            whole((rows, 1)),
+            cache_spec(0),
+            cache_spec(1),
+        ],
+        out_specs=whole((rows, head_dim)),
+        out_shape=jax.ShapeDtypeStruct((rows, head_dim), jnp.bfloat16),
+    )(q_rows, kn_rows, vn_rows, lo, hi, kv_cache, kv_cache)
+    return out.reshape(row_count, heads_kv * group_size * head_dim)
 
 
 def split_hi_lo(values):
@@ -242,9 +302,7 @@
                 ]
             )
         )
-        attended = attend(
-            queries, key_new, value_new, kv_cache[layer_index, 0], kv_cache[layer_index, 1], lengths
-        )
+        attended = attend_kernel(queries, key_new, value_new, kv_cache, layer_index, lengths)
         heads_all = gathered_rows_wide(attended)
         summed = summed_on_arrival(
             jnp.dot(heads_all, o_weight, preferred_element_type=jnp.float32), "narrow", 0

time: 265 us -> 269 us (1.015)
  matrix products: 23 us -> 12.4 us
  Pallas kernels: 0 us -> 10.4 us
  local copies, waits for them, and re-layouts: 4.86 us -> 10.7 us
    dot_general x6 -> x0, matrix products: 10.5 us -> none  [the longest x2 5.48 us: attend(): jnp.einsum('rkgd,tkd->krgt', queries, key_table, preferred_element_type=j...]
    pallas_call x0 -> x2, Pallas kernels: none -> 10.4 us  [attend_kernel(): pl.pallas_call(attention_kernel, grid=(1,), in_specs=[whole((rows, head_d...]
  transfers between devices with their start and end apart: 13 -> 13, of which waited for: 13 -> 12; matrix products, arithmetic and copies ran while one was open for 1% -> 1% of each run, Pallas kernels for 0% -> 0%
where the time goes in v8:
time: 269 us; the launch traced here: 267 us
  blocking collectives  132 us (49%)
  starting transfers between devices  44.6 us (17%)
  waiting for transfers between devices  44.1 us (16%)
  matrix products  12.4 us (5%)
  other arithmetic  11.7 us (4%)
  local copies, waits for them, and re-layouts  10.7 us (4%)
  Pallas kernels  10.4 us (4%)
    all_to_all x3, blocking collectives, chip_sum(): lax.all_to_all(pair_sum.astype(wire_type), CHIPS, row_dim, row_dim, tiled...  46.3 us
    all_to_all x4, blocking collectives, gathered_rows_wide(): lax.all_to_all(jnp.broadcast_to(shard[None], (chips, *shard.shape)), CHIP...  43 us
    all_to_all x3, blocking collectives, copy_for_each(): lax.all_to_all(jnp.broadcast_to(shard[None], (length, *shard.shape)), axi...  24.6 us
    ppermute x8, starting transfers between devices, swap_cores(): return lax.ppermute(shard, CORES, [(0, 1), (1, 0)])  20.8 us
    all_to_all x2, blocking collectives, summed_on_arrival(): lax.all_to_all(parts, axis, split_axis=0, concat_axis=0, tiled=True)  18.4 us
    all_to_all x2, starting transfers between devices, copy_for_each(): lax.all_to_all(jnp.broadcast_to(shard[None], (length, *shard.shape)), axi...  13.6 us
    all_to_all x2, waiting for transfers between devices, summed_on_arrival(): lax.all_to_all(parts, axis, split_axis=0, concat_axis=0, tiled=True)  13.2 us
    all_to_all x2, waiting for transfers between devices, copy_for_each(): lax.all_to_all(jnp.broadcast_to(shard[None], (length, *shard.shape)), axi...  11.8 us
  transfers between devices with their start and end apart: 13, of which 12 were waited for; matrix products, arithmetic and copies ran while one was open for 1% of the time, Pallas kernels for 0%

profile of v8, /device:TPU:1, one launch (start us, length us, event | category | flops | bytes accessed | tf_op | source)
XLA Modules:
  0.0 267.5 jit_solution(2457627702232078769)
XLA Ops:
  2.2 8.4 %all-to-all-start = ((f32[16,1,16]{2,1,0:T(1,128)}), f32[16,1,16]{2,1,0:T(1,128)S(1)}, u32[]{:S(2)}, u32[]{:S(2)}) async-start(f32[16,1,16]{2,1,0:T(1,128)} %broadcast_in_dim.55), calls=%async_computation | async-start | bytes 16384 | tf_op jit(solution)/shard_map/all_to_all | solution.py:63
  11.3 6.3 %all-to-all-done = f32[16,1,16]{2,1,0:T(1,128)S(1)} async-done(((f32[16,1,16]{2,1,0:T(1,128)}), f32[16,1,16]{2,1,0:T(1,128)S(1)}, u32[]{:S(2)}, u32[]{:S(2)}) %all-to-all-start) | async-done | bytes 1056 | tf_op jit(solution)/shard_map/all_to_all | solution.py:63
  19.0 5.1 %all-to-all-start.1 = ((bf16[8,16,512]{2,1,0:T(8,128)(2,1)}), bf16[8,16,512]{2,1,0:T(8,128)(2,1)S(1)}, u32[]{:S(2)}, u32[]{:S(2)}) async-start(bf16[8,16,512]{2,1,0:T(8,128)(2,1)} %broadcast_in_dim.56), calls=%async_computation.1 | async-start | bytes 262144 | tf_op jit(solution)/shard_map/all_to_all | solution.py:63
  24.2 5.6 %all-to-all-done.1 = bf16[8,16,512]{2,1,0:T(8,128)(2,1)S(1)} async-done(((bf16[8,16,512]{2,1,0:T(8,128)(2,1)}), bf16[8,16,512]{2,1,0:T(8,128)(2,1)S(1)}, u32[]{:S(2)}, u32[]{:S(2)}) %all-to-all-start.1) | async-done | bytes 131104 | tf_op jit(solution)/shard_map/all_to_all | solution.py:63
  34.8 3.4 %all-to-all-start.2 = ((f32[8,8,1280]{2,1,0:T(8,128)}), f32[8,8,1280]{2,1,0:T(8,128)S(1)}, u32[]{:S(2)}, u32[]{:S(2)}) async-start(f32[8,8,1280]{2,1,0:T(8,128)} %bitcast_add_fusion), calls=%async_computation.2 | async-start | bytes 655360 | tf_op jit(solution)/shard_map/all_to_all | solution.py:45
  38.3 8.6 %all-to-all-done.2 = f32[8,8,1280]{2,1,0:T(8,128)S(1)} async-done(((f32[8,8,1280]{2,1,0:T(8,128)}), f32[8,8,1280]{2,1,0:T(8,128)S(1)}, u32[]{:S(2)}, u32[]{:S(2)}) %all-to-all-start.2) | async-done | bytes 327712 | tf_op jit(solution)/shard_map/all_to_all | solution.py:45
  48.4 5.3 %shard_map.104 = bf16[64,128]{1,0:T(8,128)(2,1)} custom-call(bf16[64,128]{1,0:T(8,128)(2,1)} %bitcast.193, bf16[64,128]{1,0:T(8,128)(2,1)} %get-tuple-element.57.kn_ref, bf16[64,128]{1,0:T(8,128)(2,1)} %get-tuple-element.56.vn_ref, s32[64,1]{1,0:T(8,128)} %broadcast_in_dim_reshape.12.lo_ref, s32[64,1]{1,0:T(8,128)} %broadcast_in_dim_reshape.13.hi_ref, ...), custom_call_target="tpu_custom_call" | custom-call | tf_op jit(solution)/shard_map/pallas_call | solution.py:230
  54.5 9.8 %all_to_all.86 = bf16[8,8,1024]{2,1,0:T(8,128)(2,1)S(1)} all-to-all(bf16[8,8,1024]{2,1,0:T(8,128)(2,1)S(1)} %broadcast_in_dim.62), channel_id=1, replica_groups=mesh['chips'=8,'cores'=2,'narrow'=8] {'chips'}, dimensions={0} | all-to-all | bytes 262144 | tf_op jit(solution)/shard_map/all_to_all | solution.py:51
  68.6 3.4 %all-to-all-start.4 = ((f32[8,16,512]{2,1,0:T(8,128)}), f32[8,16,512]{2,1,0:T(8,128)S(1)}, u32[]{:S(2)}, u32[]{:S(2)}) async-start(f32[8,16,512]{2,1,0:T(8,128)} %fusion.26), calls=%async_computation.4 | async-start | bytes 524288 | tf_op jit(solution)/shard_map/all_to_all | solution.py:90
  72.0 6.9 %all-to-all-done.4 = f32[8,16,512]{2,1,0:T(8,128)S(1)} async-done(((f32[8,16,512]{2,1,0:T(8,128)}), f32[8,16,512]{2,1,0:T(8,128)S(1)}, u32[]{:S(2)}, u32[]{:S(2)}) %all-to-all-start.4) | async-done | bytes 262176 | tf_op jit(solution)/shard_map/all_to_all | solution.py:90
  79.4 8.1 %all_to_all.87 = bf16[8,16,514]{2,1,0:T(8,128)(2,1)S(1)} all-to-all(bf16[8,16,514]{2,1,0:T(8,128)(2,1)S(1)} %broadcast_in_dim.63), channel_id=1, replica_groups=mesh['chips'=8,'cores'=2,'narrow'=8] {'narrow'}, dimensions={0} | all-to-all | bytes 263168 | tf_op jit(solution)/shard_map/all_to_all | solution.py:63
  88.1 4.2 %fusion.13 = bf16[2,128,3584]{2,1,0:T(8,128)(2,1)S(1)} fusion(bf16[512,2,3584]{2,1,0:T(2,128)(2,1)} %param.14, bf16[8,8,512]{2,1,0:T(8,128)(2,1)S(1)} %get-tuple-element.31, bf16[8,8,512]{2,1,0:T(8,128)(2,1)S(1)} %get-tuple-element.30), kind=kOutput, calls=%fused_computation.7 | convolution fusion | flops 940703744 | bytes 9306112 | tf_op jit(solution)/shard_map/rd,dkh->krh/dot_general | solution.py:328
  93.4 2.5 collective-permute-start.2
  101.0 17.4 %all_to_all.88 = bf16[2,8,8,3585]{3,2,0,1:T(8,128)(2,1)S(1)} all-to-all(bf16[2,8,8,3585]{3,2,0,1:T(8,128)(2,1)S(1)} %copy.249), channel_id=1, replica_groups=mesh['chips'=8,'cores'=2,'narrow'=8] {'chips'}, dimensions={1} | all-to-all | bytes 1835520 | tf_op jit(solution)/shard_map/all_to_all | solution.py:45
  118.8 11.7 %all_to_all.89 = bf16[8,8,3584]{2,1,0:T(8,128)(2,1)S(1)} all-to-all(bf16[8,8,3584]{2,1,0:T(8,128)(2,1)S(1)} %broadcast_in_dim.67), channel_id=1, replica_groups=mesh['chips'=8,'cores'=2,'narrow'=8] {'chips'}, dimensions={0} | all-to-all | bytes 917504 | tf_op jit(solution)/shard_map/all_to_all | solution.py:51
  130.5 3.0 %collective-permute-start.3 = (bf16[8,8,3584]{2,1,0:T(8,128)(2,1)S(1)}, bf16[8,8,3584]{2,1,0:T(8,128)(2,1)S(1)}, u32[]{:S(2)}, u32[]{:S(2)}) collective-permute-start(bf16[8,8,3584]{2,1,0:T(8,128)(2,1)S(1)} %all_to_all.89), channel_id=1, source_target_pairs={{0,8},{8,0},{1,9},{9,1},{2,10},{10,2},{3,11},{11,3},{4,12},{12,4},... | collective-permute-start | bytes 1376264 | tf_op jit(solution)/shard_map/ppermute | solution.py:29
  135.6 9.0 %all_to_all.90 = f32[8,16,512]{2,1,0:T(8,128)S(1)} all-to-all(f32[8,16,512]{2,1,0:T(8,128)S(1)} %fusion.18), channel_id=1, replica_groups=mesh['chips'=8,'cores'=2,'narrow'=8] {'narrow'}, dimensions={0} | all-to-all | bytes 524288 | tf_op jit(solution)/shard_map/all_to_all | solution.py:90
  145.1 8.5 %all_to_all.91 = bf16[8,16,514]{2,1,0:T(8,128)(2,1)S(1)} all-to-all(bf16[8,16,514]{2,1,0:T(8,128)(2,1)S(1)} %broadcast_in_dim.68), channel_id=1, replica_groups=mesh['chips'=8,'cores'=2,'narrow'=8] {'narrow'}, dimensions={0} | all-to-all | bytes 263168 | tf_op jit(solution)/shard_map/all_to_all | solution.py:63
  154.0 2.6 collective-permute-start.4
  158.0 11.6 %all_to_all.92 = f32[8,8,1281]{2,1,0:T(8,128)S(1)} all-to-all(f32[8,8,1281]{2,1,0:T(8,128)S(1)} %fusion.42), channel_id=1, replica_groups=mesh['chips'=8,'cores'=2,'narrow'=8] {'chips'}, dimensions={0} | all-to-all | bytes 655872 | tf_op jit(solution)/shard_map/all_to_all | solution.py:45
  171.9 5.2 %shard_map.105 = bf16[64,128]{1,0:T(8,128)(2,1)} custom-call(bf16[64,128]{1,0:T(8,128)(2,1)} %bitcast.194, bf16[64,128]{1,0:T(8,128)(2,1)} %broadcast_bitcast_fusion.1.kn_ref, bf16[64,128]{1,0:T(8,128)(2,1)} %broadcast_bitcast_fusion.vn_ref, s32[64,1]{1,0:T(8,128)} %broadcast_in_dim_reshape.12.lo_ref, s32[64,1]{1,0:T(8,128)} %broadcast_in_dim_reshape.13.hi_ref, ...), custom_call_target="tpu_custom_call" | custom-call | tf_op jit(solution)/shard_map/pallas_call | solution.py:230
  177.8 9.8 %all_to_all.93 = bf16[8,8,1024]{2,1,0:T(8,128)(2,1)S(1)} all-to-all(bf16[8,8,1024]{2,1,0:T(8,128)(2,1)S(1)} %broadcast_in_dim.72), channel_id=1, replica_groups=mesh['chips'=8,'cores'=2,'narrow'=8] {'chips'}, dimensions={0} | all-to-all | bytes 262144 | tf_op jit(solution)/shard_map/all_to_all | solution.py:51
  187.6 2.8 %collective-permute-start.5 = (bf16[8,8,1024]{2,1,0:T(8,128)(2,1)S(1)}, bf16[8,8,1024]{2,1,0:T(8,128)(2,1)S(1)}, u32[]{:S(2)}, u32[]{:S(2)}) collective-permute-start(bf16[8,8,1024]{2,1,0:T(8,128)(2,1)S(1)} %all_to_all.93), channel_id=1, source_target_pairs={{0,8},{8,0},{1,9},{9,1},{2,10},{10,2},{3,11},{11,3},{4,12},{12,4},... | collective-permute-start | bytes 393224 | tf_op jit(solution)/shard_map/ppermute | solution.py:29
  191.8 9.4 %all_to_all.94 = f32[8,16,512]{2,1,0:T(8,128)S(1)} all-to-all(f32[8,16,512]{2,1,0:T(8,128)S(1)} %fusion.24), channel_id=1, replica_groups=mesh['chips'=8,'cores'=2,'narrow'=8] {'narrow'}, dimensions={0} | all-to-all | bytes 524288 | tf_op jit(solution)/shard_map/all_to_all | solution.py:90
  201.6 8.1 %all_to_all.95 = bf16[8,16,514]{2,1,0:T(8,128)(2,1)S(1)} all-to-all(bf16[8,16,514]{2,1,0:T(8,128)(2,1)S(1)} %broadcast_in_dim.73), channel_id=1, replica_groups=mesh['chips'=8,'cores'=2,'narrow'=8] {'narrow'}, dimensions={0} | all-to-all | bytes 263168 | tf_op jit(solution)/shard_map/all_to_all | solution.py:63
  210.3 4.2 %fusion.10 = bf16[2,128,3584]{2,1,0:T(8,128)(2,1)S(1)} fusion(bf16[512,2,3584]{2,1,0:T(2,128)(2,1)} %param.14, bf16[8,8,512]{2,1,0:T(8,128)(2,1)S(1)} %get-tuple-element.29, bf16[8,8,512]{2,1,0:T(8,128)(2,1)S(1)} %get-tuple-element.28), kind=kOutput, calls=%fused_computation.6 | convolution fusion | flops 940703744 | bytes 9306112 | tf_op jit(solution)/shard_map/rd,dkh->krh/dot_general | solution.py:328
  215.6 2.5 collective-permute-start.6
  221.2 17.4 %all_to_all.96 = bf16[2,8,8,3585]{3,2,0,1:T(8,128)(2,1)S(1)} all-to-all(bf16[2,8,8,3585]{3,2,0,1:T(8,128)(2,1)S(1)} %copy.266), channel_id=1, replica_groups=mesh['chips'=8,'cores'=2,'narrow'=8] {'chips'}, dimensions={1} | all-to-all | bytes 1835520 | tf_op jit(solution)/shard_map/all_to_all | solution.py:45
  239.0 11.7 %all_to_all.97 = bf16[8,8,3584]{2,1,0:T(8,128)(2,1)S(1)} all-to-all(bf16[8,8,3584]{2,1,0:T(8,128)(2,1)S(1)} %broadcast_in_dim.146), channel_id=1, replica_groups=mesh['chips'=8,'cores'=2,'narrow'=8] {'chips'}, dimensions={0} | all-to-all | bytes 917504 | tf_op jit(solution)/shard_map/all_to_all | solution.py:51
  250.7 3.0 %collective-permute-start.7 = (bf16[8,8,3584]{2,1,0:T(8,128)(2,1)S(1)}, bf16[8,8,3584]{2,1,0:T(8,128)(2,1)S(1)}, u32[]{:S(2)}, u32[]{:S(2)}) collective-permute-start(bf16[8,8,3584]{2,1,0:T(8,128)(2,1)S(1)} %all_to_all.97), channel_id=1, source_target_pairs={{0,8},{8,0},{1,9},{9,1},{2,10},{10,2},{3,11},{11,3},{4,12},{12,4},... | collective-permute-start | bytes 1376264 | tf_op jit(solution)/shard_map/ppermute | solution.py:29
  256.5 3.4 %all-to-all-start.16 = ((f32[8,16,512]{2,1,0:T(8,128)}), f32[8,16,512]{2,1,0:T(8,128)S(1)}, u32[]{:S(2)}, u32[]{:S(2)}) async-start(f32[8,16,512]{2,1,0:T(8,128)} %fusion.16), calls=%async_computation.16 | async-start | bytes 524288 | tf_op jit(solution)/shard_map/all_to_all | solution.py:90
  260.6 6.3 %all-to-all-done.16 = f32[8,16,512]{2,1,0:T(8,128)S(1)} async-done(((f32[8,16,512]{2,1,0:T(8,128)}), f32[8,16,512]{2,1,0:T(8,128)S(1)}, u32[]{:S(2)}, u32[]{:S(2)}) %all-to-all-start.16) | async-done | bytes 262176 | tf_op jit(solution)/shard_map/all_to_all | solution.py:90
  (160 shorter events, 41.3 us)
Async XLA Ops:
  0.6 29.2 %copy-start = (bf16[512,1,1280]{2,0,1:T(8,128)(2,1)S(1)}, bf16[512,1,1280]{2,0,1:T(8,128)(2,1)}, u32[]{:S(2)}) copy-start(bf16[512,1,1280]{2,0,1:T(8,128)(2,1)} %param.12) | copy-start | bytes 3932164
  2.2 15.4 %all-to-all-start = ((f32[16,1,16]{2,1,0:T(1,128)}), f32[16,1,16]{2,1,0:T(1,128)S(1)}, u32[]{:S(2)}, u32[]{:S(2)}) async-start(f32[16,1,16]{2,1,0:T(1,128)} %broadcast_in_dim.55), calls=%async_computation | async-start | bytes 16384 | tf_op jit(solution)/shard_map/all_to_all | solution.py:63
  19.0 10.7 %all-to-all-start.1 = ((bf16[8,16,512]{2,1,0:T(8,128)(2,1)}), bf16[8,16,512]{2,1,0:T(8,128)(2,1)S(1)}, u32[]{:S(2)}, u32[]{:S(2)}) async-start(bf16[8,16,512]{2,1,0:T(8,128)(2,1)} %broadcast_in_dim.56), calls=%async_computation.1 | async-start | bytes 262144 | tf_op jit(solution)/shard_map/all_to_all | solution.py:63
  24.2 8.1 %copy-start.4 = (s32[8]{0:T(128)S(1)}, s32[8]{0:T(128)}, u32[]{:S(2)}) copy-start(s32[8]{0:T(128)} %param.10) | copy-start | bytes 100
  30.2 3.8 %collective-permute-start = (f32[8,8,1280]{2,1,0:T(8,128)S(1)}, f32[8,8,1280]{2,1,0:T(8,128)S(1)}, u32[]{:S(2)}, u32[]{:S(2)}) collective-permute-start(f32[8,8,1280]{2,1,0:T(8,128)S(1)} %dynamic-slice_bitcast_fusion), channel_id=1, source_target_pairs={{0,8},{8,0},{1,9},{9,1},{2,10},{10,2},{3,11},{11,3},{4,12},{12,4},... | collective-permute-start | bytes 983048 | tf_op jit(solution)/shard_map/ppermute | solution.py:29
  34.8 12.2 %all-to-all-start.2 = ((f32[8,8,1280]{2,1,0:T(8,128)}), f32[8,8,1280]{2,1,0:T(8,128)S(1)}, u32[]{:S(2)}, u32[]{:S(2)}) async-start(f32[8,8,1280]{2,1,0:T(8,128)} %bitcast_add_fusion), calls=%async_computation.2 | async-start | bytes 655360 | tf_op jit(solution)/shard_map/all_to_all | solution.py:45
  48.4 19.1 %copy-start.1 = (bf16[1024,512]{1,0:T(8,128)(2,1)S(1)}, bf16[1024,512]{1,0:T(8,128)(2,1)}, u32[]{:S(2)}) copy-start(bf16[1024,512]{1,0:T(8,128)(2,1)} %param.13) | copy-start | bytes 3145732
  53.7 18.3 %copy-start.3 = (bf16[512]{0:T(512)(128)(2,1)S(1)}, bf16[512]{0:T(512)(128)(2,1)}, u32[]{:S(2)}) copy-start(bf16[512]{0:T(512)(128)(2,1)} %param.17) | copy-start | bytes 3076
  53.7 25.3 %copy-start.2 = (bf16[16,512]{1,0:T(8,128)(2,1)S(1)}, bf16[16,512]{1,0:T(8,128)(2,1)}, u32[]{:S(2)}) copy-start(bf16[16,512]{1,0:T(8,128)(2,1)} %param.9) | copy-start | bytes 49156
  64.3 3.3 %collective-permute-start.1 = (bf16[8,8,1024]{2,1,0:T(8,128)(2,1)S(1)}, bf16[8,8,1024]{2,1,0:T(8,128)(2,1)S(1)}, u32[]{:S(2)}, u32[]{:S(2)}) collective-permute-start(bf16[8,8,1024]{2,1,0:T(8,128)(2,1)S(1)} %all_to_all.86), channel_id=1, source_target_pairs={{0,8},{8,0},{1,9},{9,1},{2,10},{10,2},{3,11},{11,3},{4,12},{12,4},... | collective-permute-start | bytes 393224 | tf_op jit(solution)/shard_map/ppermute | solution.py:29
  68.6 10.4 %all-to-all-start.4 = ((f32[8,16,512]{2,1,0:T(8,128)}), f32[8,16,512]{2,1,0:T(8,128)S(1)}, u32[]{:S(2)}, u32[]{:S(2)}) async-start(f32[8,16,512]{2,1,0:T(8,128)} %fusion.26), calls=%async_computation.4 | async-start | bytes 524288 | tf_op jit(solution)/shard_map/all_to_all | solution.py:90
  93.4 5.0 %collective-permute-start.2 = (bf16[2,8,8,3585]{3,2,1,0:T(8,128)(2,1)}, bf16[2,8,8,3585]{3,2,1,0:T(8,128)(2,1)}, u32[]{:S(2)}, u32[]{:S(2)}) collective-permute-start(bf16[2,8,8,3585]{3,2,1,0:T(8,128)(2,1)} %get-tuple-element.11), channel_id=1, source_target_pairs={{0,8},{8,0},{1,9},{9,1},{2,10},{10,2},{3,11},{11,3},{4,12},{12,4},... | collective-permute-start | bytes 2753288 | tf_op jit(solution)/shard_map/ppermute | solution.py:29
  118.3 16.6 %copy-start.5 = (bf16[3584,512]{1,0:T(8,128)(2,1)S(1)}, bf16[3584,512]{1,0:T(8,128)(2,1)}, u32[]{:S(2)}) copy-start(bf16[3584,512]{1,0:T(8,128)(2,1)} %param.15) | copy-start | bytes 11010052
  130.5 4.4 %collective-permute-start.3 = (bf16[8,8,3584]{2,1,0:T(8,128)(2,1)S(1)}, bf16[8,8,3584]{2,1,0:T(8,128)(2,1)S(1)}, u32[]{:S(2)}, u32[]{:S(2)}) collective-permute-start(bf16[8,8,3584]{2,1,0:T(8,128)(2,1)S(1)} %all_to_all.89), channel_id=1, source_target_pairs={{0,8},{8,0},{1,9},{9,1},{2,10},{10,2},{3,11},{11,3},{4,12},{12,4},... | collective-permute-start | bytes 1376264 | tf_op jit(solution)/shard_map/ppermute | solution.py:29
  154.0 3.9 %collective-permute-start.4 = (f32[8,8,1281]{2,1,0:T(8,128)S(1)}, f32[8,8,1281]{2,1,0:T(8,128)S(1)}, u32[]{:S(2)}, u32[]{:S(2)}) collective-permute-start(f32[8,8,1281]{2,1,0:T(8,128)S(1)} %fusion.39), channel_id=1, source_target_pairs={{0,8},{8,0},{1,9},{9,1},{2,10},{10,2},{3,11},{11,3},{4,12},{12,4},... | collective-permute-start | bytes 983816 | tf_op jit(solution)/shard_map/ppermute | solution.py:29
  187.6 3.8 %collective-permute-start.5 = (bf16[8,8,1024]{2,1,0:T(8,128)(2,1)S(1)}, bf16[8,8,1024]{2,1,0:T(8,128)(2,1)S(1)}, u32[]{:S(2)}, u32[]{:S(2)}) collective-permute-start(bf16[8,8,1024]{2,1,0:T(8,128)(2,1)S(1)} %all_to_all.93), channel_id=1, source_target_pairs={{0,8},{8,0},{1,9},{9,1},{2,10},{10,2},{3,11},{11,3},{4,12},{12,4},... | collective-permute-start | bytes 393224 | tf_op jit(solution)/shard_map/ppermute | solution.py:29
  215.6 4.9 %collective-permute-start.6 = (bf16[2,8,8,3585]{3,2,1,0:T(8,128)(2,1)}, bf16[2,8,8,3585]{3,2,1,0:T(8,128)(2,1)S(1)}, u32[]{:S(2)}, u32[]{:S(2)}) collective-permute-start(bf16[2,8,8,3585]{3,2,1,0:T(8,128)(2,1)} %get-tuple-element.9), channel_id=1, source_target_pairs={{0,8},{8,0},{1,9},{9,1},{2,10},{10,2},{3,11},{11,3},{4,12},{12,4},... | collective-permute-start | bytes 2753288 | tf_op jit(solution)/shard_map/ppermute | solution.py:29
  238.5 16.6 %copy-start.6 = (bf16[3584,512]{1,0:T(8,128)(2,1)S(1)}, bf16[3584,512]{1,0:T(8,128)(2,1)}, u32[]{:S(2)}) copy-start(bf16[3584,512]{1,0:T(8,128)(2,1)} %param.15) | copy-start | bytes 11010052
  250.7 4.4 %collective-permute-start.7 = (bf16[8,8,3584]{2,1,0:T(8,128)(2,1)S(1)}, bf16[8,8,3584]{2,1,0:T(8,128)(2,1)S(1)}, u32[]{:S(2)}, u32[]{:S(2)}) collective-permute-start(bf16[8,8,3584]{2,1,0:T(8,128)(2,1)S(1)} %all_to_all.97), channel_id=1, source_target_pairs={{0,8},{8,0},{1,9},{9,1},{2,10},{10,2},{3,11},{11,3},{4,12},{12,4},... | collective-permute-start | bytes 1376264 | tf_op jit(solution)/shard_map/ppermute | solution.py:29
  256.5 10.3 %all-to-all-start.16 = ((f32[8,16,512]{2,1,0:T(8,128)}), f32[8,16,512]{2,1,0:T(8,128)S(1)}, u32[]{:S(2)}, u32[]{:S(2)}) async-start(f32[8,16,512]{2,1,0:T(8,128)} %fusion.16), calls=%async_computation.16 | async-start | bytes 524288 | tf_op jit(solution)/shard_map/all_to_all | solution.py:90

commit v9 on v6

--- a/solution.py
+++ b/solution.py
@@ -55,6 +55,26 @@
     low_core = jnp.where(first, from_chips, from_partner)
     high_core = jnp.where(first, from_partner, from_chips)
     return jnp.stack([low_core, high_core], axis=1).reshape(-1, *shard.shape[1:])
+
+
+def gathered_product(shard, weight):
+    chips = lax.axis_size(CHIPS)
+    from_chips = lax.all_to_all(
+        jnp.broadcast_to(shard[None], (chips, *shard.shape)), CHIPS, 0, 0, tiled=True
+    )
+    from_partner = swap_cores(from_chips)
+    mine = jnp.dot(
+        from_chips.reshape(-1, shard.shape[1]), weight, preferred_element_type=jnp.float32
+    )
+    other = jnp.dot(
+        from_partner.reshape(-1, shard.shape[1]), weight, preferred_element_type=jnp.float32
+    )
+    mine = mine.reshape(chips, -1, weight.shape[1])
+    other = other.reshape(chips, -1, weight.shape[1])
+    first = lax.axis_index(CORES) == 0
+    low_core = jnp.where(first, mine, other)
+    high_core = jnp.where(first, other, mine)
+    return jnp.stack([low_core, high_core], axis=1).reshape(-1, weight.shape[1])
 
 
 def copy_for_each(shard, axis):
@@ -245,10 +265,7 @@
         attended = attend(
             queries, key_new, value_new, kv_cache[layer_index, 0], kv_cache[layer_index, 1], lengths
         )
-        heads_all = gathered_rows_wide(attended)
-        summed = summed_on_arrival(
-            jnp.dot(heads_all, o_weight, preferred_element_type=jnp.float32), "narrow", 0
-        )
+        summed = summed_on_arrival(gathered_product(attended, o_weight), "narrow", 0)
         stream = (stream.astype(jnp.float32) + summed).astype(jnp.bfloat16)
         rows_in, partial_sum = gathered_rows(stream, mlp_gain)
         chips = lax.axis_size(CHIPS)
@@ -297,9 +314,7 @@
         gate = own[0, :, :hidden_dev] * scale
         up = own[1, :, :hidden_dev] * scale
         activated = (jax.nn.silu(gate) * up).astype(jnp.bfloat16)
-        partial_down = jnp.dot(
-            gathered_rows_wide(activated), down_weight, preferred_element_type=jnp.float32
-        )
+        partial_down = gathered_product(activated, down_weight)
         summed = summed_on_arrival(partial_down, "narrow", 0)
         stream = (stream.astype(jnp.float32) + summed).astype(jnp.bfloat16)
     return (stream, jnp.stack(entries))

time: 265 us -> 267 us (level)
  blocking collectives: 132 us -> 123 us
  waiting for transfers between devices: 43.8 us -> 48.4 us
  starting transfers between devices: 44.9 us -> 47.9 us
    all_to_all x4 -> x3, blocking collectives: 42.5 us -> 32.9 us  [gathered_product(): lax.all_to_all(jnp.broadcast_to(shard[None], (chips, *shard.shape)), CHIP...]
    all_to_all x0 -> x1, waiting for transfers between devices: none -> 6.69 us  [gathered_product(): lax.all_to_all(jnp.broadcast_to(shard[None], (chips, *shard.shape)), CHIP...]
    all_to_all x0 -> x1, starting transfers between devices: none -> 3.37 us  [gathered_product(): lax.all_to_all(jnp.broadcast_to(shard[None], (chips, *shard.shape)), CHIP...]
  transfers between devices with their start and end apart: 13 -> 14, of which waited for: 13 -> 14; matrix products, arithmetic and copies ran while one was open for 1% -> 2% of each run, Pallas kernels for 0% -> 0%
where the time goes in v9:
time: 267 us; the launch traced here: 265 us
  blocking collectives  123 us (46%)
  waiting for transfers between devices  48.4 us (18%)
  starting transfers between devices  47.9 us (18%)
  matrix products  23.8 us (9%)
  other arithmetic  15.5 us (6%)
  local copies, waits for them, and re-layouts  5.5 us (2%)
    all_to_all x3, blocking collectives, chip_sum(): lax.all_to_all(pair_sum.astype(wire_type), CHIPS, row_dim, row_dim, tiled...  46.8 us
    all_to_all x3, blocking collectives, gathered_product(): lax.all_to_all(jnp.broadcast_to(shard[None], (chips, *shard.shape)), CHIP...  32.9 us
    all_to_all x3, blocking collectives, copy_for_each(): lax.all_to_all(jnp.broadcast_to(shard[None], (length, *shard.shape)), axi...  24.6 us
    ppermute x8, starting transfers between devices, swap_cores(): return lax.ppermute(shard, CORES, [(0, 1), (1, 0)])  20.7 us
    all_to_all x2, blocking collectives, summed_on_arrival(): lax.all_to_all(parts, axis, split_axis=0, concat_axis=0, tiled=True)  18.4 us
    all_to_all x2, starting transfers between devices, copy_for_each(): lax.all_to_all(jnp.broadcast_to(shard[None], (length, *shard.shape)), axi...  13.6 us
    all_to_all x2, waiting for transfers between devices, summed_on_arrival(): lax.all_to_all(parts, axis, split_axis=0, concat_axis=0, tiled=True)  13.2 us
    all_to_all x2, waiting for transfers between devices, copy_for_each(): lax.all_to_all(jnp.broadcast_to(shard[None], (length, *shard.shape)), axi...  10.3 us
  transfers between devices with their start and end apart: 14, of which 14 were waited for; matrix products, arithmetic and copies ran while one was open for 2% of the time, Pallas kernels for 0%

profile of v9, /device:TPU:1, one launch (start us, length us, event | category | flops | bytes accessed | tf_op | source)
XLA Modules:
  0.0 265.2 jit_solution(7416075259174987323)
XLA Ops:
  2.2 8.4 %all-to-all-start = ((f32[16,1,16]{2,1,0:T(1,128)}), f32[16,1,16]{2,1,0:T(1,128)S(1)}, u32[]{:S(2)}, u32[]{:S(2)}) async-start(f32[16,1,16]{2,1,0:T(1,128)} %broadcast_in_dim.60), calls=%async_computation | async-start | bytes 16384 | tf_op jit(solution)/shard_map/all_to_all | solution.py:82
  12.1 5.4 %all-to-all-done = f32[16,1,16]{2,1,0:T(1,128)S(1)} async-done(((f32[16,1,16]{2,1,0:T(1,128)}), f32[16,1,16]{2,1,0:T(1,128)S(1)}, u32[]{:S(2)}, u32[]{:S(2)}) %all-to-all-start) | async-done | bytes 1056 | tf_op jit(solution)/shard_map/all_to_all | solution.py:82
  19.0 5.1 %all-to-all-start.1 = ((bf16[8,16,512]{2,1,0:T(8,128)(2,1)}), bf16[8,16,512]{2,1,0:T(8,128)(2,1)S(1)}, u32[]{:S(2)}, u32[]{:S(2)}) async-start(bf16[8,16,512]{2,1,0:T(8,128)(2,1)} %broadcast_in_dim.61), calls=%async_computation.1 | async-start | bytes 262144 | tf_op jit(solution)/shard_map/all_to_all | solution.py:82
  24.9 4.8 %all-to-all-done.1 = bf16[8,16,512]{2,1,0:T(8,128)(2,1)S(1)} async-done(((bf16[8,16,512]{2,1,0:T(8,128)(2,1)}), bf16[8,16,512]{2,1,0:T(8,128)(2,1)S(1)}, u32[]{:S(2)}, u32[]{:S(2)}) %all-to-all-start.1) | async-done | bytes 131104 | tf_op jit(solution)/shard_map/all_to_all | solution.py:82
  34.3 3.4 %all-to-all-start.2 = ((f32[8,8,1280]{2,1,0:T(8,128)}), f32[8,8,1280]{2,1,0:T(8,128)S(1)}, u32[]{:S(2)}, u32[]{:S(2)}) async-start(f32[8,8,1280]{2,1,0:T(8,128)} %bitcast_add_fusion), calls=%async_computation.2 | async-start | bytes 655360 | tf_op jit(solution)/shard_map/all_to_all | solution.py:44
  37.9 8.7 %all-to-all-done.2 = f32[8,8,1280]{2,1,0:T(8,128)S(1)} async-done(((f32[8,8,1280]{2,1,0:T(8,128)}), f32[8,8,1280]{2,1,0:T(8,128)S(1)}, u32[]{:S(2)}, u32[]{:S(2)}) %all-to-all-start.2) | async-done | bytes 327712 | tf_op jit(solution)/shard_map/all_to_all | solution.py:44
  47.1 2.7 %fusion.186 = (f32[8,8]{1,0:T(8,128)S(1)}, f32[8,8,9536]{2,1,0:T(8,128)S(1)}) fusion(bf16[8,8,128]{2,1,0:T(8,128)(2,1)S(1)} %fusion.141, bf16[2,2,9536,128]{3,2,1,0:T(8,128)(2,1)} %param.11, pred[8,9536]{1,0:T(8,128)(4,1)S(1)} %fusion.107), kind=kOutput, calls=%fused_computation.272 | convolution fusion | flops 158068672 | bytes 4975360 | tf_op jit(solution)/shard_map/rkgd,tkd->krgt/dot_general | solution.py:180
  53.5 3.4 %all-to-all-start.3 = ((bf16[8,8,1024]{2,1,0:T(8,128)(2,1)}), bf16[8,8,1024]{2,1,0:T(8,128)(2,1)S(1)}, u32[]{:S(2)}, u32[]{:S(2)}) async-start(bf16[8,8,1024]{2,1,0:T(8,128)(2,1)} %broadcast_in_dim.64), calls=%async_computation.3 | async-start | bytes 262144 | tf_op jit(solution)/shard_map/all_to_all | solution.py:62
  56.9 6.7 %all-to-all-done.3 = bf16[8,8,1024]{2,1,0:T(8,128)(2,1)S(1)} async-done(((bf16[8,8,1024]{2,1,0:T(8,128)(2,1)}), bf16[8,8,1024]{2,1,0:T(8,128)(2,1)S(1)}, u32[]{:S(2)}, u32[]{:S(2)}) %all-to-all-start.3) | async-done | bytes 131104 | tf_op jit(solution)/shard_map/all_to_all | solution.py:62
  67.8 3.4 %all-to-all-start.4 = ((f32[8,16,512]{2,1,0:T(8,128)}), f32[8,16,512]{2,1,0:T(8,128)S(1)}, u32[]{:S(2)}, u32[]{:S(2)}) async-start(f32[8,16,512]{2,1,0:T(8,128)} %copy_bitcast_fusion.3), calls=%async_computation.4 | async-start | bytes 524288 | tf_op jit(solution)/shard_map/all_to_all | solution.py:109
  71.3 6.9 %all-to-all-done.4 = f32[8,16,512]{2,1,0:T(8,128)S(1)} async-done(((f32[8,16,512]{2,1,0:T(8,128)}), f32[8,16,512]{2,1,0:T(8,128)S(1)}, u32[]{:S(2)}, u32[]{:S(2)}) %all-to-all-start.4) | async-done | bytes 262176 | tf_op jit(solution)/shard_map/all_to_all | solution.py:109
  78.7 8.1 %all_to_all.86 = bf16[8,16,514]{2,1,0:T(8,128)(2,1)S(1)} all-to-all(bf16[8,16,514]{2,1,0:T(8,128)(2,1)S(1)} %broadcast_in_dim.65), channel_id=1, replica_groups=mesh['chips'=8,'cores'=2,'narrow'=8] {'narrow'}, dimensions={0} | all-to-all | bytes 263168 | tf_op jit(solution)/shard_map/all_to_all | solution.py:82
  87.4 4.2 %fusion.15 = bf16[2,128,3584]{2,1,0:T(8,128)(2,1)S(1)} fusion(bf16[512,2,3584]{2,1,0:T(2,128)(2,1)} %param.14, bf16[8,8,512]{2,1,0:T(8,128)(2,1)S(1)} %get-tuple-element.31, bf16[8,8,512]{2,1,0:T(8,128)(2,1)S(1)} %get-tuple-element.30), kind=kOutput, calls=%fused_computation.11 | convolution fusion | flops 940703744 | bytes 9306112 | tf_op jit(solution)/shard_map/rd,dkh->krh/dot_general | solution.py:287
  100.2 17.6 %all_to_all.87 = bf16[2,8,8,3585]{3,2,0,1:T(8,128)(2,1)S(1)} all-to-all(bf16[2,8,8,3585]{3,2,0,1:T(8,128)(2,1)S(1)} %copy.260), channel_id=1, replica_groups=mesh['chips'=8,'cores'=2,'narrow'=8] {'chips'}, dimensions={1} | all-to-all | bytes 1835520 | tf_op jit(solution)/shard_map/all_to_all | solution.py:44
  118.3 11.6 %all_to_all.88 = bf16[8,8,3584]{2,1,0:T(8,128)(2,1)S(1)} all-to-all(bf16[8,8,3584]{2,1,0:T(8,128)(2,1)S(1)} %broadcast_in_dim.69), channel_id=1, replica_groups=mesh['chips'=8,'cores'=2,'narrow'=8] {'chips'}, dimensions={0} | all-to-all | bytes 917504 | tf_op jit(solution)/shard_map/all_to_all | solution.py:62
  129.9 3.0 %collective-permute-start.3 = (bf16[8,8,3584]{2,1,0:T(8,128)(2,1)S(1)}, bf16[8,8,3584]{2,1,0:T(8,128)(2,1)S(1)}, u32[]{:S(2)}, u32[]{:S(2)}) collective-permute-start(bf16[8,8,3584]{2,1,0:T(8,128)(2,1)S(1)} %all_to_all.88), channel_id=1, source_target_pairs={{0,8},{8,0},{1,9},{9,1},{2,10},{10,2},{3,11},{11,3},{4,12},{12,4},... | collective-permute-start | bytes 1376264 | tf_op jit(solution)/shard_map/ppermute | solution.py:28
  135.0 9.0 %all_to_all.89 = f32[8,16,512]{2,1,0:T(8,128)S(1)} all-to-all(f32[8,16,512]{2,1,0:T(8,128)S(1)} %copy_bitcast_fusion.2), channel_id=1, replica_groups=mesh['chips'=8,'cores'=2,'narrow'=8] {'narrow'}, dimensions={0} | all-to-all | bytes 524288 | tf_op jit(solution)/shard_map/all_to_all | solution.py:109
  144.5 8.5 %all_to_all.90 = bf16[8,16,514]{2,1,0:T(8,128)(2,1)S(1)} all-to-all(bf16[8,16,514]{2,1,0:T(8,128)(2,1)S(1)} %broadcast_in_dim.70), channel_id=1, replica_groups=mesh['chips'=8,'cores'=2,'narrow'=8] {'narrow'}, dimensions={0} | all-to-all | bytes 263168 | tf_op jit(solution)/shard_map/all_to_all | solution.py:82
  153.5 2.6 collective-permute-start.4
  157.4 11.6 %all_to_all.91 = f32[8,8,1281]{2,1,0:T(8,128)S(1)} all-to-all(f32[8,8,1281]{2,1,0:T(8,128)S(1)} %fusion.106), channel_id=1, replica_groups=mesh['chips'=8,'cores'=2,'narrow'=8] {'chips'}, dimensions={0} | all-to-all | bytes 655872 | tf_op jit(solution)/shard_map/all_to_all | solution.py:44
  169.5 2.7 %fusion.187 = (f32[8,8]{1,0:T(8,128)S(1)}, f32[8,8,9536]{2,1,0:T(8,128)S(1)}) fusion(bf16[8,8,128]{2,1,0:T(8,128)(2,1)S(1)} %fusion.142, bf16[2,2,9536,128]{3,2,1,0:T(8,128)(2,1)} %param.11, pred[8,9536]{1,0:T(8,128)(4,1)S(1)} %fusion.107), kind=kOutput, calls=%fused_computation.273 | convolution fusion | flops 158068672 | bytes 4975360 | tf_op jit(solution)/shard_map/rkgd,tkd->krgt/dot_general | solution.py:180
  175.4 9.8 %all_to_all.92 = bf16[8,8,1024]{2,1,0:T(8,128)(2,1)S(1)} all-to-all(bf16[8,8,1024]{2,1,0:T(8,128)(2,1)S(1)} %broadcast_in_dim.72), channel_id=1, replica_groups=mesh['chips'=8,'cores'=2,'narrow'=8] {'chips'}, dimensions={0} | all-to-all | bytes 262144 | tf_op jit(solution)/shard_map/all_to_all | solution.py:62
  185.1 2.8 %collective-permute-start.5 = (bf16[8,8,1024]{2,1,0:T(8,128)(2,1)S(1)}, bf16[8,8,1024]{2,1,0:T(8,128)(2,1)S(1)}, u32[]{:S(2)}, u32[]{:S(2)}) collective-permute-start(bf16[8,8,1024]{2,1,0:T(8,128)(2,1)S(1)} %all_to_all.92), channel_id=1, source_target_pairs={{0,8},{8,0},{1,9},{9,1},{2,10},{10,2},{3,11},{11,3},{4,12},{12,4},... | collective-permute-start | bytes 393224 | tf_op jit(solution)/shard_map/ppermute | solution.py:28
  189.3 9.4 %all_to_all.93 = f32[8,16,512]{2,1,0:T(8,128)S(1)} all-to-all(f32[8,16,512]{2,1,0:T(8,128)S(1)} %copy_bitcast_fusion.1), channel_id=1, replica_groups=mesh['chips'=8,'cores'=2,'narrow'=8] {'narrow'}, dimensions={0} | all-to-all | bytes 524288 | tf_op jit(solution)/shard_map/all_to_all | solution.py:109
  199.2 8.1 %all_to_all.94 = bf16[8,16,514]{2,1,0:T(8,128)(2,1)S(1)} all-to-all(bf16[8,16,514]{2,1,0:T(8,128)(2,1)S(1)} %broadcast_in_dim.73), channel_id=1, replica_groups=mesh['chips'=8,'cores'=2,'narrow'=8] {'narrow'}, dimensions={0} | all-to-all | bytes 263168 | tf_op jit(solution)/shard_map/all_to_all | solution.py:82
  207.9 4.2 %fusion.12 = bf16[2,128,3584]{2,1,0:T(8,128)(2,1)S(1)} fusion(bf16[512,2,3584]{2,1,0:T(2,128)(2,1)} %param.14, bf16[8,8,512]{2,1,0:T(8,128)(2,1)S(1)} %get-tuple-element.29, bf16[8,8,512]{2,1,0:T(8,128)(2,1)S(1)} %get-tuple-element.28), kind=kOutput, calls=%fused_computation.10 | convolution fusion | flops 940703744 | bytes 9306112 | tf_op jit(solution)/shard_map/rd,dkh->krh/dot_general | solution.py:287
  213.2 2.5 collective-permute-start.6
  218.7 17.6 %all_to_all.95 = bf16[2,8,8,3585]{3,2,0,1:T(8,128)(2,1)S(1)} all-to-all(bf16[2,8,8,3585]{3,2,0,1:T(8,128)(2,1)S(1)} %copy.276), channel_id=1, replica_groups=mesh['chips'=8,'cores'=2,'narrow'=8] {'chips'}, dimensions={1} | all-to-all | bytes 1835520 | tf_op jit(solution)/shard_map/all_to_all | solution.py:44
  236.8 11.6 %all_to_all.96 = bf16[8,8,3584]{2,1,0:T(8,128)(2,1)S(1)} all-to-all(bf16[8,8,3584]{2,1,0:T(8,128)(2,1)S(1)} %broadcast_in_dim.77), channel_id=1, replica_groups=mesh['chips'=8,'cores'=2,'narrow'=8] {'chips'}, dimensions={0} | all-to-all | bytes 917504 | tf_op jit(solution)/shard_map/all_to_all | solution.py:62
  248.4 3.0 %collective-permute-start.7 = (bf16[8,8,3584]{2,1,0:T(8,128)(2,1)S(1)}, bf16[8,8,3584]{2,1,0:T(8,128)(2,1)S(1)}, u32[]{:S(2)}, u32[]{:S(2)}) collective-permute-start(bf16[8,8,3584]{2,1,0:T(8,128)(2,1)S(1)} %all_to_all.96), channel_id=1, source_target_pairs={{0,8},{8,0},{1,9},{9,1},{2,10},{10,2},{3,11},{11,3},{4,12},{12,4},... | collective-permute-start | bytes 1376264 | tf_op jit(solution)/shard_map/ppermute | solution.py:28
  254.2 3.4 %all-to-all-start.16 = ((f32[8,16,512]{2,1,0:T(8,128)}), f32[8,16,512]{2,1,0:T(8,128)S(1)}, u32[]{:S(2)}, u32[]{:S(2)}) async-start(f32[8,16,512]{2,1,0:T(8,128)} %copy_bitcast_fusion), calls=%async_computation.16 | async-start | bytes 524288 | tf_op jit(solution)/shard_map/all_to_all | solution.py:109
  258.3 6.3 %all-to-all-done.16 = f32[8,16,512]{2,1,0:T(8,128)S(1)} async-done(((f32[8,16,512]{2,1,0:T(8,128)}), f32[8,16,512]{2,1,0:T(8,128)S(1)}, u32[]{:S(2)}, u32[]{:S(2)}) %all-to-all-start.16) | async-done | bytes 262176 | tf_op jit(solution)/shard_map/all_to_all | solution.py:109
  (170 shorter events, 47.2 us)
Async XLA Ops:
  0.6 29.1 %copy-start = (bf16[512,1,1280]{2,0,1:T(8,128)(2,1)S(1)}, bf16[512,1,1280]{2,0,1:T(8,128)(2,1)}, u32[]{:S(2)}) copy-start(bf16[512,1,1280]{2,0,1:T(8,128)(2,1)} %param.12) | copy-start | bytes 3932164
  2.2 15.4 %all-to-all-start = ((f32[16,1,16]{2,1,0:T(1,128)}), f32[16,1,16]{2,1,0:T(1,128)S(1)}, u32[]{:S(2)}, u32[]{:S(2)}) async-start(f32[16,1,16]{2,1,0:T(1,128)} %broadcast_in_dim.60), calls=%async_computation | async-start | bytes 16384 | tf_op jit(solution)/shard_map/all_to_all | solution.py:82
  19.0 10.7 %all-to-all-start.1 = ((bf16[8,16,512]{2,1,0:T(8,128)(2,1)}), bf16[8,16,512]{2,1,0:T(8,128)(2,1)S(1)}, u32[]{:S(2)}, u32[]{:S(2)}) async-start(bf16[8,16,512]{2,1,0:T(8,128)(2,1)} %broadcast_in_dim.61), calls=%async_computation.1 | async-start | bytes 262144 | tf_op jit(solution)/shard_map/all_to_all | solution.py:82
  30.2 3.4 %collective-permute-start = (f32[8,8,1280]{2,1,0:T(8,128)S(1)}, f32[8,8,1280]{2,1,0:T(8,128)S(1)}, u32[]{:S(2)}, u32[]{:S(2)}) collective-permute-start(f32[8,8,1280]{2,1,0:T(8,128)S(1)} %dynamic-slice_bitcast_fusion), channel_id=1, source_target_pairs={{0,8},{8,0},{1,9},{9,1},{2,10},{10,2},{3,11},{11,3},{4,12},{12,4},... | collective-permute-start | bytes 983048 | tf_op jit(solution)/shard_map/ppermute | solution.py:28
  34.3 12.3 %all-to-all-start.2 = ((f32[8,8,1280]{2,1,0:T(8,128)}), f32[8,8,1280]{2,1,0:T(8,128)S(1)}, u32[]{:S(2)}, u32[]{:S(2)}) async-start(f32[8,8,1280]{2,1,0:T(8,128)} %bitcast_add_fusion), calls=%async_computation.2 | async-start | bytes 655360 | tf_op jit(solution)/shard_map/all_to_all | solution.py:44
  50.4 15.4 %copy-start.3 = (bf16[1024,512]{1,0:T(8,128)(2,1)S(1)}, bf16[1024,512]{1,0:T(8,128)(2,1)}, u32[]{:S(2)}) copy-start(bf16[1024,512]{1,0:T(8,128)(2,1)} %param.13) | copy-start | bytes 3145732
  52.8 18.4 %copy-start.5 = (bf16[512]{0:T(512)(128)(2,1)S(1)}, bf16[512]{0:T(512)(128)(2,1)}, u32[]{:S(2)}) copy-start(bf16[512]{0:T(512)(128)(2,1)} %param.17) | copy-start | bytes 3076
  52.9 25.4 %copy-start.4 = (bf16[16,512]{1,0:T(8,128)(2,1)S(1)}, bf16[16,512]{1,0:T(8,128)(2,1)}, u32[]{:S(2)}) copy-start(bf16[16,512]{1,0:T(8,128)(2,1)} %param.9) | copy-start | bytes 49156
  53.5 10.1 %all-to-all-start.3 = ((bf16[8,8,1024]{2,1,0:T(8,128)(2,1)}), bf16[8,8,1024]{2,1,0:T(8,128)(2,1)S(1)}, u32[]{:S(2)}, u32[]{:S(2)}) async-start(bf16[8,8,1024]{2,1,0:T(8,128)(2,1)} %broadcast_in_dim.64), calls=%async_computation.3 | async-start | bytes 262144 | tf_op jit(solution)/shard_map/all_to_all | solution.py:62
  63.6 3.2 %collective-permute-start.1 = (bf16[8,8,1024]{2,1,0:T(8,128)(2,1)S(1)}, bf16[8,8,1024]{2,1,0:T(8,128)(2,1)S(1)}, u32[]{:S(2)}, u32[]{:S(2)}) collective-permute-start(bf16[8,8,1024]{2,1,0:T(8,128)(2,1)S(1)} %all-to-all-done.3), channel_id=1, source_target_pairs={{0,8},{8,0},{1,9},{9,1},{2,10},{10,2},{3,11},{11,3},{4,12},{12,4},... | collective-permute-start | bytes 393224 | tf_op jit(solution)/shard_map/ppermute | solution.py:28
  67.8 10.4 %all-to-all-start.4 = ((f32[8,16,512]{2,1,0:T(8,128)}), f32[8,16,512]{2,1,0:T(8,128)S(1)}, u32[]{:S(2)}, u32[]{:S(2)}) async-start(f32[8,16,512]{2,1,0:T(8,128)} %copy_bitcast_fusion.3), calls=%async_computation.4 | async-start | bytes 524288 | tf_op jit(solution)/shard_map/all_to_all | solution.py:109
  92.7 5.0 %collective-permute-start.2 = (bf16[2,8,8,3585]{3,2,1,0:T(8,128)(2,1)}, bf16[2,8,8,3585]{3,2,1,0:T(8,128)(2,1)}, u32[]{:S(2)}, u32[]{:S(2)}) collective-permute-start(bf16[2,8,8,3585]{3,2,1,0:T(8,128)(2,1)} %get-tuple-element.11), channel_id=1, source_target_pairs={{0,8},{8,0},{1,9},{9,1},{2,10},{10,2},{3,11},{11,3},{4,12},{12,4},... | collective-permute-start | bytes 2753288 | tf_op jit(solution)/shard_map/ppermute | solution.py:28
  100.2 32.6 %copy-start.1 = (bf16[3584,512]{1,0:T(8,128)(2,1)S(1)}, bf16[3584,512]{1,0:T(8,128)(2,1)}, u32[]{:S(2)}) copy-start(bf16[3584,512]{1,0:T(8,128)(2,1)} %param.15) | copy-start | bytes 11010052
  129.9 4.4 %collective-permute-start.3 = (bf16[8,8,3584]{2,1,0:T(8,128)(2,1)S(1)}, bf16[8,8,3584]{2,1,0:T(8,128)(2,1)S(1)}, u32[]{:S(2)}, u32[]{:S(2)}) collective-permute-start(bf16[8,8,3584]{2,1,0:T(8,128)(2,1)S(1)} %all_to_all.88), channel_id=1, source_target_pairs={{0,8},{8,0},{1,9},{9,1},{2,10},{10,2},{3,11},{11,3},{4,12},{12,4},... | collective-permute-start | bytes 1376264 | tf_op jit(solution)/shard_map/ppermute | solution.py:28
  153.5 3.9 %collective-permute-start.4 = (f32[8,8,1281]{2,1,0:T(8,128)S(1)}, f32[8,8,1281]{2,1,0:T(8,128)S(1)}, u32[]{:S(2)}, u32[]{:S(2)}) collective-permute-start(f32[8,8,1281]{2,1,0:T(8,128)S(1)} %fusion.103), channel_id=1, source_target_pairs={{0,8},{8,0},{1,9},{9,1},{2,10},{10,2},{3,11},{11,3},{4,12},{12,4},... | collective-permute-start | bytes 983816 | tf_op jit(solution)/shard_map/ppermute | solution.py:28
  185.1 3.8 %collective-permute-start.5 = (bf16[8,8,1024]{2,1,0:T(8,128)(2,1)S(1)}, bf16[8,8,1024]{2,1,0:T(8,128)(2,1)S(1)}, u32[]{:S(2)}, u32[]{:S(2)}) collective-permute-start(bf16[8,8,1024]{2,1,0:T(8,128)(2,1)S(1)} %all_to_all.92), channel_id=1, source_target_pairs={{0,8},{8,0},{1,9},{9,1},{2,10},{10,2},{3,11},{11,3},{4,12},{12,4},... | collective-permute-start | bytes 393224 | tf_op jit(solution)/shard_map/ppermute | solution.py:28
  213.2 4.9 %collective-permute-start.6 = (bf16[2,8,8,3585]{3,2,1,0:T(8,128)(2,1)}, bf16[2,8,8,3585]{3,2,1,0:T(8,128)(2,1)S(1)}, u32[]{:S(2)}, u32[]{:S(2)}) collective-permute-start(bf16[2,8,8,3585]{3,2,1,0:T(8,128)(2,1)} %get-tuple-element.9), channel_id=1, source_target_pairs={{0,8},{8,0},{1,9},{9,1},{2,10},{10,2},{3,11},{11,3},{4,12},{12,4},... | collective-permute-start | bytes 2753288 | tf_op jit(solution)/shard_map/ppermute | solution.py:28
  218.7 32.6 %copy-start.2 = (bf16[3584,512]{1,0:T(8,128)(2,1)S(1)}, bf16[3584,512]{1,0:T(8,128)(2,1)}, u32[]{:S(2)}) copy-start(bf16[3584,512]{1,0:T(8,128)(2,1)} %param.15) | copy-start | bytes 11010052
  248.4 4.4 %collective-permute-start.7 = (bf16[8,8,3584]{2,1,0:T(8,128)(2,1)S(1)}, bf16[8,8,3584]{2,1,0:T(8,128)(2,1)S(1)}, u32[]{:S(2)}, u32[]{:S(2)}) collective-permute-start(bf16[8,8,3584]{2,1,0:T(8,128)(2,1)S(1)} %all_to_all.96), channel_id=1, source_target_pairs={{0,8},{8,0},{1,9},{9,1},{2,10},{10,2},{3,11},{11,3},{4,12},{12,4},... | collective-permute-start | bytes 1376264 | tf_op jit(solution)/shard_map/ppermute | solution.py:28
  254.2 10.4 %all-to-all-start.16 = ((f32[8,16,512]{2,1,0:T(8,128)}), f32[8,16,512]{2,1,0:T(8,128)S(1)}, u32[]{:S(2)}, u32[]{:S(2)}) async-start(f32[8,16,512]{2,1,0:T(8,128)} %copy_bitcast_fusion), calls=%async_computation.16 | async-start | bytes 524288 | tf_op jit(solution)/shard_map/all_to_all | solution.py:109

commit v10 on v6

--- a/solution.py
+++ b/solution.py
@@ -245,7 +245,7 @@
         attended = attend(
             queries, key_new, value_new, kv_cache[layer_index, 0], kv_cache[layer_index, 1], lengths
         )
-        heads_all = gathered_rows_wide(attended)
+        heads_all = gathered_copies(attended, WIDE, 0)
         summed = summed_on_arrival(
             jnp.dot(heads_all, o_weight, preferred_element_type=jnp.float32), "narrow", 0
         )

time: 265 us -> 267 us (level)
  blocking collectives: 132 us -> 139 us
  starting transfers between devices: 44.9 us -> 39.4 us
    all_to_all x3 -> x5, blocking collectives: 24.6 us -> 50.9 us  [copy_for_each(): lax.all_to_all(jnp.broadcast_to(shard[None], (length, *shard.shape)), axi...]
    all_to_all x4 -> x2, blocking collectives: 42.5 us -> 23.3 us  [gathered_rows_wide(): lax.all_to_all(jnp.broadcast_to(shard[None], (chips, *shard.shape)), CHIP...]
    ppermute x8 -> x6, starting transfers between devices: 21.1 us -> 15.5 us  [swap_cores(): return lax.ppermute(shard, CORES, [(0, 1), (1, 0)])]
    ppermute x8 -> x6, waiting for transfers between devices: 11.6 us -> 9.61 us  [swap_cores(): return lax.ppermute(shard, CORES, [(0, 1), (1, 0)])]
  transfers between devices with their start and end apart: 13 -> 11, of which waited for: 13 -> 11; matrix products, arithmetic and copies ran while one was open for 1% -> 1% of each run, Pallas kernels for 0% -> 0%
where the time goes in v10:
time: 267 us; the launch traced here: 266 us
  blocking collectives  139 us (52%)
  waiting for transfers between devices  41.8 us (16%)
  starting transfers between devices  39.4 us (15%)
  matrix products  25 us (9%)
  other arithmetic  14.2 us (5%)
  local copies, waits for them, and re-layouts  4.87 us (2%)
    all_to_all x5, blocking collectives, copy_for_each(): lax.all_to_all(jnp.broadcast_to(shard[None], (length, *shard.shape)), axi...  50.9 us
    all_to_all x3, blocking collectives, chip_sum(): lax.all_to_all(pair_sum.astype(wire_type), CHIPS, row_dim, row_dim, tiled...  46.6 us
    all_to_all x2, blocking collectives, gathered_rows_wide(): lax.all_to_all(jnp.broadcast_to(shard[None], (chips, *shard.shape)), CHIP...  23.3 us
    all_to_all x2, blocking collectives, summed_on_arrival(): lax.all_to_all(parts, axis, split_axis=0, concat_axis=0, tiled=True)  18.5 us
    ppermute x6, starting transfers between devices, swap_cores(): return lax.ppermute(shard, CORES, [(0, 1), (1, 0)])  15.5 us
    all_to_all x2, starting transfers between devices, copy_for_each(): lax.all_to_all(jnp.broadcast_to(shard[None], (length, *shard.shape)), axi...  13.6 us
    all_to_all x2, waiting for transfers between devices, summed_on_arrival(): lax.all_to_all(parts, axis, split_axis=0, concat_axis=0, tiled=True)  13.2 us
    all_to_all x2, waiting for transfers between devices, copy_for_each(): lax.all_to_all(jnp.broadcast_to(shard[None], (length, *shard.shape)), axi...  10.3 us
  transfers between devices with their start and end apart: 11, of which 11 were waited for; matrix products, arithmetic and copies ran while one was open for 1% of the time, Pallas kernels for 0%

profile of v10, /device:TPU:1, one launch (start us, length us, event | category | flops | bytes accessed | tf_op | source)
XLA Modules:
  0.0 265.8 jit_solution(6779206439958557949)
XLA Ops:
  2.2 8.4 %all-to-all-start = ((f32[16,1,16]{2,1,0:T(1,128)}), f32[16,1,16]{2,1,0:T(1,128)S(1)}, u32[]{:S(2)}, u32[]{:S(2)}) async-start(f32[16,1,16]{2,1,0:T(1,128)} %broadcast_in_dim.60), calls=%async_computation | async-start | bytes 16384 | tf_op jit(solution)/shard_map/all_to_all | solution.py:62
  12.1 5.4 %all-to-all-done = f32[16,1,16]{2,1,0:T(1,128)S(1)} async-done(((f32[16,1,16]{2,1,0:T(1,128)}), f32[16,1,16]{2,1,0:T(1,128)S(1)}, u32[]{:S(2)}, u32[]{:S(2)}) %all-to-all-start) | async-done | bytes 1056 | tf_op jit(solution)/shard_map/all_to_all | solution.py:62
  19.0 5.1 %all-to-all-start.1 = ((bf16[8,16,512]{2,1,0:T(8,128)(2,1)}), bf16[8,16,512]{2,1,0:T(8,128)(2,1)S(1)}, u32[]{:S(2)}, u32[]{:S(2)}) async-start(bf16[8,16,512]{2,1,0:T(8,128)(2,1)} %broadcast_in_dim.61), calls=%async_computation.1 | async-start | bytes 262144 | tf_op jit(solution)/shard_map/all_to_all | solution.py:62
  24.9 4.8 %all-to-all-done.1 = bf16[8,16,512]{2,1,0:T(8,128)(2,1)S(1)} async-done(((bf16[8,16,512]{2,1,0:T(8,128)(2,1)}), bf16[8,16,512]{2,1,0:T(8,128)(2,1)S(1)}, u32[]{:S(2)}, u32[]{:S(2)}) %all-to-all-start.1) | async-done | bytes 131104 | tf_op jit(solution)/shard_map/all_to_all | solution.py:62
  34.3 3.4 %all-to-all-start.2 = ((f32[8,8,1280]{2,1,0:T(8,128)}), f32[8,8,1280]{2,1,0:T(8,128)S(1)}, u32[]{:S(2)}, u32[]{:S(2)}) async-start(f32[8,8,1280]{2,1,0:T(8,128)} %bitcast_add_fusion), calls=%async_computation.2 | async-start | bytes 655360 | tf_op jit(solution)/shard_map/all_to_all | solution.py:44
  37.9 8.7 %all-to-all-done.2 = f32[8,8,1280]{2,1,0:T(8,128)S(1)} async-done(((f32[8,8,1280]{2,1,0:T(8,128)}), f32[8,8,1280]{2,1,0:T(8,128)S(1)}, u32[]{:S(2)}, u32[]{:S(2)}) %all-to-all-start.2) | async-done | bytes 327712 | tf_op jit(solution)/shard_map/all_to_all | solution.py:44
  47.1 2.7 %fusion.183 = (f32[8,8]{1,0:T(8,128)S(1)}, f32[8,8,9536]{2,1,0:T(8,128)S(1)}) fusion(bf16[8,8,128]{2,1,0:T(8,128)(2,1)S(1)} %fusion.137, bf16[2,2,9536,128]{3,2,1,0:T(8,128)(2,1)} %param.11, pred[8,9536]{1,0:T(8,128)(4,1)S(1)} %fusion.103), kind=kOutput, calls=%fused_computation.259 | convolution fusion | flops 158068672 | bytes 4975360 | tf_op jit(solution)/shard_map/rkgd,tkd->krgt/dot_general | solution.py:160
  52.9 12.9 %all_to_all.86 = bf16[16,8,1024]{2,1,0:T(8,128)(2,1)S(1)} all-to-all(bf16[16,8,1024]{2,1,0:T(8,128)(2,1)S(1)} %broadcast_in_dim.64), channel_id=1, replica_groups=mesh['chips'=8,'cores'=2,'narrow'=8] {'chips','cores'}, dimensions={0} | all-to-all | bytes 524288 | tf_op jit(solution)/shard_map/all_to_all | solution.py:62
  66.8 3.4 %all-to-all-start.4 = ((f32[8,16,512]{2,1,0:T(8,128)}), f32[8,16,512]{2,1,0:T(8,128)S(1)}, u32[]{:S(2)}, u32[]{:S(2)}) async-start(f32[8,16,512]{2,1,0:T(8,128)} %fusion.86), calls=%async_computation.4 | async-start | bytes 524288 | tf_op jit(solution)/shard_map/all_to_all | solution.py:89
  70.2 6.9 %all-to-all-done.4 = f32[8,16,512]{2,1,0:T(8,128)S(1)} async-done(((f32[8,16,512]{2,1,0:T(8,128)}), f32[8,16,512]{2,1,0:T(8,128)S(1)}, u32[]{:S(2)}, u32[]{:S(2)}) %all-to-all-start.4) | async-done | bytes 262176 | tf_op jit(solution)/shard_map/all_to_all | solution.py:89
  77.6 8.1 %all_to_all.87 = bf16[8,16,514]{2,1,0:T(8,128)(2,1)S(1)} all-to-all(bf16[8,16,514]{2,1,0:T(8,128)(2,1)S(1)} %broadcast_in_dim.65), channel_id=1, replica_groups=mesh['chips'=8,'cores'=2,'narrow'=8] {'narrow'}, dimensions={0} | all-to-all | bytes 263168 | tf_op jit(solution)/shard_map/all_to_all | solution.py:62
  86.3 4.2 %fusion.15 = bf16[2,128,3584]{2,1,0:T(8,128)(2,1)S(1)} fusion(bf16[512,2,3584]{2,1,0:T(2,128)(2,1)} %param.14, bf16[8,8,512]{2,1,0:T(8,128)(2,1)S(1)} %get-tuple-element.27, bf16[8,8,512]{2,1,0:T(8,128)(2,1)S(1)} %get-tuple-element.26), kind=kOutput, calls=%fused_computation.11 | convolution fusion | flops 940703744 | bytes 9306112 | tf_op jit(solution)/shard_map/rd,dkh->krh/dot_general | solution.py:270
  91.6 2.5 collective-permute-start.1
  99.2 17.4 %all_to_all.88 = bf16[2,8,8,3585]{3,2,0,1:T(8,128)(2,1)S(1)} all-to-all(bf16[2,8,8,3585]{3,2,0,1:T(8,128)(2,1)S(1)} %copy.247), channel_id=1, replica_groups=mesh['chips'=8,'cores'=2,'narrow'=8] {'chips'}, dimensions={1} | all-to-all | bytes 1835520 | tf_op jit(solution)/shard_map/all_to_all | solution.py:44
  117.1 11.6 %all_to_all.89 = bf16[8,8,3584]{2,1,0:T(8,128)(2,1)S(1)} all-to-all(bf16[8,8,3584]{2,1,0:T(8,128)(2,1)S(1)} %broadcast_in_dim.69), channel_id=1, replica_groups=mesh['chips'=8,'cores'=2,'narrow'=8] {'chips'}, dimensions={0} | all-to-all | bytes 917504 | tf_op jit(solution)/shard_map/all_to_all | solution.py:50
  128.7 2.9 %collective-permute-start.2 = (bf16[8,8,3584]{2,1,0:T(8,128)(2,1)S(1)}, bf16[8,8,3584]{2,1,0:T(8,128)(2,1)S(1)}, u32[]{:S(2)}, u32[]{:S(2)}) collective-permute-start(bf16[8,8,3584]{2,1,0:T(8,128)(2,1)S(1)} %all_to_all.89), channel_id=1, source_target_pairs={{0,8},{8,0},{1,9},{9,1},{2,10},{10,2},{3,11},{11,3},{4,12},{12,4},... | collective-permute-start | bytes 1376264 | tf_op jit(solution)/shard_map/ppermute | solution.py:28
  133.1 2.7 %fusion.20 = f32[8,16,512]{2,1,0:T(8,128)S(1)} fusion(bf16[3584,512]{1,0:T(8,128)(2,1)} %param.15, bf16[8,1,8,3584]{3,2,1,0:T(8,128)(2,1)S(1)} %get-tuple-element.23, bf16[8,1,8,3584]{3,2,1,0:T(8,128)(2,1)S(1)} %get-tuple-element.22), kind=kOutput, calls=%fused_computation.14 | convolution fusion | flops 470220800 | bytes 4849664 | tf_op jit(solution)/shard_map/dot_general | solution.py:300
  135.8 9.1 %all_to_all.90 = f32[8,16,512]{2,1,0:T(8,128)S(1)} all-to-all(f32[8,16,512]{2,1,0:T(8,128)S(1)} %fusion.20), channel_id=1, replica_groups=mesh['chips'=8,'cores'=2,'narrow'=8] {'narrow'}, dimensions={0} | all-to-all | bytes 524288 | tf_op jit(solution)/shard_map/all_to_all | solution.py:89
  145.4 8.3 %all_to_all.91 = bf16[8,16,514]{2,1,0:T(8,128)(2,1)S(1)} all-to-all(bf16[8,16,514]{2,1,0:T(8,128)(2,1)S(1)} %broadcast_in_dim.70), channel_id=1, replica_groups=mesh['chips'=8,'cores'=2,'narrow'=8] {'narrow'}, dimensions={0} | all-to-all | bytes 263168 | tf_op jit(solution)/shard_map/all_to_all | solution.py:62
  154.2 2.6 collective-permute-start.3
  158.1 11.7 %all_to_all.92 = f32[8,8,1281]{2,1,0:T(8,128)S(1)} all-to-all(f32[8,8,1281]{2,1,0:T(8,128)S(1)} %fusion.102), channel_id=1, replica_groups=mesh['chips'=8,'cores'=2,'narrow'=8] {'chips'}, dimensions={0} | all-to-all | bytes 655872 | tf_op jit(solution)/shard_map/all_to_all | solution.py:44
  170.4 2.7 %fusion.184 = (f32[8,8]{1,0:T(8,128)S(1)}, f32[8,8,9536]{2,1,0:T(8,128)S(1)}) fusion(bf16[8,8,128]{2,1,0:T(8,128)(2,1)S(1)} %fusion.138, bf16[2,2,9536,128]{3,2,1,0:T(8,128)(2,1)} %param.11, pred[8,9536]{1,0:T(8,128)(4,1)S(1)} %fusion.103), kind=kOutput, calls=%fused_computation.260 | convolution fusion | flops 158068672 | bytes 4975360 | tf_op jit(solution)/shard_map/rkgd,tkd->krgt/dot_general | solution.py:160
  176.2 13.6 %all_to_all.93 = bf16[16,8,1024]{2,1,0:T(8,128)(2,1)S(1)} all-to-all(bf16[16,8,1024]{2,1,0:T(8,128)(2,1)S(1)} %broadcast_in_dim.72), channel_id=1, replica_groups=mesh['chips'=8,'cores'=2,'narrow'=8] {'chips','cores'}, dimensions={0} | all-to-all | bytes 524288 | tf_op jit(solution)/shard_map/all_to_all | solution.py:62
  190.1 9.4 %all_to_all.94 = f32[8,16,512]{2,1,0:T(8,128)S(1)} all-to-all(f32[8,16,512]{2,1,0:T(8,128)S(1)} %fusion.84), channel_id=1, replica_groups=mesh['chips'=8,'cores'=2,'narrow'=8] {'narrow'}, dimensions={0} | all-to-all | bytes 524288 | tf_op jit(solution)/shard_map/all_to_all | solution.py:89
  199.9 8.1 %all_to_all.95 = bf16[8,16,514]{2,1,0:T(8,128)(2,1)S(1)} all-to-all(bf16[8,16,514]{2,1,0:T(8,128)(2,1)S(1)} %broadcast_in_dim.73), channel_id=1, replica_groups=mesh['chips'=8,'cores'=2,'narrow'=8] {'narrow'}, dimensions={0} | all-to-all | bytes 263168 | tf_op jit(solution)/shard_map/all_to_all | solution.py:62
  208.6 4.2 %fusion.12 = bf16[2,128,3584]{2,1,0:T(8,128)(2,1)S(1)} fusion(bf16[512,2,3584]{2,1,0:T(2,128)(2,1)} %param.14, bf16[8,8,512]{2,1,0:T(8,128)(2,1)S(1)} %get-tuple-element.25, bf16[8,8,512]{2,1,0:T(8,128)(2,1)S(1)} %get-tuple-element.24), kind=kOutput, calls=%fused_computation.10 | convolution fusion | flops 940703744 | bytes 9306112 | tf_op jit(solution)/shard_map/rd,dkh->krh/dot_general | solution.py:270
  213.9 2.5 collective-permute-start.4
  219.5 17.4 %all_to_all.96 = bf16[2,8,8,3585]{3,2,0,1:T(8,128)(2,1)S(1)} all-to-all(bf16[2,8,8,3585]{3,2,0,1:T(8,128)(2,1)S(1)} %copy.262), channel_id=1, replica_groups=mesh['chips'=8,'cores'=2,'narrow'=8] {'chips'}, dimensions={1} | all-to-all | bytes 1835520 | tf_op jit(solution)/shard_map/all_to_all | solution.py:44
  237.4 11.7 %all_to_all.97 = bf16[8,8,3584]{2,1,0:T(8,128)(2,1)S(1)} all-to-all(bf16[8,8,3584]{2,1,0:T(8,128)(2,1)S(1)} %broadcast_in_dim.77), channel_id=1, replica_groups=mesh['chips'=8,'cores'=2,'narrow'=8] {'chips'}, dimensions={0} | all-to-all | bytes 917504 | tf_op jit(solution)/shard_map/all_to_all | solution.py:50
  249.1 2.9 %collective-permute-start.5 = (bf16[8,8,3584]{2,1,0:T(8,128)(2,1)S(1)}, bf16[8,8,3584]{2,1,0:T(8,128)(2,1)S(1)}, u32[]{:S(2)}, u32[]{:S(2)}) collective-permute-start(bf16[8,8,3584]{2,1,0:T(8,128)(2,1)S(1)} %all_to_all.97), channel_id=1, source_target_pairs={{0,8},{8,0},{1,9},{9,1},{2,10},{10,2},{3,11},{11,3},{4,12},{12,4},... | collective-permute-start | bytes 1376264 | tf_op jit(solution)/shard_map/ppermute | solution.py:28
  254.8 3.4 %all-to-all-start.16 = ((f32[8,16,512]{2,1,0:T(8,128)}), f32[8,16,512]{2,1,0:T(8,128)S(1)}, u32[]{:S(2)}, u32[]{:S(2)}) async-start(f32[8,16,512]{2,1,0:T(8,128)} %fusion.18), calls=%async_computation.16 | async-start | bytes 524288 | tf_op jit(solution)/shard_map/all_to_all | solution.py:89
  258.9 6.3 %all-to-all-done.16 = f32[8,16,512]{2,1,0:T(8,128)S(1)} async-done(((f32[8,16,512]{2,1,0:T(8,128)}), f32[8,16,512]{2,1,0:T(8,128)S(1)}, u32[]{:S(2)}, u32[]{:S(2)}) %all-to-all-start.16) | async-done | bytes 262176 | tf_op jit(solution)/shard_map/all_to_all | solution.py:89
  (157 shorter events, 39.2 us)
Async XLA Ops:
  0.6 29.1 %copy-start = (bf16[512,1,1280]{2,0,1:T(8,128)(2,1)S(1)}, bf16[512,1,1280]{2,0,1:T(8,128)(2,1)}, u32[]{:S(2)}) copy-start(bf16[512,1,1280]{2,0,1:T(8,128)(2,1)} %param.12) | copy-start | bytes 3932164
  2.2 15.4 %all-to-all-start = ((f32[16,1,16]{2,1,0:T(1,128)}), f32[16,1,16]{2,1,0:T(1,128)S(1)}, u32[]{:S(2)}, u32[]{:S(2)}) async-start(f32[16,1,16]{2,1,0:T(1,128)} %broadcast_in_dim.60), calls=%async_computation | async-start | bytes 16384 | tf_op jit(solution)/shard_map/all_to_all | solution.py:62
  19.0 10.7 %all-to-all-start.1 = ((bf16[8,16,512]{2,1,0:T(8,128)(2,1)}), bf16[8,16,512]{2,1,0:T(8,128)(2,1)S(1)}, u32[]{:S(2)}, u32[]{:S(2)}) async-start(bf16[8,16,512]{2,1,0:T(8,128)(2,1)} %broadcast_in_dim.61), calls=%async_computation.1 | async-start | bytes 262144 | tf_op jit(solution)/shard_map/all_to_all | solution.py:62
  30.2 3.4 %collective-permute-start = (f32[8,8,1280]{2,1,0:T(8,128)S(1)}, f32[8,8,1280]{2,1,0:T(8,128)S(1)}, u32[]{:S(2)}, u32[]{:S(2)}) collective-permute-start(f32[8,8,1280]{2,1,0:T(8,128)S(1)} %dynamic-slice_bitcast_fusion), channel_id=1, source_target_pairs={{0,8},{8,0},{1,9},{9,1},{2,10},{10,2},{3,11},{11,3},{4,12},{12,4},... | collective-permute-start | bytes 983048 | tf_op jit(solution)/shard_map/ppermute | solution.py:28
  34.3 12.3 %all-to-all-start.2 = ((f32[8,8,1280]{2,1,0:T(8,128)}), f32[8,8,1280]{2,1,0:T(8,128)S(1)}, u32[]{:S(2)}, u32[]{:S(2)}) async-start(f32[8,8,1280]{2,1,0:T(8,128)} %bitcast_add_fusion), calls=%async_computation.2 | async-start | bytes 655360 | tf_op jit(solution)/shard_map/all_to_all | solution.py:44
  50.4 15.4 %copy-start.1 = (bf16[1024,512]{1,0:T(8,128)(2,1)S(1)}, bf16[1024,512]{1,0:T(8,128)(2,1)}, u32[]{:S(2)}) copy-start(bf16[1024,512]{1,0:T(8,128)(2,1)} %param.13) | copy-start | bytes 3145732
  52.8 17.4 %copy-start.3 = (bf16[512]{0:T(512)(128)(2,1)S(1)}, bf16[512]{0:T(512)(128)(2,1)}, u32[]{:S(2)}) copy-start(bf16[512]{0:T(512)(128)(2,1)} %param.17) | copy-start | bytes 3076
  52.8 24.3 %copy-start.2 = (bf16[16,512]{1,0:T(8,128)(2,1)S(1)}, bf16[16,512]{1,0:T(8,128)(2,1)}, u32[]{:S(2)}) copy-start(bf16[16,512]{1,0:T(8,128)(2,1)} %param.9) | copy-start | bytes 49156
  66.8 10.3 %all-to-all-start.4 = ((f32[8,16,512]{2,1,0:T(8,128)}), f32[8,16,512]{2,1,0:T(8,128)S(1)}, u32[]{:S(2)}, u32[]{:S(2)}) async-start(f32[8,16,512]{2,1,0:T(8,128)} %fusion.86), calls=%async_computation.4 | async-start | bytes 524288 | tf_op jit(solution)/shard_map/all_to_all | solution.py:89
  91.6 5.0 %collective-permute-start.1 = (bf16[2,8,8,3585]{3,2,1,0:T(8,128)(2,1)}, bf16[2,8,8,3585]{3,2,1,0:T(8,128)(2,1)}, u32[]{:S(2)}, u32[]{:S(2)}) collective-permute-start(bf16[2,8,8,3585]{3,2,1,0:T(8,128)(2,1)} %get-tuple-element.11), channel_id=1, source_target_pairs={{0,8},{8,0},{1,9},{9,1},{2,10},{10,2},{3,11},{11,3},{4,12},{12,4},... | collective-permute-start | bytes 2753288 | tf_op jit(solution)/shard_map/ppermute | solution.py:28
  128.7 4.3 %collective-permute-start.2 = (bf16[8,8,3584]{2,1,0:T(8,128)(2,1)S(1)}, bf16[8,8,3584]{2,1,0:T(8,128)(2,1)S(1)}, u32[]{:S(2)}, u32[]{:S(2)}) collective-permute-start(bf16[8,8,3584]{2,1,0:T(8,128)(2,1)S(1)} %all_to_all.89), channel_id=1, source_target_pairs={{0,8},{8,0},{1,9},{9,1},{2,10},{10,2},{3,11},{11,3},{4,12},{12,4},... | collective-permute-start | bytes 1376264 | tf_op jit(solution)/shard_map/ppermute | solution.py:28
  154.2 3.9 %collective-permute-start.3 = (f32[8,8,1281]{2,1,0:T(8,128)S(1)}, f32[8,8,1281]{2,1,0:T(8,128)S(1)}, u32[]{:S(2)}, u32[]{:S(2)}) collective-permute-start(f32[8,8,1281]{2,1,0:T(8,128)S(1)} %fusion.99), channel_id=1, source_target_pairs={{0,8},{8,0},{1,9},{9,1},{2,10},{10,2},{3,11},{11,3},{4,12},{12,4},... | collective-permute-start | bytes 983816 | tf_op jit(solution)/shard_map/ppermute | solution.py:28
  213.9 4.9 %collective-permute-start.4 = (bf16[2,8,8,3585]{3,2,1,0:T(8,128)(2,1)}, bf16[2,8,8,3585]{3,2,1,0:T(8,128)(2,1)S(1)}, u32[]{:S(2)}, u32[]{:S(2)}) collective-permute-start(bf16[2,8,8,3585]{3,2,1,0:T(8,128)(2,1)} %get-tuple-element.9), channel_id=1, source_target_pairs={{0,8},{8,0},{1,9},{9,1},{2,10},{10,2},{3,11},{11,3},{4,12},{12,4},... | collective-permute-start | bytes 2753288 | tf_op jit(solution)/shard_map/ppermute | solution.py:28
  236.9 16.5 %copy-start.4 = (bf16[3584,512]{1,0:T(8,128)(2,1)S(1)}, bf16[3584,512]{1,0:T(8,128)(2,1)}, u32[]{:S(2)}) copy-start(bf16[3584,512]{1,0:T(8,128)(2,1)} %param.15) | copy-start | bytes 11010052
  249.1 4.3 %collective-permute-start.5 = (bf16[8,8,3584]{2,1,0:T(8,128)(2,1)S(1)}, bf16[8,8,3584]{2,1,0:T(8,128)(2,1)S(1)}, u32[]{:S(2)}, u32[]{:S(2)}) collective-permute-start(bf16[8,8,3584]{2,1,0:T(8,128)(2,1)S(1)} %all_to_all.97), channel_id=1, source_target_pairs={{0,8},{8,0},{1,9},{9,1},{2,10},{10,2},{3,11},{11,3},{4,12},{12,4},... | collective-permute-start | bytes 1376264 | tf_op jit(solution)/shard_map/ppermute | solution.py:28
  254.8 10.4 %all-to-all-start.16 = ((f32[8,16,512]{2,1,0:T(8,128)}), f32[8,16,512]{2,1,0:T(8,128)S(1)}, u32[]{:S(2)}, u32[]{:S(2)}) async-start(f32[8,16,512]{2,1,0:T(8,128)} %fusion.18), calls=%async_computation.16 | async-start | bytes 524288 | tf_op jit(solution)/shard_map/all_to_all | solution.py:89
